TPU v7x, 128 devices: a whole 4x4x4 slice. The times are simulated.
128 devices in a mesh: valve: 8 (over y, core), bulk: 16 (over z, x).
Axes of the slice: x: 4, y: 4, z: 4, core: 2. Of those that a mesh axis runs over, the one named last changes fastest.
Arguments:
- solution: float32 [5, 64, 131072], P(None, None, ('valve', 'bulk')), may hold values from -6 to 6
- velocity: float32 [3, 131072], P(None, ('valve', 'bulk')), may hold values from -1 to 1
- inv_jacobian: float32 [64, 131072], P(None, ('valve', 'bulk')), may hold values from 0.5 to 3
- face_speed: float32 [96, 131072], P(None, ('valve', 'bulk')), may hold values from -6 to 6
- face_link: int32 [6, 131072], P(None, ('valve', 'bulk')), may hold values from 0 to 6271, as said below
- donor_elem: int32 [1048576], P(('valve', 'bulk')), may hold values from 0 to 1023
- ref_coords: float32 [3, 1048576], P(None, ('valve', 'bulk')), may hold values from -1 to 1
- owner_list: int32 [1048576, 1], P(('valve', 'bulk')), may hold values from 0 to 15; in each aligned block of 8192 rows (0 to 8191, 8192 to 16383, ...) at most 1024 rows name the same one
Outputs:
- section_rate: float32 [5, 64, 131072], P(None, None, ('valve', 'bulk'))
- fringe_values: float32 [5, 2097152], P(None, ('valve', 'bulk'))
Inputs may be any that keep to these rules, and one draw needn't show every extreme that they name: `face_link`: on each device, the values 6 * 1024 to 6271 appear exactly once each; every other face slot links to another slot of the same device that links back to it. `owner_list`: among the receptors of one device no owner is named more than 1024 times; in every draw some device names some owner exactly 1024 times.
All inputs are finite; a program needn't handle non-finite values.
Results may differ from a plain program's by a relative error of at most 0.0003.
Values sent between devices are 32-bit elements; how exact they have to be, the bound alone decides.
No kernel may reach another device: no remote copies, remote signals or barrier semaphores. Data moves between devices by JAX's collectives and lax.ppermute only.
A program may use at most 192 MiB of HBM per device.

v0:
```python
import jax
import jax.numpy as jnp
import numpy as np
from jax import lax
from jax.sharding import PartitionSpec as P
from jax.experimental import pallas as pl
from jax.experimental.pallas import tpu as pltpu

gauss_nodes = (-0.8611363115940526, -0.3399810435848563, 0.3399810435848563, 0.8611363115940526)
quad_weights = (0.3478548451374538, 0.6521451548625461, 0.6521451548625461, 0.3478548451374538)
section_step = 0.2


def padded(shard, sides, width):
    for axis, dim in sides:
        size, length = (lax.axis_size(axis), shard.shape[dim])
        up = [(i, (i + 1) % size) for i in range(size)]
        down = [(j, i) for i, j in up]
        last = lax.slice_in_dim(shard, length - width, length, axis=dim)
        initial = lax.slice_in_dim(shard, 0, width, axis=dim)
        before = lax.ppermute(last, axis, up)
        after = lax.ppermute(initial, axis, down)
        shard = jnp.concatenate([before, shard, after], axis=dim)
    return shard


def lagrange_at(x):
    values = []
    for j in range(4):
        factor = 1.0
        for m in range(4):
            if m != j:
                factor = factor * (x - gauss_nodes[m]) / (gauss_nodes[j] - gauss_nodes[m])
        values.append(factor)
    return values


def tables():
    slopes = np.zeros((4, 4))
    for i in range(4):
        for j in range(4):
            summed = 0.0
            for m in range(4):
                if m != j:
                    product = 1.0 / (gauss_nodes[j] - gauss_nodes[m])
                    for n in range(4):
                        if n != j and n != m:
                            product = (
                                product
                                * (gauss_nodes[i] - gauss_nodes[n])
                                / (gauss_nodes[j] - gauss_nodes[n])
                            )
                    summed = summed + product
            slopes[i, j] = summed
    end_values = [lagrange_at(-1.0), lagrange_at(1.0)]
    extrapolate = np.zeros((96, 64))
    lifting = np.zeros((64, 96))
    derivative = np.zeros((3, 64, 64))
    for p in range(64):
        point_idx = (p // 16, p // 4 % 4, p % 4)
        for f in range(6):
            normal_dir = f // 2
            across = [t for t in range(3) if t != normal_dir]
            q = point_idx[across[0]] * 4 + point_idx[across[1]]
            flux_row = q * 6 + f
            extrapolate[flux_row, p] = end_values[f % 2][point_idx[normal_dir]]
            lifting[p, flux_row] = (
                end_values[f % 2][point_idx[normal_dir]] / quad_weights[point_idx[normal_dir]]
            )
        for s in range(64):
            other_idx = (s // 16, s // 4 % 4, s % 4)
            for normal_dir in range(3):
                if all((point_idx[t] == other_idx[t] for t in range(3) if t != normal_dir)):
                    derivative[normal_dir, p, s] = slopes[
                        point_idx[normal_dir], other_idx[normal_dir]
                    ]
    return (
        jnp.asarray(extrapolate, dtype=jnp.float32),
        jnp.asarray(derivative, dtype=jnp.float32),
        jnp.asarray(lifting, dtype=jnp.float32),
    )


def face_rows(solution, face_speed, extrapolate):
    nvars = solution.shape[0]
    elems = solution.shape[2]
    ext_faces = extrapolate.reshape(16, 6, 64)
    values = jnp.einsum("qfp,vpe->feqv", ext_faces, solution, precision=lax.Precision.HIGHEST)
    values = values.reshape(6 * elems, 16, nvars)
    speeds = jnp.transpose(face_speed.reshape(16, 6, elems), (1, 2, 0)).reshape(6 * elems, 16)
    return (values, speeds)


def rim_rows(table_own, links, faces_total, rim_count):
    wanted = faces_total + jnp.arange(2 * rim_count, dtype=jnp.int32)
    hits = links[None, :] == wanted[:, None]
    faces = jnp.arange(faces_total, dtype=jnp.int32)[None, :]
    senders = jnp.sum(jnp.where(hits, faces, 0), axis=1)
    return jnp.take(table_own, senders, axis=0)


def split_bf16(x):
    hi = lax.reduce_precision(x, exponent_bits=8, mantissa_bits=7)
    return hi.astype(jnp.bfloat16), (x - hi).astype(jnp.bfloat16)


def pick_dot(rows, onehot):
    hi, lo = split_bf16(rows)
    out = jnp.dot(hi, onehot, preferred_element_type=jnp.float32)
    return out + jnp.dot(lo, onehot, preferred_element_type=jnp.float32)


def _rows_kernel(idx_ref, own_ref, recv_ref, out_ref, table_ref):
    own_rows = own_ref.shape[0]
    table_ref[pl.ds(0, own_rows), :] = own_ref[...]
    table_ref[pl.ds(own_rows, recv_ref.shape[0]), :] = recv_ref[...]

    def body(i, carry):
        base = pl.multiple_of(i * 16, 16)
        for j in range(16):
            row = idx_ref[base + j]
            out_ref[pl.ds(base + j, 1), :] = table_ref[pl.ds(row, 1), :]
        return carry

    lax.fori_loop(0, out_ref.shape[0] // 16, body, 0)


def take_rows(own, received, idx):
    rows = own.shape[0] + received.shape[0]
    return pl.pallas_call(
        _rows_kernel,
        out_shape=jax.ShapeDtypeStruct((idx.shape[0], own.shape[1]), own.dtype),
        in_specs=[
            pl.BlockSpec(memory_space=pltpu.SMEM),
            pl.BlockSpec(memory_space=pltpu.VMEM),
            pl.BlockSpec(memory_space=pltpu.VMEM),
        ],
        out_specs=pl.BlockSpec(memory_space=pltpu.VMEM),
        scratch_shapes=[pltpu.VMEM((rows, own.shape[1]), own.dtype)],
        cost_estimate=pl.CostEstimate(
            flops=0, transcendentals=0, bytes_accessed=(2 * idx.shape[0] + rows) * own.shape[1] * 4
        ),
    )(idx, own, received)


def owner_ranks(owners, buckets):
    receptors = owners.shape[0]
    width = 128
    blocks = receptors // width
    member = owners[None, :] == jnp.arange(buckets, dtype=jnp.int32)[:, None]
    member = member.astype(jnp.bfloat16).reshape(buckets * blocks, width)
    upper = jnp.asarray(np.triu(np.ones((width, width))), jnp.bfloat16)
    inside = jnp.dot(member, upper, preferred_element_type=jnp.float32)
    inside = inside.reshape(buckets, blocks, width)
    totals = inside[:, :, width - 1].astype(jnp.bfloat16)
    strict = jnp.asarray(np.triu(np.ones((blocks, blocks)), 1), jnp.bfloat16)
    offsets = jnp.dot(totals, strict, preferred_element_type=jnp.float32)
    counts = (inside + offsets[:, :, None]).reshape(buckets, receptors)
    picked = jnp.sum(jnp.where(member.reshape(buckets, receptors) > 0, counts, 0.0), axis=0)
    return picked.astype(jnp.int32) - 1


def surface_term(values, speeds, table_own, links, received, lifting, elems):
    nvars = values.shape[2]
    outer = take_rows(table_own, received, links)
    outer_vals = outer[:, : 16 * nvars].reshape(6 * elems, 16, nvars)
    outer_speed = outer[:, 16 * nvars :][:, :, None]
    own_speed = speeds[:, :, None]
    normal = 0.5 * (own_speed - outer_speed)
    common = 0.5 * normal * (values + outer_vals) + 0.5 * jnp.abs(normal) * (values - outer_vals)
    jump_term = (common - own_speed * values).reshape(6, elems, 16, nvars)
    lift_faces = lifting.reshape(64, 16, 6)
    return jnp.einsum("pqf,feqv->vpe", lift_faces, jump_term, precision=lax.Precision.HIGHEST)


def volume_term(solution, velocity, derivative):
    slopes = jnp.einsum("dpq,vqe->dvpe", derivative, solution, precision=lax.Precision.HIGHEST)
    return jnp.sum(velocity[:, None, None, :] * slopes, axis=0)


def receptor_rows(advanced, donors, coords):
    nvars = advanced.shape[0]
    elems = advanced.shape[2]
    basis_x = jnp.stack(lagrange_at(coords[0]))
    basis_y = jnp.stack(lagrange_at(coords[1]))
    basis_z = jnp.stack(lagrange_at(coords[2]))
    weights = (
        jnp.repeat(basis_x, 16, axis=0)
        * jnp.tile(jnp.repeat(basis_y, 4, axis=0), (4, 1))
        * jnp.tile(basis_z, (16, 1))
    )
    onehot = (jnp.arange(elems, dtype=jnp.int32)[:, None] == donors[None, :]).astype(jnp.bfloat16)
    picked = pick_dot(advanced.reshape(nvars * 64, elems), onehot).reshape(nvars, 64, -1)
    return jnp.sum(picked * weights[None], axis=1)


def on_device(
    solution, velocity, inv_jacobian, face_speed, face_link, donor_elem, ref_coords, owner_list
):
    extrapolate, derivative, lifting = tables()
    nvars = solution.shape[0]
    elems = solution.shape[2]
    rim_count = elems // 16
    faces_total = 6 * elems
    links = face_link.reshape(faces_total)
    values, speeds = face_rows(solution, face_speed, extrapolate)
    table_own = jnp.concatenate([values.reshape(faces_total, 16 * nvars), speeds], axis=1)
    outgoing = rim_rows(table_own, links, faces_total, rim_count)
    extended = padded(outgoing, (("valve", 0),), rim_count)
    received = jnp.concatenate([extended[:rim_count], extended[3 * rim_count :]], axis=0)
    surface = surface_term(values, speeds, table_own, links, received, lifting, elems)
    volume = volume_term(solution, velocity, derivative)
    section_rate = -inv_jacobian[None] * (volume + surface)
    advanced = solution + section_step * section_rate
    receptor_vals = receptor_rows(advanced, donor_elem, ref_coords)
    buckets = lax.axis_size("bulk")
    receptors = receptor_vals.shape[1]
    capacity = 2 * receptors // buckets
    owners = owner_list[:, 0]
    ranks = owner_ranks(owners, buckets)
    chosen = owners[:, None] == jnp.arange(buckets, dtype=jnp.int32)[None, :]
    masked = jnp.where(chosen[:, :, None], jnp.transpose(receptor_vals)[:, None, :], 0.0)
    hi, lo = split_bf16(masked.reshape(receptors, buckets * nvars))
    by_rank = (jnp.arange(capacity, dtype=jnp.int32)[:, None] == ranks[None, :]).astype(jnp.bfloat16)
    both = jnp.dot(by_rank, jnp.concatenate([hi, lo], axis=1), preferred_element_type=jnp.float32)
    placed = both[:, : buckets * nvars] + both[:, buckets * nvars :]
    send = jnp.transpose(placed.reshape(capacity, buckets, nvars), (1, 2, 0))
    got = lax.all_to_all(send, "bulk", 0, 0, tiled=True)
    fringe = jnp.transpose(got, (1, 0, 2)).reshape(nvars, buckets * capacity)
    return (section_rate, fringe)


def solution(mesh):
    placed = (
        P(None, None, ("valve", "bulk")),
        P(None, ("valve", "bulk")),
        P(None, ("valve", "bulk")),
        P(None, ("valve", "bulk")),
        P(None, ("valve", "bulk")),
        P(("valve", "bulk")),
        P(None, ("valve", "bulk")),
        P(("valve", "bulk"), None),
    )
    return jax.shard_map(
        on_device,
        mesh=mesh,
        in_specs=placed,
        out_specs=(P(None, None, ("valve", "bulk")), P(None, ("valve", "bulk"))),
        check_vma=False,
    )
```

profile of v0, /device:TPU:9, one launch (start us, length us, event | category | flops | bytes accessed | tf_op | source)
XLA Modules:
  0.0 132.1 jit_solution(14359094007938326972)
XLA Ops:
  0.6 0.0 copy-start.15
  0.7 0.8 reshape.169.idx_ref
  1.4 0.6 select_reduce_fusion
  2.0 1.8 %reshape.168 = f32[16,6,1024]{2,1,0:T(8,128)} reshape(f32[96,1024]{1,0:T(8,128)} %param.16) | data formatting | bytes 786432 | tf_op jit(solution)/shard_map/reshape | solution.py:90
  3.8 1.9 %copy.33 = f32[6,1024,16]{2,1,0:T(8,128)S(1)} copy(f32[6,1024,16]{1,0,2:T(8,128)} %bitcast.79) | data formatting | bytes 786432 | tf_op jit(solution)/shard_map/transpose | solution.py:90
  5.8 4.0 %convolution_bitcast_fusion = f32[6,1024,16,5]{1,2,3,0:T(8,128)S(1)} fusion(f32[16,6,64,1]{2,0,3,1:T(8,128)S(1)} %copy-done.15, f32[5,64,1024]{2,1,0:T(8,128)} %param.13), kind=kOutput, calls=%fused_computation.35 | convolution fusion | flops 377487360 | bytes 3301376 | tf_op jit(solution)/shard_map/qfp,vpe->feqv/dot_general | solution.py:88
  9.8 1.2 copy.34
  11.0 2.5 %copy.45 = f32[10,8,6,1024]{3,1,2,0:T(8,128)} copy(f32[10,8,6,1024]{3,2,1,0:T(8,128)S(1)} %bitcast.77) | data formatting | bytes 3932160
  13.5 3.4 %copy.35 = f32[6144,80]{1,0:T(8,128)} copy(f32[6144,80]{0,1:T(8,128)} %bitcast.78) | data formatting | bytes 3932160 | tf_op jit(solution)/shard_map/reshape;reshape | solution.py:207
  17.0 0.0 copy-done.1
  17.0 0.0 copy-start.10
  17.0 0.0 copy-start.16
  17.0 0.0 copy-start.19
  17.0 0.0 copy-start.14
  17.0 4.5 %pad_maximum_fusion.own_ref = f32[6144,96]{1,0:T(8,128)} fusion(f32[6144,16]{1,0:T(8,128)S(1)} %bitcast.73, f32[6144,80]{1,0:T(8,128)} %copy.35), kind=kLoop, calls=%fused_computation.15 | loop fusion | flops 589824 | bytes 4718592 | tf_op jit(solution)/shard_map/concatenate | solution.py:207
  21.5 2.5 %gather_fusion = f32[128,96]{1,0:T(8,128)S(1)} fusion(f32[6144,96]{1,0:T(8,128)} %pad_maximum_fusion.own_ref, s32[1024]{0:T(1024)S(1)} %pad_clamp_fusion), kind=kCustom, calls=%fused_computation | custom fusion | bytes 98816 | tf_op jit(solution)/shard_map/jit(_take)/gather | solution.py:99
  24.0 0.1 broadcast_select_fusion.1
  24.1 0.6 fusion.41
  24.7 0.7 collective-permute-start.1
  25.4 1.2 collective-permute-start
  26.6 0.2 fusion.35
  26.8 0.4 fusion.37
  27.2 0.1 fusion.42
  27.3 0.2 select_reduce_fusion.1
  27.5 0.6 add_bitcast_fusion
  28.1 0.8 multiply_multiply_fusion.11
  28.9 0.1 pad_maximum_fusion.3
  29.0 1.7 %tile.19 = f32[16,4,8192]{2,1,0:T(4,128)} broadcast(f32[4,8192]{1,0:T(4,128)S(1)} %pad_maximum_fusion.3), dimensions={1,2} | broadcast | bytes 2228224 | tf_op jit(solution)/shard_map/tile | solution.py:190
  30.8 2.2 %tile.20 = f32[64,8192]{1,0:T(8,128)S(1)} reshape(f32[16,4,8192]{2,1,0:T(4,128)} %tile.19) | data formatting | bytes 4194304 | tf_op jit(solution)/shard_map/tile | solution.py:190
  32.9 0.2 pad_maximum_fusion.1
  33.2 0.1 broadcast_in_dim.74
  33.3 0.2 tile.8
  33.5 0.7 iota_compare_fusion.7
  34.2 0.1 broadcast_multiply_fusion.1
  34.3 0.0 copy-start.5
  34.4 0.0 copy-start.13
  34.4 0.0 copy-start.18
  34.4 1.7 %bitcast_multiply_fusion = f32[64,8192]{1,0:T(8,128)} fusion(f32[64,8192]{1,0:T(8,128)S(1)} %tile.20, f32[4,16,8192]{2,1,0:T(8,128)S(1)} %broadcast_multiply_fusion.1), kind=kLoop, calls=%fused_computation.22 | loop fusion | flops 524288 | bytes 6291456 | tf_op jit(solution)/shard_map/mul | solution.py:188
  36.1 0.0 copy-start.11
  36.1 4.4 %multiply_reduce_fusion.1 = f32[64,5,1024]{2,0,1:T(8,128)} fusion(f32[3,64,64,1]{2,1,3,0:T(8,128)S(1)} %copy-done.13, f32[3,1024]{1,0:T(4,128)S(1)} %copy-done.18, f32[5,64,1024]{2,1,0:T(8,128)S(1)} %copy-done.5), kind=kOutput, calls=%fused_computation.11 | convolution fusion | flops 756613120 | bytes 2682880 | tf_op jit(solution)/shard_map/dpq,vqe->dvpe/dot_general | solution.py:177
  40.5 1.0 copy.41
  41.5 0.0 collective-permute-done.1
  41.5 0.0 collective-permute-done
  41.5 1.4 %pad_maximum_fusion.4.recv_ref = f32[128,96]{1,0:T(8,128)} fusion(f32[64,96]{1,0:T(8,128)} %collective-permute-done.1, f32[64,96]{1,0:T(8,128)} %collective-permute-done), kind=kLoop, calls=%fused_computation.60 | loop fusion | flops 12288 | bytes 98304 | tf_op jit(solution)/shard_map/concatenate | solution.py:210
  43.0 10.5 %shard_map.143 = f32[6144,96]{1,0:T(8,128)} custom-call(s32[6144]{0:T(1024)} %copy-done.12, f32[6144,96]{1,0:T(8,128)} %pad_maximum_fusion.own_ref, f32[128,96]{1,0:T(8,128)} %pad_maximum_fusion.4.recv_ref), custom_call_target="tpu_custom_call" | custom-call | bytes 7127040 | tf_op jit(solution)/shard_map/pallas_call | solution.py:130
  53.4 6.5 %broadcast_multiply_fusion = (f32[6144,16]{1,0:T(8,128)}, f32[6144,16]{1,0:T(8,128)}) fusion(f32[6144,96]{1,0:T(8,128)} %shard_map.143, f32[6,1024,16]{2,1,0:T(8,128)} %copy-done.1), kind=kLoop, calls=%fused_computation.36 | loop fusion | flops 491520 | bytes 1572864 | tf_op jit(solution)/shard_map/mul | solution.py:170
  60.0 2.1 %copy.37 = f32[6144,80]{0,1:T(8,128)} copy(f32[6144,80]{1,0:T(8,128)S(1)} %bitcast.72) | data formatting | bytes 3932160 | tf_op jit(solution)/shard_map/slice | solution.py:166
  62.1 3.4 %reshape.171 = f32[6,1024,16,5]{1,0,3,2:T(8,128)} reshape(f32[6144,80]{0,1:T(8,128)} %copy.37) | data formatting | bytes 3932160 | tf_op jit(solution)/shard_map/reshape | solution.py:166
  65.5 1.8 %copy.39 = f32[6,1024,16]{1,2,0:T(8,128)} copy(f32[6,1024,16]{2,1,0:T(8,128)S(1)} %bitcast.75) | data formatting | bytes 786432 | tf_op jit(solution)/shard_map/mul | solution.py:170
  67.3 3.1 %copy.36 = f32[6,1024,16]{1,2,0:T(8,128)} copy(f32[6,1024,16]{2,1,0:T(8,128)} %bitcast.74) | data formatting | bytes 786432 | tf_op jit(solution)/shard_map/mul | solution.py:170
  70.5 6.8 %multiply_add_fusion = (f32[5,64,1024]{2,1,0:T(8,128)S(1)}, f32[5,64,1024]{2,1,0:T(8,128)}) fusion(f32[5,64,1024]{2,1,0:T(8,128)S(1)} %copy-done.6, f32[64,16,6,1]{0,1,3,2:T(8,128)} %constant.122, f32[6,1024,16,5]{1,2,3,0:T(8,128)S(1)} %copy-done.3, f32[6,1024,16,5]{1,0,3,2:T(8,128)} %reshape.171, f32[6,1024,16]{1,2,0:T(8,128)} %copy.41, ...), kind=kOutput, calls=%fused_computation.43 | convolution fusion | flops 382238720 | bytes 10641408 | tf_op jit(solution)/shard_map/pqf,feqv->vpe/dot_general | solution.py:173
  77.3 0.2 reduce-precision_convert_fusion.1
  77.5 0.6 copy-done.20
  78.1 8.9 %fusion = f32[320,8192]{1,0:T(8,128)} fusion(bf16[320,1024]{1,0:T(8,128)(2,1)S(1)} %get-tuple-element.7, s32[8192]{0:T(1024)S(1)} %copy-done.20), kind=kOutput, calls=%fused_computation.2 | convolution fusion | flops 5377097728 | bytes 11173888 | tf_op jit(solution)/shard_map/dot_general | solution.py:110
  87.0 9.6 %fusion.6 = f32[320,8192]{1,0:T(8,128)S(1)} fusion(f32[320,8192]{1,0:T(8,128)} %fusion, bf16[320,1024]{1,0:T(8,128)(2,1)S(1)} %get-tuple-element.6, s32[8192]{0:T(1024)S(1)} %copy-done.20), kind=kOutput, calls=%fused_computation.9 | convolution fusion | flops 5379719168 | bytes 21659648 | tf_op jit(solution)/shard_map/dot_general | solution.py:109
  96.6 1.5 %multiply_reduce_fusion = f32[5,8192]{1,0:T(8,128)S(1)} fusion(f32[5,64,8192]{2,1,0:T(8,128)S(1)} %bitcast.76, f32[64,8192]{1,0:T(8,128)S(1)} %copy-done.7), kind=kLoop, calls=%fused_computation.10 | loop fusion | flops 5201920 | bytes 12746752 | tf_op jit(solution)/shard_map/reduce_sum | solution.py:194
  98.1 2.6 %broadcast_select_fusion = f32[8192,16,5]{0,2,1:T(8,128)} fusion(f32[8192,5]{0,1:T(8,128)S(1)} %bitcast.83, pred[8192,16]{0,1:T(8,128)(4,1)S(1)} %copy-done.9), kind=kLoop, calls=%fused_computation.23 | loop fusion | flops 655360 | bytes 2916352 | tf_op jit(solution)/shard_map/jit(_where)/select_n | solution.py:222
  100.7 2.7 %select_n.43 = f32[8192,80]{0,1:T(8,128)S(1)} reshape(f32[8192,16,5]{0,2,1:T(8,128)} %broadcast_select_fusion) | data formatting | bytes 5242880 | tf_op jit(solution)/shard_map/jit(_where)/select_n | solution.py:222
  103.4 0.4 reduce-precision_convert_fusion
  103.8 0.3 copy-done.17
  104.2 7.3 %fusion.2 = f32[1024,160]{0,1:T(8,128)S(1)} fusion(s32[8192]{0:T(1024)S(1)} %copy-done.17, bf16[8192,80]{0,1:T(8,128)(2,1)S(1)} %get-tuple-element.5, bf16[8192,80]{0,1:T(8,128)(2,1)S(1)} %get-tuple-element.4), kind=kOutput, calls=%fused_computation.5 | convolution fusion | flops 2697986048 | bytes 3309568 | tf_op jit(solution)/shard_map/dot_general | solution.py:225
  111.5 0.1 reshape.175
  111.6 19.8 %all_to_all.5 = f32[16,5,1024]{2,1,0:T(8,128)S(1)} all-to-all(f32[16,5,1024]{2,1,0:T(8,128)S(1)} %bitcast.82), channel_id=1, replica_groups=mesh['valve'=8,'bulk'=16] {'bulk'}, dimensions={0} | all-to-all | bytes 655360 | tf_op jit(solution)/shard_map/all_to_all | solution.py:228
  131.3 0.8 copy.59
  (36 shorter events, 0.1 us)
Async XLA Ops:
  0.6 5.2 %copy-start.15 = (f32[16,6,64,1]{2,0,3,1:T(8,128)S(1)}, f32[16,6,64,1]{2,0,3,1:T(8,128)}, u32[]{:S(2)}) copy-start(f32[16,6,64,1]{2,0,3,1:T(8,128)} %constant.121) | copy-start | bytes 73732
  1.4 2.4 %copy-start.12 = (s32[6144]{0:T(1024)}, s32[6144]{0:T(1024)S(1)}, u32[]{:S(2)}) copy-start(s32[6144]{0:T(1024)S(1)} %reshape.169.idx_ref) | copy-start | bytes 73732
  5.8 11.2 %copy-start.1 = (f32[6,1024,16]{2,1,0:T(8,128)}, f32[6,1024,16]{2,1,0:T(8,128)S(1)}, u32[]{:S(2)}) copy-start(f32[6,1024,16]{2,1,0:T(8,128)S(1)} %copy.33) | copy-start | bytes 1179652
  9.8 3.7 %copy-start.2 = (f32[6,1024,16,5]{1,2,3,0:T(8,128)}, f32[6,1024,16,5]{1,2,3,0:T(8,128)S(1)}, u32[]{:S(2)}) copy-start(f32[6,1024,16,5]{1,2,3,0:T(8,128)S(1)} %convolution_bitcast_fusion) | copy-start | bytes 5898244
  17.0 9.6 %copy-start.10 = (s32[8192,1]{0,1:T(1,128)S(1)}, s32[8192,1]{0,1:T(1,128)}, u32[]{:S(2)}) copy-start(s32[8192,1]{0,1:T(1,128)} %param.20) | copy-start | bytes 98308
  17.0 9.6 %copy-start.16 = (bf16[128,128,1]{1,0,2:T(8,128)(2,1)S(1)}, bf16[128,128,1]{1,0,2:T(8,128)(2,1)}, u32[]{:S(2)}) copy-start(bf16[128,128,1]{1,0,2:T(8,128)(2,1)} %constant.123) | copy-start | bytes 98308
  17.0 10.2 %copy-start.19 = (bf16[64,64]{1,0:T(8,128)(2,1)S(1)}, bf16[64,64]{1,0:T(8,128)(2,1)}, u32[]{:S(2)}) copy-start(bf16[64,64]{1,0:T(8,128)(2,1)} %constant.117.clone) | copy-start | bytes 24580
  17.0 11.1 %copy-start.14 = (f32[3,8192]{1,0:T(4,128)S(1)}, f32[3,8192]{1,0:T(4,128)}, u32[]{:S(2)}) copy-start(f32[3,8192]{1,0:T(4,128)} %param.19) | copy-start | bytes 294916
  24.7 16.8 %collective-permute-start.1 = (f32[64,96]{1,0:T(8,128)}, f32[64,96]{1,0:T(8,128)}, u32[]{:S(2)}, u32[]{:S(2)}) collective-permute-start(f32[64,96]{1,0:T(8,128)} %get-tuple-element.21), channel_id=1, source_target_pairs={{16,0},{32,16},{48,32},{64,48},{80,64},{96,80},{112,96},{0,112},{1... | collective-permute-start | bytes 73736 | tf_op jit(solution)/shard_map/ppermute | solution.py:22
  25.4 16.1 %collective-permute-start = (f32[64,96]{1,0:T(8,128)}, f32[64,96]{1,0:T(8,128)}, u32[]{:S(2)}, u32[]{:S(2)}) collective-permute-start(f32[64,96]{1,0:T(8,128)} %get-tuple-element.20), channel_id=1, source_target_pairs={{0,16},{16,32},{32,48},{48,64},{64,80},{80,96},{96,112},{112,0},{1... | collective-permute-start | bytes 73736 | tf_op jit(solution)/shard_map/ppermute | solution.py:21
  34.3 1.8 %copy-start.5 = (f32[5,64,1024]{2,1,0:T(8,128)S(1)}, f32[5,64,1024]{2,1,0:T(8,128)}, u32[]{:S(2)}) copy-start(f32[5,64,1024]{2,1,0:T(8,128)} %param.13) | copy-start | bytes 3932164
  34.4 1.8 %copy-start.13 = (f32[3,64,64,1]{2,1,3,0:T(8,128)S(1)}, f32[3,64,64,1]{2,1,3,0:T(8,128)}, u32[]{:S(2)}) copy-start(f32[3,64,64,1]{2,1,3,0:T(8,128)} %constant.120) | copy-start | bytes 147460
  34.4 1.7 %copy-start.18 = (f32[3,1024]{1,0:T(4,128)S(1)}, f32[3,1024]{1,0:T(4,128)}, u32[]{:S(2)}) copy-start(f32[3,1024]{1,0:T(4,128)} %param.14) | copy-start | bytes 36868
  36.1 4.4 %copy-start.8 = (f32[16,6,1024]{2,1,0:T(8,128)S(1)}, f32[16,6,1024]{2,1,0:T(8,128)}, u32[]{:S(2)}) copy-start(f32[16,6,1024]{2,1,0:T(8,128)} %reshape.168) | copy-start | bytes 1179652
  36.1 5.4 %copy-start.11 = (f32[64,1024]{1,0:T(8,128)S(1)}, f32[64,1024]{1,0:T(8,128)}, u32[]{:S(2)}) copy-start(f32[64,1024]{1,0:T(8,128)} %param.15) | copy-start | bytes 786436
  53.4 6.5 %copy-start = (f32[6144,96]{1,0:T(8,128)S(1)}, f32[6144,96]{1,0:T(8,128)}, u32[]{:S(2)}) copy-start(f32[6144,96]{1,0:T(8,128)} %shard_map.143) | copy-start | bytes 7077892
  62.1 3.4 %copy-start.4 = (f32[6144,16]{1,0:T(8,128)S(1)}, f32[6144,16]{1,0:T(8,128)}, u32[]{:S(2)}) copy-start(f32[6144,16]{1,0:T(8,128)} %get-tuple-element.3) | copy-start | bytes 1179652
  67.3 3.1 %copy-start.3 = (f32[6,1024,16,5]{1,2,3,0:T(8,128)S(1)}, f32[6,1024,16,5]{1,2,3,0:T(8,128)}, u32[]{:S(2)}) copy-start(f32[6,1024,16,5]{1,2,3,0:T(8,128)} %copy-done.2) | copy-start | bytes 5898244
  67.3 3.1 %copy-start.6 = (f32[5,64,1024]{2,1,0:T(8,128)S(1)}, f32[5,64,1024]{2,1,0:T(8,128)}, u32[]{:S(2)}) copy-start(f32[5,64,1024]{2,1,0:T(8,128)} %param.13) | copy-start | bytes 3932164
  77.3 0.8 copy-start.20
  87.0 9.6 %copy-start.7 = (f32[64,8192]{1,0:T(8,128)S(1)}, f32[64,8192]{1,0:T(8,128)}, u32[]{:S(2)}) copy-start(f32[64,8192]{1,0:T(8,128)} %bitcast_multiply_fusion) | copy-start | bytes 6291460
  96.6 1.5 %copy-start.9 = (pred[8192,16]{0,1:T(8,128)(4,1)S(1)}, pred[8192,16]{0,1:T(8,128)(4,1)}, u32[]{:S(2)}) copy-start(pred[8192,16]{0,1:T(8,128)(4,1)} %iota_compare_fusion.7) | copy-start | bytes 393220
  103.4 0.8 copy-start.17
where the time goes:
time: 133 us; the launch traced here: 132 us
  matrix products  41.3 us (31%)
  local copies, waits for them, and re-layouts  35.4 us (27%)
  other arithmetic  22.3 us (17%)
  blocking collectives  19.8 us (15%)
  Pallas kernels  10.5 us (8%)
  starting transfers between devices  1.86 us (1%)
    all_to_all x1, blocking collectives, on_device(): got = lax.all_to_all(send, 'bulk', 0, 0, tiled=True)  19.8 us
    pallas_call x1, Pallas kernels, take_rows(): pl.pallas_call(_rows_kernel, out_shape=jax.ShapeDtypeStruct((idx.shape[0]...  10.5 us
    dot_general x1, matrix products, pick_dot(): out = jnp.dot(hi, onehot, preferred_element_type=jnp.float32)  9.57 us
    dot_general x1, matrix products, pick_dot(): return out + jnp.dot(lo, onehot, preferred_element_type=jnp.float32)  8.93 us
    dot_general x1, matrix products, on_device(): jnp.dot(by_rank, jnp.concatenate([hi, lo], axis=1), preferred_element_typ...  7.27 us
    dot_general x1, matrix products, surface_term(): jnp.einsum('pqf,feqv->vpe', lift_faces, jump_term, precision=lax.Precisio...  6.84 us
    mul x1, other arithmetic, surface_term(): 0.5 * normal * (values + outer_vals)  6.52 us
    concatenate x1, other arithmetic, on_device(): jnp.concatenate([values.reshape(faces_total, 16 * nvars), speeds], axis=1)  4.48 us
  transfers between devices with their start and end apart: 2, of which 0 were waited for; matrix products, arithmetic and copies ran while one was open for 11% of the time, Pallas kernels for 0%

commit v1 on v0

--- a/solution.py
+++ b/solution.py
@@ -106,8 +106,8 @@
 
 def pick_dot(rows, onehot):
     hi, lo = split_bf16(rows)
-    out = jnp.dot(hi, onehot, preferred_element_type=jnp.float32)
-    return out + jnp.dot(lo, onehot, preferred_element_type=jnp.float32)
+    both = jnp.dot(jnp.concatenate([hi, lo], axis=0), onehot, preferred_element_type=jnp.float32)
+    return both[: rows.shape[0]] + both[rows.shape[0] :]
 
 
 def _rows_kernel(idx_ref, own_ref, recv_ref, out_ref, table_ref):
@@ -218,9 +218,13 @@
     capacity = 2 * receptors // buckets
     owners = owner_list[:, 0]
     ranks = owner_ranks(owners, buckets)
-    chosen = owners[:, None] == jnp.arange(buckets, dtype=jnp.int32)[None, :]
-    masked = jnp.where(chosen[:, :, None], jnp.transpose(receptor_vals)[:, None, :], 0.0)
-    hi, lo = split_bf16(masked.reshape(receptors, buckets * nvars))
+    copies = jnp.asarray(np.tile(np.eye(nvars), (1, buckets)), jnp.float32)
+    spread = lax.dot_general(
+        receptor_vals, copies, (((0,), (0,)), ((), ())), precision=lax.Precision.HIGHEST
+    )
+    column_owner = jnp.arange(buckets * nvars, dtype=jnp.int32) // nvars
+    masked = jnp.where(owners[:, None] == column_owner[None, :], spread, 0.0)
+    hi, lo = split_bf16(masked)
     by_rank = (jnp.arange(capacity, dtype=jnp.int32)[:, None] == ranks[None, :]).astype(jnp.bfloat16)
     both = jnp.dot(by_rank, jnp.concatenate([hi, lo], axis=1), preferred_element_type=jnp.float32)
     placed = both[:, : buckets * nvars] + both[:, buckets * nvars :]

time: 133 us -> 145 us (1.090); the launches traced: 132 us -> 143 us
  other arithmetic: 22.3 us -> 35 us
  blocking collectives: 19.8 us -> 18 us
    add x0 -> x1, other arithmetic: none -> 12.9 us  [pick_dot(): return both[:rows.shape[0]] + both[rows.shape[0]:]]
    reduce_sum x1, other arithmetic: 1.5 us -> 5.49 us  [receptor_rows(): return jnp.sum(picked * weights[None], axis=1)]
    select_n x1 -> x0, local copies, waits for them, and re-layouts: 2.73 us -> none  [on_device(): jnp.where(chosen[:, :, None], jnp.transpose(receptor_vals)[:, None, :], 0.0)]
    select_n x1, other arithmetic: 2.56 us -> 0.01 us  [on_device(): column_owner = jnp.arange(buckets * nvars, dtype=jnp.int32) // nvars]
    another operation x1, local copies, waits for them, and re-layouts: 0.18 us -> 2.03 us  [receptor_rows(): jnp.tile(jnp.repeat(basis_y, 4, axis=0), (4, 1))]
    dot_general x2, matrix products: 18.5 us -> 16.7 us  [the longest x1 14.1 us: pick_dot(): jnp.dot(jnp.concatenate([hi, lo], axis=0), onehot, preferred_element_type...]
    all_to_all x1, blocking collectives: 19.8 us -> 18 us  [on_device(): got = lax.all_to_all(send, 'bulk', 0, 0, tiled=True)]
    dot_general x1, matrix products: 4.38 us -> 5.94 us  [volume_term(): jnp.einsum('dpq,vqe->dvpe', derivative, solution, precision=lax.Precision...]
  transfers between devices with their start and end apart: 2 -> 2, of which waited for: 0 -> 0; matrix products, arithmetic and copies ran while one was open for 11% -> 13% of each run, Pallas kernels for 0% -> 0%
where the time goes in v1:
time: 145 us; the launch traced here: 143 us
  matrix products  40.2 us (28%)
  local copies, waits for them, and re-layouts  36.3 us (25%)
  other arithmetic  35 us (24%)
  blocking collectives  18 us (12%)
  Pallas kernels  10.5 us (7%)
  starting transfers between devices  1.86 us (1%)
    all_to_all x1, blocking collectives, on_device(): got = lax.all_to_all(send, 'bulk', 0, 0, tiled=True)  18 us
    dot_general x1, matrix products, pick_dot(): jnp.dot(jnp.concatenate([hi, lo], axis=0), onehot, preferred_element_type...  14.1 us
    add x1, other arithmetic, pick_dot(): return both[:rows.shape[0]] + both[rows.shape[0]:]  12.9 us
    pallas_call x1, Pallas kernels, take_rows(): pl.pallas_call(_rows_kernel, out_shape=jax.ShapeDtypeStruct((idx.shape[0]...  10.5 us
    dot_general x1, matrix products, on_device(): jnp.dot(by_rank, jnp.concatenate([hi, lo], axis=1), preferred_element_typ...  7.28 us
    dot_general x1, matrix products, surface_term(): jnp.einsum('pqf,feqv->vpe', lift_faces, jump_term, precision=lax.Precisio...  6.9 us
    dot_general x1, matrix products, volume_term(): jnp.einsum('dpq,vqe->dvpe', derivative, solution, precision=lax.Precision...  5.94 us
    reduce_sum x1, other arithmetic, receptor_rows(): return jnp.sum(picked * weights[None], axis=1)  5.49 us
  transfers between devices with their start and end apart: 2, of which 0 were waited for; matrix products, arithmetic and copies ran while one was open for 13% of the time, Pallas kernels for 0%

profile of v1, /device:TPU:9, one launch (start us, length us, event | category | flops | bytes accessed | tf_op | source)
XLA Modules:
  0.0 142.6 jit_solution(9488062571738816602)
XLA Ops:
  0.6 0.0 copy-start.17
  0.7 0.8 reshape.154.idx_ref
  1.4 0.6 select_reduce_fusion
  2.0 1.8 %reshape.153 = f32[16,6,1024]{2,1,0:T(8,128)} reshape(f32[96,1024]{1,0:T(8,128)} %param.17) | data formatting | bytes 786432 | tf_op jit(solution)/shard_map/reshape | solution.py:90
  3.8 0.0 copy-done.11
  3.8 1.9 %copy.34 = f32[6,1024,16]{2,1,0:T(8,128)S(1)} copy(f32[6,1024,16]{1,0,2:T(8,128)} %bitcast.76) | data formatting | bytes 786432 | tf_op jit(solution)/shard_map/transpose | solution.py:90
  5.8 0.0 copy-done.17
  5.8 3.0 %convolution_bitcast_fusion = f32[6,1024,16,5]{1,2,3,0:T(8,128)S(1)} fusion(f32[16,6,64,1]{2,0,3,1:T(8,128)S(1)} %copy-done.17, f32[5,64,1024]{2,1,0:T(8,128)} %param.14), kind=kOutput, calls=%fused_computation.33 | convolution fusion | flops 377487360 | bytes 3301376 | tf_op jit(solution)/shard_map/qfp,vpe->feqv/dot_general | solution.py:88
  8.8 0.0 copy-start.1
  8.8 1.2 copy.35
  10.0 2.5 %copy.46 = f32[10,8,6,1024]{3,1,2,0:T(8,128)} copy(f32[10,8,6,1024]{3,2,1,0:T(8,128)S(1)} %bitcast.74) | data formatting | bytes 3932160
  12.5 0.0 copy-done.1
  12.5 3.4 %copy.36 = f32[6144,80]{1,0:T(8,128)} copy(f32[6144,80]{0,1:T(8,128)} %bitcast.75) | data formatting | bytes 3932160 | tf_op jit(solution)/shard_map/reshape;reshape | solution.py:207
  15.9 4.5 %pad_maximum_fusion.own_ref = f32[6144,96]{1,0:T(8,128)} fusion(f32[6144,16]{1,0:T(8,128)S(1)} %bitcast.71, f32[6144,80]{1,0:T(8,128)} %copy.36), kind=kLoop, calls=%fused_computation.14 | loop fusion | flops 589824 | bytes 4718592 | tf_op jit(solution)/shard_map/concatenate | solution.py:207
  20.4 2.5 %gather_fusion = f32[128,96]{1,0:T(8,128)S(1)} fusion(f32[6144,96]{1,0:T(8,128)} %pad_maximum_fusion.own_ref, s32[1024]{0:T(1024)S(1)} %pad_clamp_fusion), kind=kCustom, calls=%fused_computation | custom fusion | bytes 98816 | tf_op jit(solution)/shard_map/jit(_take)/gather | solution.py:99
  22.9 0.1 broadcast_select_fusion
  23.0 0.6 fusion.42
  23.6 1.9 %collective-permute-start = (f32[64,96]{1,0:T(8,128)}, f32[64,96]{1,0:T(8,128)}, u32[]{:S(2)}, u32[]{:S(2)}) collective-permute-start(f32[64,96]{1,0:T(8,128)} %get-tuple-element.20), channel_id=1, source_target_pairs={{0,16},{16,32},{32,48},{48,64},{64,80},{80,96},{96,112},{112,0},{1... | collective-permute-start | bytes 73736 | tf_op jit(solution)/shard_map/ppermute | solution.py:21
  25.5 0.0 collective-permute-start.1
  25.5 0.8 multiply_multiply_fusion.11
  26.3 0.2 pad_maximum_fusion.1
  26.5 0.9 broadcast_in_dim.55
  27.4 2.0 %tile.8 = f32[16,8192]{1,0:T(8,128)} reshape(f32[4,4,8192]{2,1,0:T(4,128)} %broadcast_in_dim.55) | data formatting | bytes 1048576 | tf_op jit(solution)/shard_map/tile | solution.py:189
  29.4 0.1 pad_maximum_fusion.3
  29.6 1.8 %tile.19 = f32[16,4,8192]{2,1,0:T(4,128)} broadcast(f32[4,8192]{1,0:T(4,128)S(1)} %pad_maximum_fusion.3), dimensions={1,2} | broadcast | bytes 2228224 | tf_op jit(solution)/shard_map/tile | solution.py:190
  31.3 0.0 copy-start.20
  31.3 3.0 %tile.20 = f32[64,8192]{1,0:T(8,128)} reshape(f32[16,4,8192]{2,1,0:T(4,128)} %tile.19) | data formatting | bytes 4194304 | tf_op jit(solution)/shard_map/tile | solution.py:190
  34.3 0.0 copy-done.12
  34.3 0.2 fusion.35
  34.6 0.3 fusion.37
  34.9 0.1 fusion.43
  35.0 0.2 select_reduce_fusion.1
  35.3 0.6 add_bitcast_fusion
  35.9 0.0 copy-done.14
  35.9 5.9 %multiply_reduce_fusion.1 = f32[64,5,1024]{2,0,1:T(8,128)} fusion(f32[3,64,64,1]{2,1,3,0:T(8,128)S(1)} %copy-done.14, f32[3,1024]{1,0:T(4,128)S(1)} %copy-done.20, f32[5,64,1024]{2,1,0:T(8,128)} %param.14), kind=kOutput, calls=%fused_computation.10 | convolution fusion | flops 756613120 | bytes 2682880 | tf_op jit(solution)/shard_map/dpq,vqe->dvpe/dot_general | solution.py:177
  41.8 0.2 broadcast_multiply_fusion.1
  42.0 0.0 copy-start.5
  42.0 0.0 copy-start.10
  42.0 1.5 %bitcast_multiply_fusion = f32[64,8192]{1,0:T(8,128)} fusion(f32[64,8192]{1,0:T(8,128)S(1)} %copy-done.4, f32[4,16,8192]{2,1,0:T(8,128)S(1)} %broadcast_multiply_fusion.1), kind=kLoop, calls=%fused_computation.21 | loop fusion | flops 524288 | bytes 6291456 | tf_op jit(solution)/shard_map/mul | solution.py:188
  43.6 0.2 copy.42
  43.8 0.7 neg.4
  44.5 0.0 collective-permute-done
  44.5 0.0 collective-permute-done.1
  44.5 1.4 pad_maximum_fusion.4.recv_ref
  46.0 10.5 %shard_map.149 = f32[6144,96]{1,0:T(8,128)} custom-call(s32[6144]{0:T(1024)} %copy-done.11, f32[6144,96]{1,0:T(8,128)} %pad_maximum_fusion.own_ref, f32[128,96]{1,0:T(8,128)} %pad_maximum_fusion.4.recv_ref), custom_call_target="tpu_custom_call" | custom-call | bytes 7127040 | tf_op jit(solution)/shard_map/pallas_call | solution.py:130
  56.4 5.4 %broadcast_multiply_fusion = (f32[6144,16]{1,0:T(8,128)}, f32[6144,16]{1,0:T(8,128)}) fusion(f32[6144,96]{1,0:T(8,128)} %shard_map.149, f32[6,1024,16]{2,1,0:T(8,128)S(1)} %copy.34), kind=kLoop, calls=%fused_computation.34 | loop fusion | flops 491520 | bytes 1572864 | tf_op jit(solution)/shard_map/mul | solution.py:170
  61.8 3.0 %copy.37 = f32[6,1024,16]{1,2,0:T(8,128)} copy(f32[6,1024,16]{2,1,0:T(8,128)} %bitcast.73) | data formatting | bytes 786432 | tf_op jit(solution)/shard_map/mul | solution.py:170
  64.8 3.1 %copy.40 = f32[6,1024,16]{1,2,0:T(8,128)} copy(f32[6,1024,16]{2,1,0:T(8,128)} %bitcast.72) | data formatting | bytes 786432 | tf_op jit(solution)/shard_map/mul | solution.py:170
  68.0 2.1 %copy.38 = f32[6144,80]{0,1:T(8,128)} copy(f32[6144,80]{1,0:T(8,128)S(1)} %bitcast.70) | data formatting | bytes 3932160 | tf_op jit(solution)/shard_map/slice | solution.py:166
  70.1 0.0 copy-start.16
  70.2 3.5 %reshape.156 = f32[6,1024,16,5]{1,0,3,2:T(8,128)} reshape(f32[6144,80]{0,1:T(8,128)} %copy.38) | data formatting | bytes 3932160 | tf_op jit(solution)/shard_map/reshape | solution.py:166
  73.6 0.0 copy-done.9
  73.6 0.0 copy-done.16
  73.6 6.9 %multiply_add_fusion = (f32[5,64,1024]{2,1,0:T(8,128)S(1)}, f32[5,64,1024]{2,1,0:T(8,128)}) fusion(f32[5,64,1024]{2,1,0:T(8,128)} %param.14, f32[64,16,6,1]{0,1,3,2:T(8,128)S(1)} %copy-done.16, f32[6,1024,16,5]{1,2,3,0:T(8,128)S(1)} %copy-done.2, f32[6,1024,16,5]{1,0,3,2:T(8,128)} %reshape.156, f32[6,1024,16]{1,2,0:T(8,128)S(1)} %copy.42, ...), kind=kOutput, calls=%fused_computation.44 | convolution fusion | flops 382238720 | bytes 10641408 | tf_op jit(solution)/shard_map/pqf,feqv->vpe/dot_general | solution.py:173
  80.5 0.2 reduce-precision_convert_fusion.1
  80.7 0.6 copy-done.22
  81.3 14.1 %fusion = f32[640,8192]{1,0:T(8,128)} fusion(s32[8192]{0:T(1024)S(1)} %copy-done.22, bf16[320,1024]{1,0:T(8,128)(2,1)S(1)} %get-tuple-element.7, bf16[320,1024]{1,0:T(8,128)(2,1)S(1)} %get-tuple-element.6), kind=kOutput, calls=%fused_computation.3 | convolution fusion | flops 10748428288 | bytes 22315008 | tf_op jit(solution)/shard_map/dot_general | solution.py:109
  95.4 12.9 %slice_add_fusion = f32[320,8192]{1,0:T(8,128)} fusion(f32[640,8192]{1,0:T(8,128)} %fusion), kind=kLoop, calls=%fused_computation.7 | loop fusion | flops 2621440 | bytes 31457280 | tf_op jit(solution)/shard_map/add | solution.py:110
  108.4 5.5 %multiply_reduce_fusion = f32[5,8192]{1,0:T(8,128)S(1)} fusion(f32[5,64,8192]{2,1,0:T(8,128)} %bitcast.69, f32[64,8192]{1,0:T(8,128)S(1)} %copy-done.3), kind=kLoop, calls=%fused_computation.8 | loop fusion | flops 5201920 | bytes 12746752 | tf_op jit(solution)/shard_map/reduce_sum | solution.py:194
  113.9 2.6 %reduce-precision_convert_fusion = (bf16[8192,80]{0,1:T(8,128)(2,1)S(1)}, bf16[8192,80]{0,1:T(8,128)(2,1)S(1)}) fusion(f32[5,8192]{1,0:T(8,128)S(1)} %multiply_reduce_fusion, f32[5,80]{1,0:T(8,128)S(1)} %copy-done.23, s32[80]{0:T(128)S(1)} %and_select_fusion, s32[8192]{0:T(1024)S(1)} %bitcast.82), kind=kOutput, calls=%fused_computation.12 | convolution fusion | flops 43253760 | bytes 2819968 | tf_op jit(solution)/shard_map/dot_general | solution.py:222
  116.5 7.3 %fusion.1 = f32[1024,160]{0,1:T(8,128)S(1)} fusion(s32[8192]{0:T(1024)S(1)} %copy-done.19, bf16[8192,80]{0,1:T(8,128)(2,1)S(1)} %get-tuple-element.5, bf16[8192,80]{0,1:T(8,128)(2,1)S(1)} %get-tuple-element.4), kind=kOutput, calls=%fused_computation.4 | convolution fusion | flops 2697986048 | bytes 3309568 | tf_op jit(solution)/shard_map/dot_general | solution.py:229
  123.8 0.1 reshape.160
  123.9 18.0 %all_to_all.5 = f32[16,5,1024]{2,1,0:T(8,128)S(1)} all-to-all(f32[16,5,1024]{2,1,0:T(8,128)S(1)} %bitcast.79), channel_id=1, replica_groups=mesh['valve'=8,'bulk'=16] {'bulk'}, dimensions={0} | all-to-all | bytes 655360 | tf_op jit(solution)/shard_map/all_to_all | solution.py:232
  141.8 0.8 copy.60
  (40 shorter events, 0.1 us)
Async XLA Ops:
  0.6 5.2 %copy-start.17 = (f32[16,6,64,1]{2,0,3,1:T(8,128)S(1)}, f32[16,6,64,1]{2,0,3,1:T(8,128)}, u32[]{:S(2)}) copy-start(f32[16,6,64,1]{2,0,3,1:T(8,128)} %constant.133) | copy-start | bytes 73732
  1.4 2.4 %copy-start.11 = (s32[6144]{0:T(1024)}, s32[6144]{0:T(1024)S(1)}, u32[]{:S(2)}) copy-start(s32[6144]{0:T(1024)S(1)} %reshape.154.idx_ref) | copy-start | bytes 73732
  8.8 3.7 %copy-start.1 = (f32[6,1024,16,5]{1,2,3,0:T(8,128)}, f32[6,1024,16,5]{1,2,3,0:T(8,128)S(1)}, u32[]{:S(2)}) copy-start(f32[6,1024,16,5]{1,2,3,0:T(8,128)S(1)} %convolution_bitcast_fusion) | copy-start | bytes 5898244
  15.9 9.6 %copy-start.15 = (f32[3,8192]{1,0:T(4,128)S(1)}, f32[3,8192]{1,0:T(4,128)}, u32[]{:S(2)}) copy-start(f32[3,8192]{1,0:T(4,128)} %param.20) | copy-start | bytes 294916
  23.6 20.9 %collective-permute-start = (f32[64,96]{1,0:T(8,128)}, f32[64,96]{1,0:T(8,128)}, u32[]{:S(2)}, u32[]{:S(2)}) collective-permute-start(f32[64,96]{1,0:T(8,128)} %get-tuple-element.20), channel_id=1, source_target_pairs={{0,16},{16,32},{32,48},{48,64},{64,80},{80,96},{96,112},{112,0},{1... | collective-permute-start | bytes 73736 | tf_op jit(solution)/shard_map/ppermute | solution.py:21
  25.5 19.1 %collective-permute-start.1 = (f32[64,96]{1,0:T(8,128)}, f32[64,96]{1,0:T(8,128)}, u32[]{:S(2)}, u32[]{:S(2)}) collective-permute-start(f32[64,96]{1,0:T(8,128)} %get-tuple-element.21), channel_id=1, source_target_pairs={{16,0},{32,16},{48,32},{64,48},{80,64},{96,80},{112,96},{0,112},{1... | collective-permute-start | bytes 73736 | tf_op jit(solution)/shard_map/ppermute | solution.py:22
  31.3 3.0 %copy-start.12 = (s32[8192,1]{0,1:T(1,128)S(1)}, s32[8192,1]{0,1:T(1,128)}, u32[]{:S(2)}) copy-start(s32[8192,1]{0,1:T(1,128)} %param.21) | copy-start | bytes 98308
  31.3 3.0 %copy-start.18 = (bf16[128,128,1]{1,0,2:T(8,128)(2,1)S(1)}, bf16[128,128,1]{1,0,2:T(8,128)(2,1)}, u32[]{:S(2)}) copy-start(bf16[128,128,1]{1,0,2:T(8,128)(2,1)} %constant.135) | copy-start | bytes 98308
  31.3 3.6 %copy-start.21 = (bf16[64,64]{1,0:T(8,128)(2,1)S(1)}, bf16[64,64]{1,0:T(8,128)(2,1)}, u32[]{:S(2)}) copy-start(bf16[64,64]{1,0:T(8,128)(2,1)} %constant.128.clone) | copy-start | bytes 24580
  31.3 4.6 %copy-start.14 = (f32[3,64,64,1]{2,1,3,0:T(8,128)S(1)}, f32[3,64,64,1]{2,1,3,0:T(8,128)}, u32[]{:S(2)}) copy-start(f32[3,64,64,1]{2,1,3,0:T(8,128)} %constant.132) | copy-start | bytes 147460
  31.3 4.5 %copy-start.20 = (f32[3,1024]{1,0:T(4,128)S(1)}, f32[3,1024]{1,0:T(4,128)}, u32[]{:S(2)}) copy-start(f32[3,1024]{1,0:T(4,128)} %param.15) | copy-start | bytes 36868
  34.3 7.5 %copy-start.6 = (f32[16,8192]{1,0:T(8,128)S(1)}, f32[16,8192]{1,0:T(8,128)}, u32[]{:S(2)}) copy-start(f32[16,8192]{1,0:T(8,128)} %tile.8) | copy-start | bytes 1572868
  35.9 6.1 %copy-start.4 = (f32[64,8192]{1,0:T(8,128)S(1)}, f32[64,8192]{1,0:T(8,128)}, u32[]{:S(2)}) copy-start(f32[64,8192]{1,0:T(8,128)} %tile.20) | copy-start | bytes 6291460
  42.0 1.6 %copy-start.5 = (f32[16,6,1024]{2,1,0:T(8,128)S(1)}, f32[16,6,1024]{2,1,0:T(8,128)}, u32[]{:S(2)}) copy-start(f32[16,6,1024]{2,1,0:T(8,128)} %reshape.153) | copy-start | bytes 1179652
  42.0 1.8 %copy-start.10 = (f32[64,1024]{1,0:T(8,128)S(1)}, f32[64,1024]{1,0:T(8,128)}, u32[]{:S(2)}) copy-start(f32[64,1024]{1,0:T(8,128)} %param.16) | copy-start | bytes 786436
  64.8 3.2 %copy-start = (f32[6144,96]{1,0:T(8,128)S(1)}, f32[6144,96]{1,0:T(8,128)}, u32[]{:S(2)}) copy-start(f32[6144,96]{1,0:T(8,128)} %shard_map.149) | copy-start | bytes 7077892
  70.1 3.5 %copy-start.2 = (f32[6,1024,16,5]{1,2,3,0:T(8,128)S(1)}, f32[6,1024,16,5]{1,2,3,0:T(8,128)}, u32[]{:S(2)}) copy-start(f32[6,1024,16,5]{1,2,3,0:T(8,128)} %copy-done.1) | copy-start | bytes 5898244
  70.1 3.5 %copy-start.7 = (f32[6,1024,16]{1,2,0:T(8,128)S(1)}, f32[6,1024,16]{1,2,0:T(8,128)}, u32[]{:S(2)}) copy-start(f32[6,1024,16]{1,2,0:T(8,128)} %copy.37) | copy-start | bytes 1179652
  70.1 3.5 %copy-start.8 = (f32[6,1024,16]{1,2,0:T(8,128)S(1)}, f32[6,1024,16]{1,2,0:T(8,128)}, u32[]{:S(2)}) copy-start(f32[6,1024,16]{1,2,0:T(8,128)} %copy.40) | copy-start | bytes 1179652
  70.1 3.5 %copy-start.9 = (f32[64,1024]{1,0:T(8,128)S(1)}, f32[64,1024]{1,0:T(8,128)}, u32[]{:S(2)}) copy-start(f32[64,1024]{1,0:T(8,128)} %neg.4) | copy-start | bytes 786436
  70.1 3.5 %copy-start.16 = (f32[64,16,6,1]{0,1,3,2:T(8,128)S(1)}, f32[64,16,6,1]{0,1,3,2:T(8,128)}, u32[]{:S(2)}) copy-start(f32[64,16,6,1]{0,1,3,2:T(8,128)} %constant.134) | copy-start | bytes 73732
  80.5 0.8 copy-start.22
  95.4 12.9 %copy-start.3 = (f32[64,8192]{1,0:T(8,128)S(1)}, f32[64,8192]{1,0:T(8,128)}, u32[]{:S(2)}) copy-start(f32[64,8192]{1,0:T(8,128)} %bitcast_multiply_fusion) | copy-start | bytes 6291460
  108.4 5.5 %copy-start.13 = (s32[8192,1]{0,1:T(1,128)S(1)}, s32[8192,1]{0,1:T(1,128)}, u32[]{:S(2)}) copy-start(s32[8192,1]{0,1:T(1,128)} %param.21) | copy-start | bytes 98308
  108.4 5.5 %copy-start.23 = (f32[5,80]{1,0:T(8,128)S(1)}, f32[5,80]{1,0:T(8,128)}, u32[]{:S(2)}) copy-start(f32[5,80]{1,0:T(8,128)} %constant.129.clone) | copy-start | bytes 4804
  113.9 2.6 %copy-start.19 = (s32[8192]{0:T(1024)S(1)}, s32[8192]{0:T(1024)}, u32[]{:S(2)}) copy-start(s32[8192]{0:T(1024)} %add_bitcast_fusion) | copy-start | bytes 98308

commit v2 on v1

--- a/solution.py
+++ b/solution.py
@@ -178,9 +178,22 @@
     return jnp.sum(velocity[:, None, None, :] * slopes, axis=0)
 
 
+def _interp_kernel(rows_ref, donors_ref, weights_ref, out_ref):
+    elems = rows_ref.shape[1]
+    tile = donors_ref.shape[1]
+    half = rows_ref.shape[0] // 2
+    onehot = lax.broadcasted_iota(jnp.int32, (elems, tile), 0) == donors_ref[...]
+    picked = jnp.dot(rows_ref[...], onehot.astype(jnp.bfloat16), preferred_element_type=jnp.float32)
+    picked = picked[:half] + picked[half:]
+    nvars = out_ref.shape[0]
+    picked = picked.reshape(nvars, half // nvars, tile) * weights_ref[...][None]
+    out_ref[...] = jnp.sum(picked, axis=1)
+
+
 def receptor_rows(advanced, donors, coords):
     nvars = advanced.shape[0]
     elems = advanced.shape[2]
+    receptors = donors.shape[0]
     basis_x = jnp.stack(lagrange_at(coords[0]))
     basis_y = jnp.stack(lagrange_at(coords[1]))
     basis_z = jnp.stack(lagrange_at(coords[2]))
@@ -189,9 +202,25 @@
         * jnp.tile(jnp.repeat(basis_y, 4, axis=0), (4, 1))
         * jnp.tile(basis_z, (16, 1))
     )
-    onehot = (jnp.arange(elems, dtype=jnp.int32)[:, None] == donors[None, :]).astype(jnp.bfloat16)
-    picked = pick_dot(advanced.reshape(nvars * 64, elems), onehot).reshape(nvars, 64, -1)
-    return jnp.sum(picked * weights[None], axis=1)
+    hi, lo = split_bf16(advanced.reshape(nvars * 64, elems))
+    rows = jnp.concatenate([hi, lo], axis=0)
+    tile = 512
+    return pl.pallas_call(
+        _interp_kernel,
+        out_shape=jax.ShapeDtypeStruct((nvars, receptors), jnp.float32),
+        grid=(receptors // tile,),
+        in_specs=[
+            pl.BlockSpec((2 * nvars * 64, elems), lambda i: (0, 0)),
+            pl.BlockSpec((1, tile), lambda i: (0, i)),
+            pl.BlockSpec((64, tile), lambda i: (0, i)),
+        ],
+        out_specs=pl.BlockSpec((nvars, tile), lambda i: (0, i)),
+        cost_estimate=pl.CostEstimate(
+            flops=2 * 2 * nvars * 64 * elems * receptors,
+            transcendentals=0,
+            bytes_accessed=2 * nvars * 64 * elems * 2 + receptors * (1 + 64 + nvars) * 4,
+        ),
+    )(rows, donors.reshape(1, receptors), weights)
 
 
 def on_device(

time: 145 us -> 129 us (0.89)
  other arithmetic: 35 us -> 17.8 us
  Pallas kernels: 10.5 us -> 26.8 us
  matrix products: 40.2 us -> 25.4 us
    pallas_call x0 -> x1, Pallas kernels: none -> 16.4 us  [receptor_rows(): pl.pallas_call(_interp_kernel, out_shape=jax.ShapeDtypeStruct((nvars, rec...]
    dot_general x1 -> x0, matrix products: 14.1 us -> none  [pick_dot(): jnp.dot(jnp.concatenate([hi, lo], axis=0), onehot, preferred_element_type...]
    add x1 -> x0, other arithmetic: 12.9 us -> none  [pick_dot(): return both[:rows.shape[0]] + both[rows.shape[0]:]]
    reduce_sum x1 -> x0, other arithmetic: 5.49 us -> none  [receptor_rows(): return jnp.sum(picked * weights[None], axis=1)]
    dot_general x1, matrix products: 5.94 us -> 4.36 us  [volume_term(): jnp.einsum('dpq,vqe->dvpe', derivative, solution, precision=lax.Precision...]
    unnamed x50 -> x48, local copies, waits for them, and re-layouts: 3.97 us -> 3.62 us
  transfers between devices with their start and end apart: 2 -> 2, of which waited for: 0 -> 0; matrix products, arithmetic and copies ran while one was open for 13% -> 14% of each run, Pallas kernels for 0% -> 0%
where the time goes in v2:
time: 129 us; the launch traced here: 127 us
  local copies, waits for them, and re-layouts  35.9 us (28%)
  Pallas kernels  26.8 us (21%)
  matrix products  25.4 us (20%)
  blocking collectives  17.9 us (14%)
  other arithmetic  17.8 us (14%)
  starting transfers between devices  1.86 us (1%)
    all_to_all x1, blocking collectives, on_device(): got = lax.all_to_all(send, 'bulk', 0, 0, tiled=True)  17.9 us
    pallas_call x1, Pallas kernels, receptor_rows(): pl.pallas_call(_interp_kernel, out_shape=jax.ShapeDtypeStruct((nvars, rec...  16.4 us
    pallas_call x1, Pallas kernels, take_rows(): pl.pallas_call(_rows_kernel, out_shape=jax.ShapeDtypeStruct((idx.shape[0]...  10.5 us
    dot_general x1, matrix products, on_device(): jnp.dot(by_rank, jnp.concatenate([hi, lo], axis=1), preferred_element_typ...  7.28 us
    dot_general x1, matrix products, surface_term(): jnp.einsum('pqf,feqv->vpe', lift_faces, jump_term, precision=lax.Precisio...  6.89 us
    mul x1, other arithmetic, surface_term(): 0.5 * normal * (values + outer_vals)  5.43 us
    another operation x2, local copies, waits for them, and re-layouts, receptor_rows(): jnp.tile(basis_z, (16, 1))  4.75 us
    concatenate x1, other arithmetic, on_device(): jnp.concatenate([values.reshape(faces_total, 16 * nvars), speeds], axis=1)  4.46 us
  transfers between devices with their start and end apart: 2, of which 0 were waited for; matrix products, arithmetic and copies ran while one was open for 14% of the time, Pallas kernels for 0%

profile of v2, /device:TPU:9, one launch (start us, length us, event | category | flops | bytes accessed | tf_op | source)
XLA Modules:
  0.0 126.6 jit_solution(9712388769563567054)
XLA Ops:
  0.6 0.8 reshape.135.idx_ref
  1.4 0.6 select_reduce_fusion
  2.0 0.0 copy-start.17
  2.0 1.9 %reshape.134 = f32[16,6,1024]{2,1,0:T(8,128)} reshape(f32[96,1024]{1,0:T(8,128)} %param.17) | data formatting | bytes 786432 | tf_op jit(solution)/shard_map/reshape | solution.py:90
  3.9 0.0 copy-done.11
  3.9 1.9 %copy.34 = f32[6,1024,16]{2,1,0:T(8,128)S(1)} copy(f32[6,1024,16]{1,0,2:T(8,128)} %bitcast.75) | data formatting | bytes 786432 | tf_op jit(solution)/shard_map/transpose | solution.py:90
  5.8 3.0 %convolution_bitcast_fusion = f32[6,1024,16,5]{1,2,3,0:T(8,128)S(1)} fusion(f32[16,6,64,1]{2,0,3,1:T(8,128)S(1)} %copy-done.17, f32[5,64,1024]{2,1,0:T(8,128)} %param.14), kind=kOutput, calls=%fused_computation.28 | convolution fusion | flops 377487360 | bytes 3301376 | tf_op jit(solution)/shard_map/qfp,vpe->feqv/dot_general | solution.py:88
  8.8 1.2 copy.35
  10.0 0.2 copy-done.1
  10.2 2.5 %copy.46 = f32[10,8,6,1024]{3,1,2,0:T(8,128)} copy(f32[10,8,6,1024]{3,2,1,0:T(8,128)S(1)} %bitcast.73) | data formatting | bytes 3932160
  12.8 3.4 %copy.36 = f32[6144,80]{1,0:T(8,128)} copy(f32[6144,80]{0,1:T(8,128)} %bitcast.74) | data formatting | bytes 3932160 | tf_op jit(solution)/shard_map/reshape;reshape | solution.py:236
  16.1 4.5 %pad_maximum_fusion.own_ref = f32[6144,96]{1,0:T(8,128)} fusion(f32[6144,16]{1,0:T(8,128)S(1)} %bitcast.70, f32[6144,80]{1,0:T(8,128)} %copy.36), kind=kLoop, calls=%fused_computation.9 | loop fusion | flops 589824 | bytes 4718592 | tf_op jit(solution)/shard_map/concatenate | solution.py:236
  20.6 2.5 %gather_fusion = f32[128,96]{1,0:T(8,128)S(1)} fusion(f32[6144,96]{1,0:T(8,128)} %pad_maximum_fusion.own_ref, s32[1024]{0:T(1024)S(1)} %pad_clamp_fusion), kind=kCustom, calls=%fused_computation | custom fusion | bytes 98816 | tf_op jit(solution)/shard_map/jit(_take)/gather | solution.py:99
  23.1 0.1 broadcast_select_fusion
  23.2 0.6 fusion.36
  23.9 1.9 %collective-permute-start = (f32[64,96]{1,0:T(8,128)}, f32[64,96]{1,0:T(8,128)}, u32[]{:S(2)}, u32[]{:S(2)}) collective-permute-start(f32[64,96]{1,0:T(8,128)} %get-tuple-element.20), channel_id=1, source_target_pairs={{0,16},{16,32},{32,48},{48,64},{64,80},{80,96},{96,112},{112,0},{1... | collective-permute-start | bytes 73736 | tf_op jit(solution)/shard_map/ppermute | solution.py:21
  25.7 0.0 collective-permute-start.1
  25.7 0.0 copy-done.15
  25.7 0.8 multiply_multiply_fusion.11
  26.5 0.2 pad_maximum_fusion.2
  26.7 0.9 broadcast_in_dim.52
  27.6 2.0 %tile.8 = f32[16,8192]{1,0:T(8,128)} reshape(f32[4,4,8192]{2,1,0:T(4,128)} %broadcast_in_dim.52) | data formatting | bytes 1048576 | tf_op jit(solution)/shard_map/tile | solution.py:202
  29.7 0.1 pad_maximum_fusion.4
  29.8 1.8 %tile.19 = f32[16,4,8192]{2,1,0:T(4,128)} broadcast(f32[4,8192]{1,0:T(4,128)S(1)} %pad_maximum_fusion.4), dimensions={1,2} | broadcast | bytes 2228224 | tf_op jit(solution)/shard_map/tile | solution.py:203
  31.6 0.0 copy-start.20
  31.6 3.0 %tile.20 = f32[64,8192]{1,0:T(8,128)} reshape(f32[16,4,8192]{2,1,0:T(4,128)} %tile.19) | data formatting | bytes 4194304 | tf_op jit(solution)/shard_map/tile | solution.py:203
  34.6 0.2 fusion.30
  34.8 0.4 fusion.32
  35.2 0.1 fusion.37
  35.3 0.2 select_reduce_fusion.1
  35.5 0.6 add_bitcast_fusion
  36.1 4.4 %multiply_reduce_fusion = f32[64,5,1024]{2,0,1:T(8,128)} fusion(f32[3,64,64,1]{2,1,3,0:T(8,128)S(1)} %copy-done.14, f32[3,1024]{1,0:T(4,128)S(1)} %copy-done.20, f32[5,64,1024]{2,1,0:T(8,128)S(1)} %copy-done.3), kind=kOutput, calls=%fused_computation.5 | convolution fusion | flops 756613120 | bytes 2682880 | tf_op jit(solution)/shard_map/dpq,vqe->dvpe/dot_general | solution.py:177
  40.5 0.2 broadcast_multiply_fusion.1
  40.7 0.0 copy-done.4
  40.7 0.0 copy-start.5
  40.7 0.0 copy-start.10
  40.7 1.5 %bitcast_multiply_fusion.weights_ref = f32[64,8192]{1,0:T(8,128)} fusion(f32[64,8192]{1,0:T(8,128)S(1)} %copy-done.4, f32[4,16,8192]{2,1,0:T(8,128)S(1)} %broadcast_multiply_fusion.1), kind=kLoop, calls=%fused_computation.16 | loop fusion | flops 524288 | bytes 6291456 | tf_op jit(solution)/shard_map/mul | solution.py:201
  42.2 0.2 copy.42
  42.5 0.0 copy-done.10
  42.5 0.7 neg.4
  43.2 0.0 collective-permute-done
  43.2 0.0 collective-permute-done.1
  43.2 1.4 %pad_maximum_fusion.5.recv_ref = f32[128,96]{1,0:T(8,128)} fusion(f32[64,96]{1,0:T(8,128)} %collective-permute-done.1, f32[64,96]{1,0:T(8,128)} %collective-permute-done), kind=kLoop, calls=%fused_computation.53 | loop fusion | flops 12288 | bytes 98304 | tf_op jit(solution)/shard_map/concatenate | solution.py:239
  44.6 10.5 %shard_map.149 = f32[6144,96]{1,0:T(8,128)} custom-call(s32[6144]{0:T(1024)} %copy-done.11, f32[6144,96]{1,0:T(8,128)} %pad_maximum_fusion.own_ref, f32[128,96]{1,0:T(8,128)} %pad_maximum_fusion.5.recv_ref), custom_call_target="tpu_custom_call" | custom-call | bytes 7127040 | tf_op jit(solution)/shard_map/pallas_call | solution.py:130
  55.1 5.4 %broadcast_multiply_fusion = (f32[6144,16]{1,0:T(8,128)}, f32[6144,16]{1,0:T(8,128)}) fusion(f32[6144,96]{1,0:T(8,128)} %shard_map.149, f32[6,1024,16]{2,1,0:T(8,128)S(1)} %copy.34), kind=kLoop, calls=%fused_computation.29 | loop fusion | flops 491520 | bytes 1572864 | tf_op jit(solution)/shard_map/mul | solution.py:170
  60.5 3.0 %copy.37 = f32[6,1024,16]{1,2,0:T(8,128)} copy(f32[6,1024,16]{2,1,0:T(8,128)} %bitcast.72) | data formatting | bytes 786432 | tf_op jit(solution)/shard_map/mul | solution.py:170
  63.5 3.1 %copy.40 = f32[6,1024,16]{1,2,0:T(8,128)} copy(f32[6,1024,16]{2,1,0:T(8,128)} %bitcast.71) | data formatting | bytes 786432 | tf_op jit(solution)/shard_map/mul | solution.py:170
  66.7 2.1 %copy.38 = f32[6144,80]{0,1:T(8,128)} copy(f32[6144,80]{1,0:T(8,128)S(1)} %bitcast.69) | data formatting | bytes 3932160 | tf_op jit(solution)/shard_map/slice | solution.py:166
  68.8 0.0 copy-start.16
  68.8 3.4 %reshape.137 = f32[6,1024,16,5]{1,0,3,2:T(8,128)} reshape(f32[6144,80]{0,1:T(8,128)} %copy.38) | data formatting | bytes 3932160 | tf_op jit(solution)/shard_map/reshape | solution.py:166
  72.3 0.0 copy-done.2
  72.3 0.0 copy-done.8
  72.3 6.9 %multiply_add_fusion = (f32[5,64,1024]{2,1,0:T(8,128)S(1)}, f32[5,64,1024]{2,1,0:T(8,128)}) fusion(f32[5,64,1024]{2,1,0:T(8,128)} %param.14, f32[64,16,6,1]{0,1,3,2:T(8,128)S(1)} %copy-done.16, f32[6,1024,16,5]{1,2,3,0:T(8,128)S(1)} %copy-done.2, f32[6,1024,16,5]{1,0,3,2:T(8,128)} %reshape.137, f32[6,1024,16]{1,2,0:T(8,128)S(1)} %copy.42, ...), kind=kOutput, calls=%fused_computation.37 | convolution fusion | flops 382238720 | bytes 10641408 | tf_op jit(solution)/shard_map/pqf,feqv->vpe/dot_general | solution.py:173
  79.2 0.2 reduce-precision_convert_fusion.1
  79.4 1.2 pad_maximum_fusion.1.rows_ref
  80.6 16.4 %shard_map.150 = f32[5,8192]{1,0:T(8,128)} custom-call(bf16[640,1024]{1,0:T(8,128)(2,1)} %pad_maximum_fusion.1.rows_ref, s32[1,8192]{1,0:T(1,128)} %bitcast.82, f32[64,8192]{1,0:T(8,128)} %bitcast_multiply_fusion.weights_ref), custom_call_target="tpu_custom_call" | custom-call | flops 10737418240 | bytes 3604480 | tf_op jit(solution)/shard_map/pallas_call | solution.py:208
  97.0 0.0 copy-done.13
  97.0 0.0 copy-done.22
  97.0 3.5 %reduce-precision_convert_fusion = (bf16[8192,80]{0,1:T(8,128)(2,1)S(1)}, bf16[8192,80]{0,1:T(8,128)(2,1)S(1)}) fusion(f32[5,8192]{1,0:T(8,128)} %shard_map.150, f32[5,80]{1,0:T(8,128)S(1)} %copy-done.22, s32[80]{0:T(128)S(1)} %and_select_fusion, s32[8192]{0:T(1024)S(1)} %bitcast.81), kind=kOutput, calls=%fused_computation.7 | convolution fusion | flops 43253760 | bytes 2819968 | tf_op jit(solution)/shard_map/dot_general | solution.py:251
  100.5 0.0 copy-done.19
  100.5 7.3 %fusion = f32[1024,160]{0,1:T(8,128)S(1)} fusion(s32[8192]{0:T(1024)S(1)} %copy-done.19, bf16[8192,80]{0,1:T(8,128)(2,1)S(1)} %get-tuple-element.5, bf16[8192,80]{0,1:T(8,128)(2,1)S(1)} %get-tuple-element.4), kind=kOutput, calls=%fused_computation.2 | convolution fusion | flops 2697986048 | bytes 3309568 | tf_op jit(solution)/shard_map/dot_general | solution.py:258
  107.8 0.1 reshape.141
  107.9 17.9 %all_to_all.5 = f32[16,5,1024]{2,1,0:T(8,128)S(1)} all-to-all(f32[16,5,1024]{2,1,0:T(8,128)S(1)} %bitcast.78), channel_id=1, replica_groups=mesh['valve'=8,'bulk'=16] {'bulk'}, dimensions={0} | all-to-all | bytes 655360 | tf_op jit(solution)/shard_map/all_to_all | solution.py:261
  125.8 0.8 copy.60
  (37 shorter events, 0.1 us)
Async XLA Ops:
  1.4 2.4 %copy-start.11 = (s32[6144]{0:T(1024)}, s32[6144]{0:T(1024)S(1)}, u32[]{:S(2)}) copy-start(s32[6144]{0:T(1024)S(1)} %reshape.135.idx_ref) | copy-start | bytes 73732
  2.0 3.8 %copy-start.17 = (f32[16,6,64,1]{2,0,3,1:T(8,128)S(1)}, f32[16,6,64,1]{2,0,3,1:T(8,128)}, u32[]{:S(2)}) copy-start(f32[16,6,64,1]{2,0,3,1:T(8,128)} %constant.133) | copy-start | bytes 73732
  8.8 1.4 %copy-start.1 = (f32[6,1024,16,5]{1,2,3,0:T(8,128)}, f32[6,1024,16,5]{1,2,3,0:T(8,128)S(1)}, u32[]{:S(2)}) copy-start(f32[6,1024,16,5]{1,2,3,0:T(8,128)S(1)} %convolution_bitcast_fusion) | copy-start | bytes 5898244
  16.1 9.6 %copy-start.15 = (f32[3,8192]{1,0:T(4,128)S(1)}, f32[3,8192]{1,0:T(4,128)}, u32[]{:S(2)}) copy-start(f32[3,8192]{1,0:T(4,128)} %param.20) | copy-start | bytes 294916
  23.9 19.3 %collective-permute-start = (f32[64,96]{1,0:T(8,128)}, f32[64,96]{1,0:T(8,128)}, u32[]{:S(2)}, u32[]{:S(2)}) collective-permute-start(f32[64,96]{1,0:T(8,128)} %get-tuple-element.20), channel_id=1, source_target_pairs={{0,16},{16,32},{32,48},{48,64},{64,80},{80,96},{96,112},{112,0},{1... | collective-permute-start | bytes 73736 | tf_op jit(solution)/shard_map/ppermute | solution.py:21
  25.7 17.5 %collective-permute-start.1 = (f32[64,96]{1,0:T(8,128)}, f32[64,96]{1,0:T(8,128)}, u32[]{:S(2)}, u32[]{:S(2)}) collective-permute-start(f32[64,96]{1,0:T(8,128)} %get-tuple-element.21), channel_id=1, source_target_pairs={{16,0},{32,16},{48,32},{64,48},{80,64},{96,80},{112,96},{0,112},{1... | collective-permute-start | bytes 73736 | tf_op jit(solution)/shard_map/ppermute | solution.py:22
  31.5 3.0 %copy-start.12 = (s32[8192,1]{0,1:T(1,128)S(1)}, s32[8192,1]{0,1:T(1,128)}, u32[]{:S(2)}) copy-start(s32[8192,1]{0,1:T(1,128)} %param.21) | copy-start | bytes 98308
  31.5 3.0 %copy-start.18 = (bf16[128,128,1]{1,0,2:T(8,128)(2,1)S(1)}, bf16[128,128,1]{1,0,2:T(8,128)(2,1)}, u32[]{:S(2)}) copy-start(bf16[128,128,1]{1,0,2:T(8,128)(2,1)} %constant.135) | copy-start | bytes 98308
  31.5 3.6 %copy-start.21 = (bf16[64,64]{1,0:T(8,128)(2,1)S(1)}, bf16[64,64]{1,0:T(8,128)(2,1)}, u32[]{:S(2)}) copy-start(bf16[64,64]{1,0:T(8,128)(2,1)} %constant.128.clone) | copy-start | bytes 24580
  31.6 4.6 %copy-start.14 = (f32[3,64,64,1]{2,1,3,0:T(8,128)S(1)}, f32[3,64,64,1]{2,1,3,0:T(8,128)}, u32[]{:S(2)}) copy-start(f32[3,64,64,1]{2,1,3,0:T(8,128)} %constant.132) | copy-start | bytes 147460
  31.6 4.6 %copy-start.20 = (f32[3,1024]{1,0:T(4,128)S(1)}, f32[3,1024]{1,0:T(4,128)}, u32[]{:S(2)}) copy-start(f32[3,1024]{1,0:T(4,128)} %param.15) | copy-start | bytes 36868
  34.6 1.6 %copy-start.3 = (f32[5,64,1024]{2,1,0:T(8,128)S(1)}, f32[5,64,1024]{2,1,0:T(8,128)}, u32[]{:S(2)}) copy-start(f32[5,64,1024]{2,1,0:T(8,128)} %param.14) | copy-start | bytes 3932164
  34.6 5.9 %copy-start.6 = (f32[16,8192]{1,0:T(8,128)S(1)}, f32[16,8192]{1,0:T(8,128)}, u32[]{:S(2)}) copy-start(f32[16,8192]{1,0:T(8,128)} %tile.8) | copy-start | bytes 1572868
  36.1 4.5 %copy-start.4 = (f32[64,8192]{1,0:T(8,128)S(1)}, f32[64,8192]{1,0:T(8,128)}, u32[]{:S(2)}) copy-start(f32[64,8192]{1,0:T(8,128)} %tile.20) | copy-start | bytes 6291460
  40.7 1.6 %copy-start.5 = (f32[16,6,1024]{2,1,0:T(8,128)S(1)}, f32[16,6,1024]{2,1,0:T(8,128)}, u32[]{:S(2)}) copy-start(f32[16,6,1024]{2,1,0:T(8,128)} %reshape.134) | copy-start | bytes 1179652
  40.7 1.8 %copy-start.10 = (f32[64,1024]{1,0:T(8,128)S(1)}, f32[64,1024]{1,0:T(8,128)}, u32[]{:S(2)}) copy-start(f32[64,1024]{1,0:T(8,128)} %param.16) | copy-start | bytes 786436
  63.5 3.2 %copy-start = (f32[6144,96]{1,0:T(8,128)S(1)}, f32[6144,96]{1,0:T(8,128)}, u32[]{:S(2)}) copy-start(f32[6144,96]{1,0:T(8,128)} %shard_map.149) | copy-start | bytes 7077892
  68.8 3.5 %copy-start.2 = (f32[6,1024,16,5]{1,2,3,0:T(8,128)S(1)}, f32[6,1024,16,5]{1,2,3,0:T(8,128)}, u32[]{:S(2)}) copy-start(f32[6,1024,16,5]{1,2,3,0:T(8,128)} %copy-done.1) | copy-start | bytes 5898244
  68.8 3.5 %copy-start.7 = (f32[6,1024,16]{1,2,0:T(8,128)S(1)}, f32[6,1024,16]{1,2,0:T(8,128)}, u32[]{:S(2)}) copy-start(f32[6,1024,16]{1,2,0:T(8,128)} %copy.37) | copy-start | bytes 1179652
  68.8 3.5 %copy-start.8 = (f32[6,1024,16]{1,2,0:T(8,128)S(1)}, f32[6,1024,16]{1,2,0:T(8,128)}, u32[]{:S(2)}) copy-start(f32[6,1024,16]{1,2,0:T(8,128)} %copy.40) | copy-start | bytes 1179652
  68.8 3.5 %copy-start.9 = (f32[64,1024]{1,0:T(8,128)S(1)}, f32[64,1024]{1,0:T(8,128)}, u32[]{:S(2)}) copy-start(f32[64,1024]{1,0:T(8,128)} %neg.4) | copy-start | bytes 786436
  68.8 3.5 %copy-start.16 = (f32[64,16,6,1]{0,1,3,2:T(8,128)S(1)}, f32[64,16,6,1]{0,1,3,2:T(8,128)}, u32[]{:S(2)}) copy-start(f32[64,16,6,1]{0,1,3,2:T(8,128)} %constant.134) | copy-start | bytes 73732
  80.6 16.4 %copy-start.13 = (s32[8192,1]{0,1:T(1,128)S(1)}, s32[8192,1]{0,1:T(1,128)}, u32[]{:S(2)}) copy-start(s32[8192,1]{0,1:T(1,128)} %param.21) | copy-start | bytes 98308
  80.6 16.4 %copy-start.22 = (f32[5,80]{1,0:T(8,128)S(1)}, f32[5,80]{1,0:T(8,128)}, u32[]{:S(2)}) copy-start(f32[5,80]{1,0:T(8,128)} %constant.129.clone) | copy-start | bytes 4804
  97.0 3.5 %copy-start.19 = (s32[8192]{0:T(1024)S(1)}, s32[8192]{0:T(1024)}, u32[]{:S(2)}) copy-start(s32[8192]{0:T(1024)} %add_bitcast_fusion) | copy-start | bytes 98308

commit v3 on v2

--- a/solution.py
+++ b/solution.py
@@ -91,12 +91,14 @@
     return (values, speeds)
 
 
-def rim_rows(table_own, links, faces_total, rim_count):
+def rim_rows(values, speeds, links, faces_total, rim_count):
     wanted = faces_total + jnp.arange(2 * rim_count, dtype=jnp.int32)
     hits = links[None, :] == wanted[:, None]
     faces = jnp.arange(faces_total, dtype=jnp.int32)[None, :]
     senders = jnp.sum(jnp.where(hits, faces, 0), axis=1)
-    return jnp.take(table_own, senders, axis=0)
+    return jnp.concatenate(
+        [jnp.take(values, senders, axis=0), jnp.take(speeds, senders, axis=0)], axis=1
+    )
 
 
 def split_bf16(x):
@@ -110,9 +112,10 @@
     return both[: rows.shape[0]] + both[rows.shape[0] :]
 
 
-def _rows_kernel(idx_ref, own_ref, recv_ref, out_ref, table_ref):
-    own_rows = own_ref.shape[0]
-    table_ref[pl.ds(0, own_rows), :] = own_ref[...]
+def _rows_kernel(idx_ref, values_ref, speeds_ref, recv_ref, out_ref, table_ref):
+    own_rows, width = values_ref.shape
+    table_ref[pl.ds(0, own_rows), pl.ds(0, width)] = values_ref[...]
+    table_ref[pl.ds(0, own_rows), pl.ds(width, speeds_ref.shape[1])] = speeds_ref[...]
     table_ref[pl.ds(own_rows, recv_ref.shape[0]), :] = recv_ref[...]
 
     def body(i, carry):
@@ -125,22 +128,24 @@
     lax.fori_loop(0, out_ref.shape[0] // 16, body, 0)
 
 
-def take_rows(own, received, idx):
-    rows = own.shape[0] + received.shape[0]
+def take_rows(values, speeds, received, idx):
+    rows = values.shape[0] + received.shape[0]
+    width = received.shape[1]
     return pl.pallas_call(
         _rows_kernel,
-        out_shape=jax.ShapeDtypeStruct((idx.shape[0], own.shape[1]), own.dtype),
+        out_shape=jax.ShapeDtypeStruct((idx.shape[0], width), values.dtype),
         in_specs=[
             pl.BlockSpec(memory_space=pltpu.SMEM),
             pl.BlockSpec(memory_space=pltpu.VMEM),
             pl.BlockSpec(memory_space=pltpu.VMEM),
+            pl.BlockSpec(memory_space=pltpu.VMEM),
         ],
         out_specs=pl.BlockSpec(memory_space=pltpu.VMEM),
-        scratch_shapes=[pltpu.VMEM((rows, own.shape[1]), own.dtype)],
+        scratch_shapes=[pltpu.VMEM((rows, width), values.dtype)],
         cost_estimate=pl.CostEstimate(
-            flops=0, transcendentals=0, bytes_accessed=(2 * idx.shape[0] + rows) * own.shape[1] * 4
+            flops=0, transcendentals=0, bytes_accessed=(2 * idx.shape[0] + rows) * width * 4
         ),
-    )(idx, own, received)
+    )(idx, values, speeds, received)
 
 
 def owner_ranks(owners, buckets):
@@ -162,7 +167,7 @@
 
 def surface_term(values, speeds, table_own, links, received, lifting, elems):
     nvars = values.shape[2]
-    outer = take_rows(table_own, received, links)
+    outer = take_rows(table_own, speeds, received, links)
     outer_vals = outer[:, : 16 * nvars].reshape(6 * elems, 16, nvars)
     outer_speed = outer[:, 16 * nvars :][:, :, None]
     own_speed = speeds[:, :, None]
@@ -233,11 +238,11 @@
     faces_total = 6 * elems
     links = face_link.reshape(faces_total)
     values, speeds = face_rows(solution, face_speed, extrapolate)
-    table_own = jnp.concatenate([values.reshape(faces_total, 16 * nvars), speeds], axis=1)
-    outgoing = rim_rows(table_own, links, faces_total, rim_count)
+    flat_values = values.reshape(faces_total, 16 * nvars)
+    outgoing = rim_rows(flat_values, speeds, links, faces_total, rim_count)
     extended = padded(outgoing, (("valve", 0),), rim_count)
     received = jnp.concatenate([extended[:rim_count], extended[3 * rim_count :]], axis=0)
-    surface = surface_term(values, speeds, table_own, links, received, lifting, elems)
+    surface = surface_term(values, speeds, flat_values, links, received, lifting, elems)
     volume = volume_term(solution, velocity, derivative)
     section_rate = -inv_jacobian[None] * (volume + surface)
     advanced = solution + section_step * section_rate

time: 129 us -> 129 us (level)
  other arithmetic: 17.8 us -> 14.2 us
  matrix products: 25.4 us -> 28.9 us
  Pallas kernels: 26.8 us -> 28.8 us
  local copies, waits for them, and re-layouts: 35.9 us -> 34 us
    concatenate x1, other arithmetic: 4.46 us -> 0.71 us  [rim_rows(): jnp.concatenate([jnp.take(values, senders, axis=0), jnp.take(speeds, send...]
    pallas_call x1, Pallas kernels: 10.5 us -> 12.2 us  [take_rows(): pl.pallas_call(_rows_kernel, out_shape=jax.ShapeDtypeStruct((idx.shape[0]...]
    gather x1 -> x2, local copies, waits for them, and re-layouts: 2.53 us -> 3.18 us  [the longest x1 2.53 us: rim_rows(): jnp.take(values, senders, axis=0)]
    unnamed x48 -> x36, local copies, waits for them, and re-layouts: 3.62 us -> 3.57 us
where the time goes in v3:
time: 129 us; the launch traced here: 127 us
  local copies, waits for them, and re-layouts  34 us (26%)
  matrix products  28.9 us (22%)
  Pallas kernels  28.8 us (22%)
  blocking collectives  17.9 us (14%)
  other arithmetic  14.2 us (11%)
  starting transfers between devices  1.86 us (1%)
    all_to_all x1, blocking collectives, on_device(): got = lax.all_to_all(send, 'bulk', 0, 0, tiled=True)  17.9 us
    pallas_call x1, Pallas kernels, receptor_rows(): pl.pallas_call(_interp_kernel, out_shape=jax.ShapeDtypeStruct((nvars, rec...  16.6 us
    pallas_call x1, Pallas kernels, take_rows(): pl.pallas_call(_rows_kernel, out_shape=jax.ShapeDtypeStruct((idx.shape[0]...  12.2 us
    dot_general x1, matrix products, on_device(): jnp.dot(by_rank, jnp.concatenate([hi, lo], axis=1), preferred_element_typ...  7.27 us
    dot_general x1, matrix products, surface_term(): jnp.einsum('pqf,feqv->vpe', lift_faces, jump_term, precision=lax.Precisio...  6.84 us
    dot_general x1, matrix products, volume_term(): jnp.einsum('dpq,vqe->dvpe', derivative, solution, precision=lax.Precision...  5.37 us
    mul x1, other arithmetic, surface_term(): 0.5 * normal * (values + outer_vals)  5.34 us
    another operation x2, local copies, waits for them, and re-layouts, receptor_rows(): jnp.tile(basis_z, (16, 1))  4.01 us
  transfers between devices with their start and end apart: 2, of which 0 were waited for; matrix products, arithmetic and copies ran while one was open for 14% of the time, Pallas kernels for 0%

profile of v3, /device:TPU:9, one launch (start us, length us, event | category | flops | bytes accessed | tf_op | source)
XLA Modules:
  0.0 126.6 jit_solution(15999877380082029738)
XLA Ops:
  0.6 0.8 reshape.135.idx_ref
  1.4 0.6 select_reduce_fusion
  2.0 0.0 copy-start.13
  2.0 1.9 %reshape.134 = f32[16,6,1024]{2,1,0:T(8,128)} reshape(f32[96,1024]{1,0:T(8,128)} %param.17) | data formatting | bytes 786432 | tf_op jit(solution)/shard_map/reshape | solution.py:90
  3.9 0.0 copy-done.10
  3.9 1.9 %copy.35 = f32[6,1024,16]{2,1,0:T(8,128)S(1)} copy(f32[6,1024,16]{1,0,2:T(8,128)} %bitcast.76) | data formatting | bytes 786432 | tf_op jit(solution)/shard_map/transpose | solution.py:90
  5.8 0.0 copy-start
  5.8 0.0 copy-done.13
  5.8 4.0 %convolution_bitcast_fusion = f32[6,1024,16,5]{1,2,3,0:T(8,128)S(1)} fusion(f32[16,6,64,1]{2,0,3,1:T(8,128)S(1)} %copy-done.13, f32[5,64,1024]{2,1,0:T(8,128)} %param.14), kind=kOutput, calls=%fused_computation.28 | convolution fusion | flops 377487360 | bytes 3301376 | tf_op jit(solution)/shard_map/qfp,vpe->feqv/dot_general | solution.py:88
  9.8 0.0 copy-start.3
  9.8 1.2 copy.36
  11.0 0.2 copy-done.3
  11.2 2.5 %copy.48 = f32[10,8,6,1024]{3,1,2,0:T(8,128)} copy(f32[10,8,6,1024]{3,2,1,0:T(8,128)S(1)} %bitcast.74) | data formatting | bytes 3932160
  13.7 3.4 %copy.38.values_ref = f32[6144,80]{1,0:T(8,128)} copy(f32[6144,80]{0,1:T(8,128)} %bitcast.75) | data formatting | bytes 3932160 | tf_op jit(solution)/shard_map/reshape;reshape | solution.py:241
  17.1 0.0 copy-done
  17.1 0.6 gather_fusion.1
  17.8 2.5 %gather_fusion = f32[128,80]{1,0:T(8,128)S(1)} fusion(f32[6144,80]{1,0:T(8,128)} %copy.38.values_ref, s32[1024]{0:T(1024)S(1)} %pad_clamp_fusion), kind=kCustom, calls=%fused_computation | custom fusion | bytes 82432 | tf_op jit(solution)/shard_map/jit(_take)/gather | solution.py:100
  20.3 0.1 broadcast_select_fusion
  20.4 0.1 broadcast_select_fusion.1
  20.5 0.7 fusion.34
  21.2 1.9 %collective-permute-start = (f32[64,96]{1,0:T(8,128)}, f32[64,96]{1,0:T(8,128)}, u32[]{:S(2)}, u32[]{:S(2)}) collective-permute-start(f32[64,96]{1,0:T(8,128)} %get-tuple-element.20), channel_id=1, source_target_pairs={{0,16},{16,32},{32,48},{48,64},{64,80},{80,96},{96,112},{112,0},{1... | collective-permute-start | bytes 73736 | tf_op jit(solution)/shard_map/ppermute | solution.py:21
  23.0 0.0 collective-permute-start.1
  23.0 0.0 copy-done.12
  23.1 0.8 multiply_multiply_fusion.11
  23.8 0.2 pad_maximum_fusion.1
  24.1 0.1 broadcast_in_dim.64
  24.2 1.0 tile.8
  25.2 0.1 pad_maximum_fusion.3
  25.3 1.7 %tile.19 = f32[16,4,8192]{2,1,0:T(4,128)} broadcast(f32[4,8192]{1,0:T(4,128)S(1)} %pad_maximum_fusion.3), dimensions={1,2} | broadcast | bytes 2228224 | tf_op jit(solution)/shard_map/tile | solution.py:208
  27.1 2.3 %tile.20 = f32[64,8192]{1,0:T(8,128)S(1)} reshape(f32[16,4,8192]{2,1,0:T(4,128)} %tile.19) | data formatting | bytes 4194304 | tf_op jit(solution)/shard_map/tile | solution.py:208
  29.3 0.0 copy-start.8
  29.3 1.1 fusion.30
  30.4 0.3 fusion.32
  30.7 0.8 fusion.37
  31.6 1.0 select_reduce_fusion.1
  32.5 0.6 add_bitcast_fusion
  33.2 5.4 %multiply_reduce_fusion = f32[64,5,1024]{2,0,1:T(8,128)} fusion(f32[3,64,64,1]{2,1,3,0:T(8,128)} %constant.144, f32[3,1024]{1,0:T(4,128)S(1)} %copy-done.15, f32[5,64,1024]{2,1,0:T(8,128)S(1)} %copy-done.5), kind=kOutput, calls=%fused_computation.6 | convolution fusion | flops 756613120 | bytes 2682880 | tf_op jit(solution)/shard_map/dpq,vqe->dvpe/dot_general | solution.py:182
  38.5 0.2 broadcast_multiply_fusion.1
  38.7 0.0 copy-start.7
  38.7 0.0 copy-start.9
  38.7 1.7 %bitcast_multiply_fusion.weights_ref = f32[64,8192]{1,0:T(8,128)} fusion(f32[64,8192]{1,0:T(8,128)S(1)} %tile.20, f32[4,16,8192]{2,1,0:T(8,128)S(1)} %broadcast_multiply_fusion.1), kind=kLoop, calls=%fused_computation.16 | loop fusion | flops 524288 | bytes 6291456 | tf_op jit(solution)/shard_map/mul | solution.py:206
  40.4 1.0 copy.44
  41.4 0.0 copy-done.9
  41.4 0.0 collective-permute-done
  41.5 0.0 collective-permute-done.1
  41.5 1.4 %pad_maximum_fusion.4.recv_ref = f32[128,96]{1,0:T(8,128)} fusion(f32[64,96]{1,0:T(8,128)} %collective-permute-done.1, f32[64,96]{1,0:T(8,128)} %collective-permute-done), kind=kLoop, calls=%fused_computation.55 | loop fusion | flops 12288 | bytes 98304 | tf_op jit(solution)/shard_map/concatenate | solution.py:244
  42.9 12.2 %shard_map.149 = f32[6144,96]{1,0:T(8,128)} custom-call(s32[6144]{0:T(1024)} %copy-done.10, f32[6144,80]{1,0:T(8,128)} %copy.38.values_ref, f32[6144,16]{1,0:T(8,128)} %bitcast.70, f32[128,96]{1,0:T(8,128)} %pad_maximum_fusion.4.recv_ref), custom_call_target="tpu_custom_call" | custom-call | bytes 7127040 | tf_op jit(solution)/shard_map/pallas_call | solution.py:134
  55.1 0.0 copy-done.1
  55.1 5.3 %broadcast_multiply_fusion = (f32[6144,16]{1,0:T(8,128)}, f32[6144,16]{1,0:T(8,128)}) fusion(f32[6144,96]{1,0:T(8,128)} %shard_map.149, f32[6,1024,16]{2,1,0:T(8,128)S(1)} %copy-done.1), kind=kLoop, calls=%fused_computation.29 | loop fusion | flops 491520 | bytes 1572864 | tf_op jit(solution)/shard_map/mul | solution.py:175
  60.5 3.0 %copy.39 = f32[6,1024,16]{1,2,0:T(8,128)} copy(f32[6,1024,16]{2,1,0:T(8,128)} %bitcast.73) | data formatting | bytes 786432 | tf_op jit(solution)/shard_map/mul | solution.py:175
  63.5 3.2 %copy.42 = f32[6,1024,16]{1,2,0:T(8,128)} copy(f32[6,1024,16]{2,1,0:T(8,128)} %bitcast.72) | data formatting | bytes 786432 | tf_op jit(solution)/shard_map/mul | solution.py:175
  66.6 2.1 %copy.40 = f32[6144,80]{0,1:T(8,128)} copy(f32[6144,80]{1,0:T(8,128)S(1)} %bitcast.71) | data formatting | bytes 3932160 | tf_op jit(solution)/shard_map/slice | solution.py:171
  68.7 3.4 %reshape.137 = f32[6,1024,16,5]{1,0,3,2:T(8,128)} reshape(f32[6144,80]{0,1:T(8,128)} %copy.40) | data formatting | bytes 3932160 | tf_op jit(solution)/shard_map/reshape | solution.py:171
  72.2 6.8 %multiply_add_fusion = (f32[5,64,1024]{2,1,0:T(8,128)S(1)}, f32[5,64,1024]{2,1,0:T(8,128)}) fusion(f32[5,64,1024]{2,1,0:T(8,128)S(1)} %copy-done.6, f32[64,16,6,1]{0,1,3,2:T(8,128)} %constant.146, f32[6,1024,16,5]{1,2,3,0:T(8,128)S(1)} %copy-done.4, f32[6,1024,16,5]{1,0,3,2:T(8,128)} %reshape.137, f32[6,1024,16]{1,2,0:T(8,128)} %copy.44, ...), kind=kOutput, calls=%fused_computation.37 | convolution fusion | flops 382238720 | bytes 10641408 | tf_op jit(solution)/shard_map/pqf,feqv->vpe/dot_general | solution.py:178
  79.0 0.2 reduce-precision_convert_fusion.1
  79.2 1.2 pad_maximum_fusion.rows_ref
  80.4 16.6 %shard_map.150 = f32[5,8192]{1,0:T(8,128)} custom-call(bf16[640,1024]{1,0:T(8,128)(2,1)} %pad_maximum_fusion.rows_ref, s32[1,8192]{1,0:T(1,128)} %bitcast.83, f32[64,8192]{1,0:T(8,128)} %bitcast_multiply_fusion.weights_ref), custom_call_target="tpu_custom_call" | custom-call | flops 10737418240 | bytes 3604480 | tf_op jit(solution)/shard_map/pallas_call | solution.py:213
  97.0 0.0 copy-done.16
  97.0 3.5 %reduce-precision_convert_fusion = (bf16[8192,80]{0,1:T(8,128)(2,1)S(1)}, bf16[8192,80]{0,1:T(8,128)(2,1)S(1)}) fusion(f32[5,8192]{1,0:T(8,128)} %shard_map.150, f32[5,80]{1,0:T(8,128)S(1)} %copy-done.16, s32[80]{0:T(128)S(1)} %and_select_fusion, s32[8192]{0:T(1024)S(1)} %bitcast.82), kind=kOutput, calls=%fused_computation.8 | convolution fusion | flops 43253760 | bytes 2819968 | tf_op jit(solution)/shard_map/dot_general | solution.py:256
  100.5 0.0 copy-done.14
  100.5 7.3 %fusion = f32[1024,160]{0,1:T(8,128)S(1)} fusion(s32[8192]{0:T(1024)S(1)} %copy-done.14, bf16[8192,80]{0,1:T(8,128)(2,1)S(1)} %get-tuple-element.5, bf16[8192,80]{0,1:T(8,128)(2,1)S(1)} %get-tuple-element.4), kind=kOutput, calls=%fused_computation.3 | convolution fusion | flops 2697986048 | bytes 3309568 | tf_op jit(solution)/shard_map/dot_general | solution.py:263
  107.8 0.1 reshape.141
  107.9 17.9 %all_to_all.5 = f32[16,5,1024]{2,1,0:T(8,128)S(1)} all-to-all(f32[16,5,1024]{2,1,0:T(8,128)S(1)} %bitcast.79), channel_id=1, replica_groups=mesh['valve'=8,'bulk'=16] {'bulk'}, dimensions={0} | all-to-all | bytes 655360 | tf_op jit(solution)/shard_map/all_to_all | solution.py:266
  125.8 0.8 copy.62
  (26 shorter events, 0.1 us)
Async XLA Ops:
  1.4 2.4 %copy-start.10 = (s32[6144]{0:T(1024)}, s32[6144]{0:T(1024)S(1)}, u32[]{:S(2)}) copy-start(s32[6144]{0:T(1024)S(1)} %reshape.135.idx_ref) | copy-start | bytes 73732
  2.0 3.8 %copy-start.13 = (f32[16,6,64,1]{2,0,3,1:T(8,128)S(1)}, f32[16,6,64,1]{2,0,3,1:T(8,128)}, u32[]{:S(2)}) copy-start(f32[16,6,64,1]{2,0,3,1:T(8,128)} %constant.145) | copy-start | bytes 73732
  5.8 11.3 %copy-start = (f32[6,1024,16]{2,1,0:T(8,128)}, f32[6,1024,16]{2,1,0:T(8,128)S(1)}, u32[]{:S(2)}) copy-start(f32[6,1024,16]{2,1,0:T(8,128)S(1)} %copy.35) | copy-start | bytes 1179652
  9.8 1.4 %copy-start.3 = (f32[6,1024,16,5]{1,2,3,0:T(8,128)}, f32[6,1024,16,5]{1,2,3,0:T(8,128)S(1)}, u32[]{:S(2)}) copy-start(f32[6,1024,16,5]{1,2,3,0:T(8,128)S(1)} %convolution_bitcast_fusion) | copy-start | bytes 5898244
  13.7 9.3 %copy-start.12 = (f32[3,8192]{1,0:T(4,128)S(1)}, f32[3,8192]{1,0:T(4,128)}, u32[]{:S(2)}) copy-start(f32[3,8192]{1,0:T(4,128)} %param.20) | copy-start | bytes 294916
  21.2 20.3 %collective-permute-start = (f32[64,96]{1,0:T(8,128)}, f32[64,96]{1,0:T(8,128)}, u32[]{:S(2)}, u32[]{:S(2)}) collective-permute-start(f32[64,96]{1,0:T(8,128)} %get-tuple-element.20), channel_id=1, source_target_pairs={{0,16},{16,32},{32,48},{48,64},{64,80},{80,96},{96,112},{112,0},{1... | collective-permute-start | bytes 73736 | tf_op jit(solution)/shard_map/ppermute | solution.py:21
  23.0 18.4 %collective-permute-start.1 = (f32[64,96]{1,0:T(8,128)}, f32[64,96]{1,0:T(8,128)}, u32[]{:S(2)}, u32[]{:S(2)}) collective-permute-start(f32[64,96]{1,0:T(8,128)} %get-tuple-element.21), channel_id=1, source_target_pairs={{16,0},{32,16},{48,32},{64,48},{80,64},{96,80},{112,96},{0,112},{1... | collective-permute-start | bytes 73736 | tf_op jit(solution)/shard_map/ppermute | solution.py:22
  27.1 6.1 %copy-start.5 = (f32[5,64,1024]{2,1,0:T(8,128)S(1)}, f32[5,64,1024]{2,1,0:T(8,128)}, u32[]{:S(2)}) copy-start(f32[5,64,1024]{2,1,0:T(8,128)} %param.14) | copy-start | bytes 3932164
  27.1 6.1 %copy-start.15 = (f32[3,1024]{1,0:T(4,128)S(1)}, f32[3,1024]{1,0:T(4,128)}, u32[]{:S(2)}) copy-start(f32[3,1024]{1,0:T(4,128)} %param.15) | copy-start | bytes 36868
  29.3 9.2 %copy-start.8 = (f32[16,8192]{1,0:T(8,128)S(1)}, f32[16,8192]{1,0:T(8,128)}, u32[]{:S(2)}) copy-start(f32[16,8192]{1,0:T(8,128)} %tile.8) | copy-start | bytes 1572868
  38.7 1.7 %copy-start.7 = (f32[16,6,1024]{2,1,0:T(8,128)S(1)}, f32[16,6,1024]{2,1,0:T(8,128)}, u32[]{:S(2)}) copy-start(f32[16,6,1024]{2,1,0:T(8,128)} %reshape.134) | copy-start | bytes 1179652
  38.7 2.7 %copy-start.9 = (f32[64,1024]{1,0:T(8,128)S(1)}, f32[64,1024]{1,0:T(8,128)}, u32[]{:S(2)}) copy-start(f32[64,1024]{1,0:T(8,128)} %param.16) | copy-start | bytes 786436
  42.9 12.3 %copy-start.1 = (f32[6,1024,16]{2,1,0:T(8,128)S(1)}, f32[6,1024,16]{2,1,0:T(8,128)}, u32[]{:S(2)}) copy-start(f32[6,1024,16]{2,1,0:T(8,128)} %copy-done) | copy-start | bytes 1179652
  63.5 3.2 %copy-start.2 = (f32[6144,96]{1,0:T(8,128)S(1)}, f32[6144,96]{1,0:T(8,128)}, u32[]{:S(2)}) copy-start(f32[6144,96]{1,0:T(8,128)} %shard_map.149) | copy-start | bytes 7077892
  68.7 3.4 %copy-start.4 = (f32[6,1024,16,5]{1,2,3,0:T(8,128)S(1)}, f32[6,1024,16,5]{1,2,3,0:T(8,128)}, u32[]{:S(2)}) copy-start(f32[6,1024,16,5]{1,2,3,0:T(8,128)} %copy-done.3) | copy-start | bytes 5898244
  68.7 3.4 %copy-start.6 = (f32[5,64,1024]{2,1,0:T(8,128)S(1)}, f32[5,64,1024]{2,1,0:T(8,128)}, u32[]{:S(2)}) copy-start(f32[5,64,1024]{2,1,0:T(8,128)} %param.14) | copy-start | bytes 3932164
  80.4 16.6 %copy-start.11 = (s32[8192,1]{0,1:T(1,128)S(1)}, s32[8192,1]{0,1:T(1,128)}, u32[]{:S(2)}) copy-start(s32[8192,1]{0,1:T(1,128)} %param.21) | copy-start | bytes 98308
  80.4 16.6 %copy-start.16 = (f32[5,80]{1,0:T(8,128)S(1)}, f32[5,80]{1,0:T(8,128)}, u32[]{:S(2)}) copy-start(f32[5,80]{1,0:T(8,128)} %constant.141.clone) | copy-start | bytes 4804
  96.9 3.5 %copy-start.14 = (s32[8192]{0:T(1024)S(1)}, s32[8192]{0:T(1024)}, u32[]{:S(2)}) copy-start(s32[8192]{0:T(1024)} %add_bitcast_fusion) | copy-start | bytes 98308

commit v4 on v3

--- a/solution.py
+++ b/solution.py
@@ -183,7 +183,14 @@
     return jnp.sum(velocity[:, None, None, :] * slopes, axis=0)
 
 
-def _interp_kernel(rows_ref, donors_ref, weights_ref, out_ref):
+def _pick_row(basis, first, index):
+    out = basis[first : first + 1]
+    for i in range(1, 4):
+        out = jnp.where(index == i, basis[first + i : first + i + 1], out)
+    return out
+
+
+def _interp_kernel(rows_ref, donors_ref, basis_ref, out_ref):
     elems = rows_ref.shape[1]
     tile = donors_ref.shape[1]
     half = rows_ref.shape[0] // 2
@@ -191,7 +198,15 @@
     picked = jnp.dot(rows_ref[...], onehot.astype(jnp.bfloat16), preferred_element_type=jnp.float32)
     picked = picked[:half] + picked[half:]
     nvars = out_ref.shape[0]
-    picked = picked.reshape(nvars, half // nvars, tile) * weights_ref[...][None]
+    points = half // nvars
+    basis = basis_ref[...]
+    point = lax.broadcasted_iota(jnp.int32, (points, tile), 0)
+    weights = (
+        _pick_row(basis, 0, point // 16)
+        * _pick_row(basis, 4, point // 4 % 4)
+        * _pick_row(basis, 8, point % 4)
+    )
+    picked = picked.reshape(nvars, points, tile) * weights[None]
     out_ref[...] = jnp.sum(picked, axis=1)
 
 
@@ -199,14 +214,7 @@
     nvars = advanced.shape[0]
     elems = advanced.shape[2]
     receptors = donors.shape[0]
-    basis_x = jnp.stack(lagrange_at(coords[0]))
-    basis_y = jnp.stack(lagrange_at(coords[1]))
-    basis_z = jnp.stack(lagrange_at(coords[2]))
-    weights = (
-        jnp.repeat(basis_x, 16, axis=0)
-        * jnp.tile(jnp.repeat(basis_y, 4, axis=0), (4, 1))
-        * jnp.tile(basis_z, (16, 1))
-    )
+    basis = jnp.concatenate([jnp.stack(lagrange_at(coords[d])) for d in range(3)], axis=0)
     hi, lo = split_bf16(advanced.reshape(nvars * 64, elems))
     rows = jnp.concatenate([hi, lo], axis=0)
     tile = 512
@@ -217,15 +225,15 @@
         in_specs=[
             pl.BlockSpec((2 * nvars * 64, elems), lambda i: (0, 0)),
             pl.BlockSpec((1, tile), lambda i: (0, i)),
-            pl.BlockSpec((64, tile), lambda i: (0, i)),
+            pl.BlockSpec((12, tile), lambda i: (0, i)),
         ],
         out_specs=pl.BlockSpec((nvars, tile), lambda i: (0, i)),
         cost_estimate=pl.CostEstimate(
             flops=2 * 2 * nvars * 64 * elems * receptors,
             transcendentals=0,
-            bytes_accessed=2 * nvars * 64 * elems * 2 + receptors * (1 + 64 + nvars) * 4,
+            bytes_accessed=2 * nvars * 64 * elems * 2 + receptors * (1 + 12 + nvars) * 4,
         ),
-    )(rows, donors.reshape(1, receptors), weights)
+    )(rows, donors.reshape(1, receptors), basis)
 
 
 def on_device(

time: 129 us -> 119 us (0.922)
  other arithmetic: 14.2 us -> 9.82 us
  local copies, waits for them, and re-layouts: 34 us -> 30.9 us
  matrix products: 28.9 us -> 27 us
    another operation x3 -> x0, local copies, waits for them, and re-layouts: 5.01 us -> none  [the longest x2 4.01 us: receptor_rows(): jnp.tile(basis_z, (16, 1))]
    concatenate x0 -> x1, local copies, waits for them, and re-layouts: none -> 1.95 us  [receptor_rows(): jnp.concatenate([jnp.stack(lagrange_at(coords[d])) for d in range(3)], ax...]
    mul x2 -> x0, other arithmetic: 1.87 us -> none  [receptor_rows(): jnp.repeat(basis_x, 16, axis=0)]
    unnamed x36 -> x40, local copies, waits for them, and re-layouts: 3.57 us -> 3.49 us
  transfers between devices with their start and end apart: 2 -> 2, of which waited for: 0 -> 0; matrix products, arithmetic and copies ran while one was open for 14% -> 9% of each run, Pallas kernels for 0% -> 0%
where the time goes in v4:
time: 119 us; the launch traced here: 117 us
  local copies, waits for them, and re-layouts  30.9 us (26%)
  Pallas kernels  28.2 us (24%)
  matrix products  27 us (23%)
  blocking collectives  17.9 us (15%)
  other arithmetic  9.82 us (8%)
  starting transfers between devices  1.87 us (2%)
    all_to_all x1, blocking collectives, on_device(): got = lax.all_to_all(send, 'bulk', 0, 0, tiled=True)  17.9 us
    pallas_call x1, Pallas kernels, receptor_rows(): pl.pallas_call(_interp_kernel, out_shape=jax.ShapeDtypeStruct((nvars, rec...  16 us
    pallas_call x1, Pallas kernels, take_rows(): pl.pallas_call(_rows_kernel, out_shape=jax.ShapeDtypeStruct((idx.shape[0]...  12.2 us
    dot_general x1, matrix products, on_device(): jnp.dot(by_rank, jnp.concatenate([hi, lo], axis=1), preferred_element_typ...  7.28 us
    dot_general x1, matrix products, surface_term(): jnp.einsum('pqf,feqv->vpe', lift_faces, jump_term, precision=lax.Precisio...  6.84 us
    mul x1, other arithmetic, surface_term(): 0.5 * normal * (values + outer_vals)  5.37 us
    dot_general x1, matrix products, volume_term(): jnp.einsum('dpq,vqe->dvpe', derivative, solution, precision=lax.Precision...  4.36 us
    dot_general x1, matrix products, face_rows(): jnp.einsum('qfp,vpe->feqv', ext_faces, solution, precision=lax.Precision....  3.99 us
  transfers between devices with their start and end apart: 2, of which 0 were waited for; matrix products, arithmetic and copies ran while one was open for 9% of the time, Pallas kernels for 0%

profile of v4, /device:TPU:9, one launch (start us, length us, event | category | flops | bytes accessed | tf_op | source)
XLA Modules:
  0.0 116.7 jit_solution(1682708318385056707)
XLA Ops:
  0.6 0.8 reshape.125.idx_ref
  1.4 0.6 select_reduce_fusion
  2.0 1.8 %reshape.124 = f32[16,6,1024]{2,1,0:T(8,128)} reshape(f32[96,1024]{1,0:T(8,128)} %param.17) | data formatting | bytes 786432 | tf_op jit(solution)/shard_map/reshape | solution.py:90
  3.8 1.9 %copy.35 = f32[6,1024,16]{2,1,0:T(8,128)S(1)} copy(f32[6,1024,16]{1,0,2:T(8,128)} %bitcast.74) | data formatting | bytes 786432 | tf_op jit(solution)/shard_map/transpose | solution.py:90
  5.8 0.0 copy-done.9
  5.8 0.0 copy-start
  5.8 0.0 copy-done.14
  5.8 4.0 %convolution_bitcast_fusion = f32[6,1024,16,5]{1,2,3,0:T(8,128)S(1)} fusion(f32[16,6,64,1]{2,0,3,1:T(8,128)S(1)} %copy-done.14, f32[5,64,1024]{2,1,0:T(8,128)} %param.14), kind=kOutput, calls=%fused_computation.27 | convolution fusion | flops 377487360 | bytes 3301376 | tf_op jit(solution)/shard_map/qfp,vpe->feqv/dot_general | solution.py:88
  9.8 0.0 copy-start.3
  9.8 1.2 %copy.36 = f32[6,1024,16,5]{1,0,3,2:T(8,128)S(1)} copy(f32[6,1024,16,5]{1,2,3,0:T(8,128)S(1)} %convolution_bitcast_fusion) | data formatting | bytes 3932160 | tf_op jit(solution)/shard_map/qfp,vpe->feqv/transpose | solution.py:88
  11.0 0.1 copy-done.3
  11.1 2.5 %copy.48 = f32[10,8,6,1024]{3,1,2,0:T(8,128)} copy(f32[10,8,6,1024]{3,2,1,0:T(8,128)S(1)} %bitcast.72) | data formatting | bytes 3932160
  13.6 3.4 %copy.38.values_ref = f32[6144,80]{1,0:T(8,128)} copy(f32[6144,80]{0,1:T(8,128)} %bitcast.73) | data formatting | bytes 3932160 | tf_op jit(solution)/shard_map/reshape;reshape | solution.py:249
  17.1 0.0 copy-done
  17.1 0.6 gather_fusion.1
  17.8 2.6 %gather_fusion = f32[128,80]{1,0:T(8,128)S(1)} fusion(f32[6144,80]{1,0:T(8,128)} %copy.38.values_ref, s32[1024]{0:T(1024)S(1)} %pad_clamp_fusion), kind=kCustom, calls=%fused_computation | custom fusion | bytes 82432 | tf_op jit(solution)/shard_map/jit(_take)/gather | solution.py:100
  20.4 0.1 broadcast_select_fusion
  20.5 0.1 broadcast_select_fusion.1
  20.6 0.1 fusion.34
  20.7 1.9 %collective-permute-start = (f32[64,96]{1,0:T(8,128)S(1)}, f32[64,96]{1,0:T(8,128)S(1)}, u32[]{:S(2)}, u32[]{:S(2)}) collective-permute-start(f32[64,96]{1,0:T(8,128)S(1)} %get-tuple-element.20), channel_id=1, source_target_pairs={{0,16},{16,32},{32,48},{48,64},{64,80},{80,96},{96,112},{112,0},{1... | collective-permute-start | bytes 73736 | tf_op jit(solution)/shard_map/ppermute | solution.py:21
  22.5 0.0 collective-permute-start.1
  22.5 0.0 copy-done.13
  22.5 0.8 multiply_multiply_fusion
  23.3 0.0 copy-done.10
  23.3 0.0 copy-done.15
  23.3 0.2 fusion.30
  23.5 0.0 copy-start.7
  23.6 0.3 fusion.32
  23.9 0.8 fusion.37
  24.7 0.2 select_reduce_fusion.1
  25.0 0.0 copy-start.8
  25.0 0.6 add_bitcast_fusion
  25.6 0.0 copy-done.12
  25.6 0.0 copy-done.17
  25.6 0.0 copy-done.5
  25.6 4.4 %multiply_reduce_fusion = f32[64,5,1024]{2,0,1:T(8,128)} fusion(f32[3,64,64,1]{2,1,3,0:T(8,128)S(1)} %copy-done.12, f32[3,1024]{1,0:T(4,128)S(1)} %copy-done.17, f32[5,64,1024]{2,1,0:T(8,128)S(1)} %copy-done.5), kind=kOutput, calls=%fused_computation.6 | convolution fusion | flops 756613120 | bytes 2682880 | tf_op jit(solution)/shard_map/dpq,vqe->dvpe/dot_general | solution.py:182
  30.0 0.0 copy-done.7
  30.0 1.0 copy.44
  30.9 0.0 copy-done.8
  31.0 2.0 %concatenate.18.basis_ref = f32[12,8192]{1,0:T(8,128)} concatenate(f32[1,8192]{1,0:T(1,128)S(1)} %get-tuple-element.17, f32[1,8192]{1,0:T(1,128)S(1)} %get-tuple-element.9, f32[1,8192]{1,0:T(1,128)S(1)} %get-tuple-element.10, f32[1,8192]{1,0:T(1,128)S(1)} %get-tuple-element.11, f32[1,8192]{1,0:T(1,128)S(1)} %get-tuple-element.19, f32[1,8192]{1,0:T(1,128)S(1)} %get-tuple-element.12, ...), dimensions={0} | concatenate | bytes 786432 | tf_op jit(solution)/shard_map/concatenate | solution.py:217
  32.9 0.0 collective-permute-done
  32.9 0.0 collective-permute-done.1
  32.9 0.6 pad_maximum_fusion.1.recv_ref
  33.6 12.2 %shard_map.149 = f32[6144,96]{1,0:T(8,128)} custom-call(s32[6144]{0:T(1024)} %copy-done.9, f32[6144,80]{1,0:T(8,128)} %copy.38.values_ref, f32[6144,16]{1,0:T(8,128)} %bitcast.68, f32[128,96]{1,0:T(8,128)} %pad_maximum_fusion.1.recv_ref), custom_call_target="tpu_custom_call" | custom-call | bytes 7127040 | tf_op jit(solution)/shard_map/pallas_call | solution.py:134
  45.8 0.0 copy-done.1
  45.8 5.4 %broadcast_multiply_fusion = (f32[6144,16]{1,0:T(8,128)}, f32[6144,16]{1,0:T(8,128)}) fusion(f32[6144,96]{1,0:T(8,128)} %shard_map.149, f32[6,1024,16]{2,1,0:T(8,128)S(1)} %copy-done.1), kind=kLoop, calls=%fused_computation.28 | loop fusion | flops 491520 | bytes 1572864 | tf_op jit(solution)/shard_map/mul | solution.py:175
  51.1 3.0 %copy.39 = f32[6,1024,16]{1,2,0:T(8,128)} copy(f32[6,1024,16]{2,1,0:T(8,128)} %bitcast.71) | data formatting | bytes 786432 | tf_op jit(solution)/shard_map/mul | solution.py:175
  54.1 3.1 %copy.42 = f32[6,1024,16]{1,2,0:T(8,128)} copy(f32[6,1024,16]{2,1,0:T(8,128)} %bitcast.70) | data formatting | bytes 786432 | tf_op jit(solution)/shard_map/mul | solution.py:175
  57.3 0.0 copy-done.2
  57.3 2.1 %copy.40 = f32[6144,80]{0,1:T(8,128)} copy(f32[6144,80]{1,0:T(8,128)S(1)} %bitcast.69) | data formatting | bytes 3932160 | tf_op jit(solution)/shard_map/slice | solution.py:171
  59.4 3.4 %reshape.127 = f32[6,1024,16,5]{1,0,3,2:T(8,128)} reshape(f32[6144,80]{0,1:T(8,128)} %copy.40) | data formatting | bytes 3932160 | tf_op jit(solution)/shard_map/reshape | solution.py:171
  62.8 0.0 copy-done.4
  62.8 0.0 copy-done.6
  62.8 6.8 %multiply_add_fusion = (f32[5,64,1024]{2,1,0:T(8,128)S(1)}, f32[5,64,1024]{2,1,0:T(8,128)}) fusion(f32[5,64,1024]{2,1,0:T(8,128)S(1)} %copy-done.6, f32[64,16,6,1]{0,1,3,2:T(8,128)} %constant.146, f32[6,1024,16,5]{1,2,3,0:T(8,128)S(1)} %copy-done.4, f32[6,1024,16,5]{1,0,3,2:T(8,128)} %reshape.127, f32[6,1024,16]{1,2,0:T(8,128)} %copy.44, ...), kind=kOutput, calls=%fused_computation.36 | convolution fusion | flops 382238720 | bytes 10641408 | tf_op jit(solution)/shard_map/pqf,feqv->vpe/dot_general | solution.py:178
  69.7 0.2 reduce-precision_convert_fusion.1
  69.9 1.2 %pad_maximum_fusion.rows_ref = bf16[640,1024]{1,0:T(8,128)(2,1)} fusion(bf16[320,1024]{1,0:T(8,128)(2,1)S(1)} %get-tuple-element.7, bf16[320,1024]{1,0:T(8,128)(2,1)S(1)} %get-tuple-element.6), kind=kLoop, calls=%fused_computation.33 | loop fusion | flops 2621440 | bytes 2621440 | tf_op jit(solution)/shard_map/concatenate | solution.py:219
  71.0 16.0 %shard_map.150 = f32[5,8192]{1,0:T(8,128)} custom-call(bf16[640,1024]{1,0:T(8,128)(2,1)} %pad_maximum_fusion.rows_ref, s32[1,8192]{1,0:T(1,128)} %bitcast.81, f32[12,8192]{1,0:T(8,128)} %concatenate.18.basis_ref), custom_call_target="tpu_custom_call" | custom-call | flops 10737418240 | bytes 1900544 | tf_op jit(solution)/shard_map/pallas_call | solution.py:221
  87.0 0.0 copy-done.11
  87.0 0.0 copy-done.18
  87.0 3.5 %reduce-precision_convert_fusion = (bf16[8192,80]{0,1:T(8,128)(2,1)S(1)}, bf16[8192,80]{0,1:T(8,128)(2,1)S(1)}) fusion(f32[5,8192]{1,0:T(8,128)} %shard_map.150, f32[5,80]{1,0:T(8,128)S(1)} %copy-done.18, s32[80]{0:T(128)S(1)} %and_select_fusion, s32[8192]{0:T(1024)S(1)} %bitcast.80), kind=kOutput, calls=%fused_computation.8 | convolution fusion | flops 43253760 | bytes 2819968 | tf_op jit(solution)/shard_map/dot_general | solution.py:264
  90.5 7.3 %fusion = f32[1024,160]{0,1:T(8,128)S(1)} fusion(s32[8192]{0:T(1024)S(1)} %copy-done.16, bf16[8192,80]{0,1:T(8,128)(2,1)S(1)} %get-tuple-element.5, bf16[8192,80]{0,1:T(8,128)(2,1)S(1)} %get-tuple-element.4), kind=kOutput, calls=%fused_computation.3 | convolution fusion | flops 2697986048 | bytes 3309568 | tf_op jit(solution)/shard_map/dot_general | solution.py:271
  97.9 0.1 reshape.131
  97.9 17.9 %all_to_all.5 = f32[16,5,1024]{2,1,0:T(8,128)S(1)} all-to-all(f32[16,5,1024]{2,1,0:T(8,128)S(1)} %bitcast.77), channel_id=1, replica_groups=mesh['valve'=8,'bulk'=16] {'bulk'}, dimensions={0} | all-to-all | bytes 655360 | tf_op jit(solution)/shard_map/all_to_all | solution.py:274
  115.9 0.8 copy.62
  (23 shorter events, 0.1 us)
Async XLA Ops:
  1.4 4.4 %copy-start.9 = (s32[6144]{0:T(1024)}, s32[6144]{0:T(1024)S(1)}, u32[]{:S(2)}) copy-start(s32[6144]{0:T(1024)S(1)} %reshape.125.idx_ref) | copy-start | bytes 73732
  3.8 2.0 %copy-start.14 = (f32[16,6,64,1]{2,0,3,1:T(8,128)S(1)}, f32[16,6,64,1]{2,0,3,1:T(8,128)}, u32[]{:S(2)}) copy-start(f32[16,6,64,1]{2,0,3,1:T(8,128)} %constant.145) | copy-start | bytes 73732
  5.8 11.3 %copy-start = (f32[6,1024,16]{2,1,0:T(8,128)}, f32[6,1024,16]{2,1,0:T(8,128)S(1)}, u32[]{:S(2)}) copy-start(f32[6,1024,16]{2,1,0:T(8,128)S(1)} %copy.35) | copy-start | bytes 1179652
  9.8 1.3 %copy-start.3 = (f32[6,1024,16,5]{1,2,3,0:T(8,128)}, f32[6,1024,16,5]{1,2,3,0:T(8,128)S(1)}, u32[]{:S(2)}) copy-start(f32[6,1024,16,5]{1,2,3,0:T(8,128)S(1)} %convolution_bitcast_fusion) | copy-start | bytes 5898244
  13.6 8.9 %copy-start.13 = (f32[3,8192]{1,0:T(4,128)S(1)}, f32[3,8192]{1,0:T(4,128)}, u32[]{:S(2)}) copy-start(f32[3,8192]{1,0:T(4,128)} %param.20) | copy-start | bytes 294916
  17.1 6.2 %copy-start.10 = (s32[8192,1]{0,1:T(1,128)S(1)}, s32[8192,1]{0,1:T(1,128)}, u32[]{:S(2)}) copy-start(s32[8192,1]{0,1:T(1,128)} %param.21) | copy-start | bytes 98308
  17.1 6.2 %copy-start.15 = (bf16[128,128,1]{1,0,2:T(8,128)(2,1)S(1)}, bf16[128,128,1]{1,0,2:T(8,128)(2,1)}, u32[]{:S(2)}) copy-start(bf16[128,128,1]{1,0,2:T(8,128)(2,1)} %constant.147) | copy-start | bytes 98308
  17.1 8.5 %copy-start.12 = (f32[3,64,64,1]{2,1,3,0:T(8,128)S(1)}, f32[3,64,64,1]{2,1,3,0:T(8,128)}, u32[]{:S(2)}) copy-start(f32[3,64,64,1]{2,1,3,0:T(8,128)} %constant.144) | copy-start | bytes 147460
  17.1 8.5 %copy-start.17 = (f32[3,1024]{1,0:T(4,128)S(1)}, f32[3,1024]{1,0:T(4,128)}, u32[]{:S(2)}) copy-start(f32[3,1024]{1,0:T(4,128)} %param.15) | copy-start | bytes 36868
  17.8 7.8 %copy-start.5 = (f32[5,64,1024]{2,1,0:T(8,128)S(1)}, f32[5,64,1024]{2,1,0:T(8,128)}, u32[]{:S(2)}) copy-start(f32[5,64,1024]{2,1,0:T(8,128)} %param.14) | copy-start | bytes 3932164
  20.7 12.2 %collective-permute-start = (f32[64,96]{1,0:T(8,128)S(1)}, f32[64,96]{1,0:T(8,128)S(1)}, u32[]{:S(2)}, u32[]{:S(2)}) collective-permute-start(f32[64,96]{1,0:T(8,128)S(1)} %get-tuple-element.20), channel_id=1, source_target_pairs={{0,16},{16,32},{32,48},{48,64},{64,80},{80,96},{96,112},{112,0},{1... | collective-permute-start | bytes 73736 | tf_op jit(solution)/shard_map/ppermute | solution.py:21
  22.5 10.4 %collective-permute-start.1 = (f32[64,96]{1,0:T(8,128)S(1)}, f32[64,96]{1,0:T(8,128)S(1)}, u32[]{:S(2)}, u32[]{:S(2)}) collective-permute-start(f32[64,96]{1,0:T(8,128)S(1)} %get-tuple-element.21), channel_id=1, source_target_pairs={{16,0},{32,16},{48,32},{64,48},{80,64},{96,80},{112,96},{0,112},{1... | collective-permute-start | bytes 73736 | tf_op jit(solution)/shard_map/ppermute | solution.py:22
  23.5 6.4 %copy-start.7 = (f32[16,6,1024]{2,1,0:T(8,128)S(1)}, f32[16,6,1024]{2,1,0:T(8,128)}, u32[]{:S(2)}) copy-start(f32[16,6,1024]{2,1,0:T(8,128)} %reshape.124) | copy-start | bytes 1179652
  25.0 6.0 %copy-start.8 = (f32[64,1024]{1,0:T(8,128)S(1)}, f32[64,1024]{1,0:T(8,128)}, u32[]{:S(2)}) copy-start(f32[64,1024]{1,0:T(8,128)} %param.16) | copy-start | bytes 786436
  33.5 12.2 %copy-start.1 = (f32[6,1024,16]{2,1,0:T(8,128)S(1)}, f32[6,1024,16]{2,1,0:T(8,128)}, u32[]{:S(2)}) copy-start(f32[6,1024,16]{2,1,0:T(8,128)} %copy-done) | copy-start | bytes 1179652
  54.1 3.1 %copy-start.2 = (f32[6144,96]{1,0:T(8,128)S(1)}, f32[6144,96]{1,0:T(8,128)}, u32[]{:S(2)}) copy-start(f32[6144,96]{1,0:T(8,128)} %shard_map.149) | copy-start | bytes 7077892
  59.4 3.5 %copy-start.4 = (f32[6,1024,16,5]{1,2,3,0:T(8,128)S(1)}, f32[6,1024,16,5]{1,2,3,0:T(8,128)}, u32[]{:S(2)}) copy-start(f32[6,1024,16,5]{1,2,3,0:T(8,128)} %copy-done.3) | copy-start | bytes 5898244
  59.4 3.5 %copy-start.6 = (f32[5,64,1024]{2,1,0:T(8,128)S(1)}, f32[5,64,1024]{2,1,0:T(8,128)}, u32[]{:S(2)}) copy-start(f32[5,64,1024]{2,1,0:T(8,128)} %param.14) | copy-start | bytes 3932164
  71.0 16.0 %copy-start.11 = (s32[8192,1]{0,1:T(1,128)S(1)}, s32[8192,1]{0,1:T(1,128)}, u32[]{:S(2)}) copy-start(s32[8192,1]{0,1:T(1,128)} %param.21) | copy-start | bytes 98308
  71.0 16.0 %copy-start.18 = (f32[5,80]{1,0:T(8,128)S(1)}, f32[5,80]{1,0:T(8,128)}, u32[]{:S(2)}) copy-start(f32[5,80]{1,0:T(8,128)} %constant.141.clone) | copy-start | bytes 4804
  87.0 3.5 %copy-start.16 = (s32[8192]{0:T(1024)S(1)}, s32[8192]{0:T(1024)}, u32[]{:S(2)}) copy-start(s32[8192]{0:T(1024)} %add_bitcast_fusion) | copy-start | bytes 98308

commit v5 on v4

--- a/solution.py
+++ b/solution.py
@@ -112,7 +112,17 @@
     return both[: rows.shape[0]] + both[rows.shape[0] :]
 
 
-def _rows_kernel(idx_ref, values_ref, speeds_ref, recv_ref, out_ref, table_ref):
+def _exact_spread(x, spread):
+    hi = x.astype(jnp.bfloat16)
+    rest = x - hi.astype(jnp.float32)
+    mid = rest.astype(jnp.bfloat16)
+    lo = (rest - mid.astype(jnp.float32)).astype(jnp.bfloat16)
+    out = jnp.dot(hi, spread, preferred_element_type=jnp.float32)
+    out = out + jnp.dot(mid, spread, preferred_element_type=jnp.float32)
+    return out + jnp.dot(lo, spread, preferred_element_type=jnp.float32)
+
+
+def _jump_kernel(idx_ref, values_ref, speeds_ref, recv_ref, spread_ref, jump_ref, table_ref, outer_ref):
     own_rows, width = values_ref.shape
     table_ref[pl.ds(0, own_rows), pl.ds(0, width)] = values_ref[...]
     table_ref[pl.ds(0, own_rows), pl.ds(width, speeds_ref.shape[1])] = speeds_ref[...]
@@ -122,30 +132,53 @@
         base = pl.multiple_of(i * 16, 16)
         for j in range(16):
             row = idx_ref[base + j]
-            out_ref[pl.ds(base + j, 1), :] = table_ref[pl.ds(row, 1), :]
+            outer_ref[pl.ds(base + j, 1), :] = table_ref[pl.ds(row, 1), :]
         return carry
 
-    lax.fori_loop(0, out_ref.shape[0] // 16, body, 0)
-
-
-def take_rows(values, speeds, received, idx):
+    lax.fori_loop(0, own_rows // 16, body, 0)
+    chunk = 512
+    spread = spread_ref[...]
+
+    def rows(c, carry):
+        start = pl.multiple_of(c * chunk, chunk)
+        own = table_ref[pl.ds(start, chunk), :]
+        other = outer_ref[pl.ds(start, chunk), :]
+        own_speed = _exact_spread(own, spread)
+        outer_speed = _exact_spread(other, spread)
+        own_vals = own[:, :width]
+        outer_vals = other[:, :width]
+        normal = 0.5 * (own_speed - outer_speed)
+        common = 0.5 * normal * (own_vals + outer_vals) + 0.5 * jnp.abs(normal) * (own_vals - outer_vals)
+        jump_ref[pl.ds(start, chunk), :] = common - own_speed * own_vals
+        return carry
+
+    lax.fori_loop(0, own_rows // chunk, rows, 0)
+
+
+def jump_rows(values, speeds, received, idx):
     rows = values.shape[0] + received.shape[0]
-    width = received.shape[1]
+    full = received.shape[1]
+    width = values.shape[1]
+    nvars = width // speeds.shape[1]
+    spread = np.zeros((full, width))
+    for c in range(width):
+        spread[width + c // nvars, c] = 1.0
     return pl.pallas_call(
-        _rows_kernel,
+        _jump_kernel,
         out_shape=jax.ShapeDtypeStruct((idx.shape[0], width), values.dtype),
-        in_specs=[
-            pl.BlockSpec(memory_space=pltpu.SMEM),
-            pl.BlockSpec(memory_space=pltpu.VMEM),
-            pl.BlockSpec(memory_space=pltpu.VMEM),
-            pl.BlockSpec(memory_space=pltpu.VMEM),
+        in_specs=[pl.BlockSpec(memory_space=pltpu.SMEM)]
+        + [pl.BlockSpec(memory_space=pltpu.VMEM)] * 4,
+        out_specs=pl.BlockSpec(memory_space=pltpu.VMEM),
+        scratch_shapes=[
+            pltpu.VMEM((rows, full), values.dtype),
+            pltpu.VMEM((idx.shape[0], full), values.dtype),
         ],
-        out_specs=pl.BlockSpec(memory_space=pltpu.VMEM),
-        scratch_shapes=[pltpu.VMEM((rows, width), values.dtype)],
         cost_estimate=pl.CostEstimate(
-            flops=0, transcendentals=0, bytes_accessed=(2 * idx.shape[0] + rows) * width * 4
+            flops=12 * idx.shape[0] * full * width,
+            transcendentals=0,
+            bytes_accessed=(3 * idx.shape[0] + rows) * full * 4,
         ),
-    )(idx, values, speeds, received)
+    )(idx, values, speeds, received, jnp.asarray(spread, jnp.bfloat16))
 
 
 def owner_ranks(owners, buckets):
@@ -165,15 +198,9 @@
     return picked.astype(jnp.int32) - 1
 
 
-def surface_term(values, speeds, table_own, links, received, lifting, elems):
-    nvars = values.shape[2]
-    outer = take_rows(table_own, speeds, received, links)
-    outer_vals = outer[:, : 16 * nvars].reshape(6 * elems, 16, nvars)
-    outer_speed = outer[:, 16 * nvars :][:, :, None]
-    own_speed = speeds[:, :, None]
-    normal = 0.5 * (own_speed - outer_speed)
-    common = 0.5 * normal * (values + outer_vals) + 0.5 * jnp.abs(normal) * (values - outer_vals)
-    jump_term = (common - own_speed * values).reshape(6, elems, 16, nvars)
+def surface_term(values, speeds, links, received, lifting, elems):
+    nvars = received.shape[1] // 16 - 1
+    jump_term = jump_rows(values, speeds, received, links).reshape(6, elems, 16, nvars)
     lift_faces = lifting.reshape(64, 16, 6)
     return jnp.einsum("pqf,feqv->vpe", lift_faces, jump_term, precision=lax.Precision.HIGHEST)
 
@@ -250,7 +277,7 @@
     outgoing = rim_rows(flat_values, speeds, links, faces_total, rim_count)
     extended = padded(outgoing, (("valve", 0),), rim_count)
     received = jnp.concatenate([extended[:rim_count], extended[3 * rim_count :]], axis=0)
-    surface = surface_term(values, speeds, flat_values, links, received, lifting, elems)
+    surface = surface_term(flat_values, speeds, links, received, lifting, elems)
     volume = volume_term(solution, velocity, derivative)
     section_rate = -inv_jacobian[None] * (volume + surface)
     advanced = solution + section_step * section_rate

time: 119 us -> 107 us (0.90); the launches traced: 117 us -> 107 us
  local copies, waits for them, and re-layouts: 30.9 us -> 21.9 us
  other arithmetic: 9.82 us -> 4.47 us
  Pallas kernels: 28.2 us -> 32.9 us
  matrix products: 27 us -> 24.7 us
  blocking collectives: 17.9 us -> 19.9 us
    mul x2 -> x0, local copies, waits for them, and re-layouts: 6.13 us -> none  [the longest x1 3.14 us: surface_term(): 0.5 * jnp.abs(normal) * (values - outer_vals)]
    mul x1 -> x0, other arithmetic: 5.37 us -> none  [surface_term(): 0.5 * normal * (values + outer_vals)]
    pallas_call x1, Pallas kernels: 12.2 us -> 16.7 us  [jump_rows(): pl.pallas_call(_jump_kernel, out_shape=jax.ShapeDtypeStruct((idx.shape[0]...]
    pallas_call x0 -> x1, local copies, waits for them, and re-layouts: none -> 2.35 us  [jump_rows(): pl.pallas_call(_jump_kernel, out_shape=jax.ShapeDtypeStruct((idx.shape[0]...]
    slice x1 -> x0, local copies, waits for them, and re-layouts: 2.1 us -> none  [surface_term(): outer_vals = outer[:, :16 * nvars].reshape(6 * elems, 16, nvars)]
    gather x1, local copies, waits for them, and re-layouts: 2.64 us -> 0.65 us  [rim_rows(): jnp.take(values, senders, axis=0)]
    gather x1, local copies, waits for them, and re-layouts: 0.65 us -> 2.64 us  [rim_rows(): jnp.take(speeds, senders, axis=0)]
    all_to_all x1, blocking collectives: 17.9 us -> 19.9 us  [on_device(): got = lax.all_to_all(send, 'bulk', 0, 0, tiled=True)]
  transfers between devices with their start and end apart: 2 -> 2, of which waited for: 0 -> 0; matrix products, arithmetic and copies ran while one was open for 9% -> 8% of each run, Pallas kernels for 0% -> 0%
where the time goes in v5:
time: 107 us
  Pallas kernels  32.9 us (31%)
  matrix products  24.7 us (23%)
  local copies, waits for them, and re-layouts  21.9 us (20%)
  blocking collectives  19.9 us (19%)
  other arithmetic  4.47 us (4%)
  starting transfers between devices  1.89 us (2%)
    all_to_all x1, blocking collectives, on_device(): got = lax.all_to_all(send, 'bulk', 0, 0, tiled=True)  19.9 us
    pallas_call x1, Pallas kernels, jump_rows(): pl.pallas_call(_jump_kernel, out_shape=jax.ShapeDtypeStruct((idx.shape[0]...  16.7 us
    pallas_call x1, Pallas kernels, receptor_rows(): pl.pallas_call(_interp_kernel, out_shape=jax.ShapeDtypeStruct((nvars, rec...  16.2 us
    dot_general x1, matrix products, on_device(): jnp.dot(by_rank, jnp.concatenate([hi, lo], axis=1), preferred_element_typ...  7.27 us
    dot_general x1, matrix products, surface_term(): jnp.einsum('pqf,feqv->vpe', lift_faces, jump_term, precision=lax.Precisio...  6.18 us
    dot_general x1, matrix products, volume_term(): jnp.einsum('dpq,vqe->dvpe', derivative, solution, precision=lax.Precision...  4.37 us
    dot_general x1, matrix products, on_device(): lax.dot_general(receptor_vals, copies, (((0,), (0,)), ((), ())), precisio...  3.52 us
    unnamed x30, local copies, waits for them, and re-layouts  3.38 us
  transfers between devices with their start and end apart: 2, of which 0 were waited for; matrix products, arithmetic and copies ran while one was open for 8% of the time, Pallas kernels for 0%

profile of v5, /device:TPU:9, one launch (start us, length us, event | category | flops | bytes accessed | tf_op | source)
XLA Modules:
  0.0 106.7 jit_solution(7740050518176722877)
XLA Ops:
  0.6 0.8 reshape.108.idx_ref
  1.4 0.0 copy-start.4
  1.4 0.6 select_reduce_fusion
  2.0 3.0 %convolution_bitcast_fusion = f32[6,1024,16,5]{1,2,3,0:T(8,128)S(1)} fusion(f32[16,6,64,1]{2,0,3,1:T(8,128)} %constant.144, f32[5,64,1024]{2,1,0:T(8,128)} %param.15), kind=kOutput, calls=%fused_computation.18 | convolution fusion | flops 377487360 | bytes 3301376 | tf_op jit(solution)/shard_map/qfp,vpe->feqv/dot_general | solution.py:88
  5.0 1.2 %copy.26 = f32[6,1024,16,5]{1,0,3,2:T(8,128)S(1)} copy(f32[6,1024,16,5]{1,2,3,0:T(8,128)S(1)} %convolution_bitcast_fusion) | data formatting | bytes 3932160 | tf_op jit(solution)/shard_map/qfp,vpe->feqv/transpose | solution.py:88
  6.2 0.0 copy-done.4
  6.2 2.5 %copy.35 = f32[10,8,6,1024]{3,1,2,0:T(8,128)} copy(f32[10,8,6,1024]{3,2,1,0:T(8,128)S(1)} %bitcast.63) | data formatting | bytes 3932160
  8.8 0.0 copy-start.2
  8.8 2.2 %copy.29.values_ref = f32[6144,80]{1,0:T(8,128)S(1)} copy(f32[6144,80]{0,1:T(8,128)} %bitcast.64) | data formatting | bytes 3932160 | tf_op jit(solution)/shard_map/reshape;reshape | solution.py:276
  11.0 0.0 copy-done.2
  11.0 0.0 copy-start
  11.0 0.9 reshape.110
  12.0 0.0 copy-start.5
  12.0 0.0 copy-start.9
  12.0 3.3 %copy.27 = f32[6,1024,16]{2,1,0:T(8,128)} copy(f32[6,1024,16]{1,0,2:T(8,128)} %bitcast.65) | data formatting | bytes 786432 | tf_op jit(solution)/shard_map/transpose | solution.py:90
  15.3 0.0 copy-start.12
  15.3 0.0 copy-start.8
  15.3 0.0 copy-start.7
  15.3 0.0 copy-start.11
  15.3 0.0 copy-done
  15.3 0.6 gather_fusion
  16.0 0.0 copy-start.1
  16.0 2.6 %gather_fusion.1 = f32[128,16]{1,0:T(8,128)S(1)} fusion(f32[6144,16]{1,0:T(8,128)} %bitcast.61, s32[1024]{0:T(1024)S(1)} %pad_clamp_fusion), kind=kCustom, calls=%fused_computation.1 | custom fusion | bytes 16896 | tf_op jit(solution)/shard_map/jit(_take)/gather | solution.py:100
  18.6 0.1 broadcast_select_fusion.1
  18.7 0.1 broadcast_select_fusion
  18.8 0.1 fusion.24
  18.9 0.7 collective-permute-start.1
  19.6 1.2 %collective-permute-start = (f32[64,96]{1,0:T(8,128)S(1)}, f32[64,96]{1,0:T(8,128)S(1)}, u32[]{:S(2)}, u32[]{:S(2)}) collective-permute-start(f32[64,96]{1,0:T(8,128)S(1)} %get-tuple-element.18), channel_id=1, source_target_pairs={{0,16},{16,32},{32,48},{48,64},{64,80},{80,96},{96,112},{112,0},{1... | collective-permute-start | bytes 73736 | tf_op jit(solution)/shard_map/ppermute | solution.py:21
  20.8 0.0 copy-done.5
  20.8 0.0 copy-done.9
  20.8 0.2 fusion.20
  21.0 0.4 fusion.22
  21.4 0.0 copy-done.12
  21.4 0.0 copy-start.3
  21.4 0.1 fusion.27
  21.5 0.2 select_reduce_fusion.1
  21.7 0.6 add_bitcast_fusion
  22.3 0.0 copy-done.8
  22.3 0.8 multiply_multiply_fusion
  23.1 0.0 copy-done.7
  23.1 0.0 copy-done.11
  23.1 0.0 copy-done.1
  23.1 4.4 %multiply_reduce_fusion = f32[64,5,1024]{2,0,1:T(8,128)} fusion(f32[3,64,64,1]{2,1,3,0:T(8,128)S(1)} %copy-done.7, f32[3,1024]{1,0:T(4,128)S(1)} %copy-done.11, f32[5,64,1024]{2,1,0:T(8,128)S(1)} %copy-done.1), kind=kOutput, calls=%fused_computation.6 | convolution fusion | flops 756613120 | bytes 2682880 | tf_op jit(solution)/shard_map/dpq,vqe->dvpe/dot_general | solution.py:209
  27.5 0.0 copy-done.3
  27.5 2.0 %concatenate.18.basis_ref = f32[12,8192]{1,0:T(8,128)} concatenate(f32[1,8192]{1,0:T(1,128)S(1)} %get-tuple-element.15, f32[1,8192]{1,0:T(1,128)S(1)} %get-tuple-element.7, f32[1,8192]{1,0:T(1,128)S(1)} %get-tuple-element.8, f32[1,8192]{1,0:T(1,128)S(1)} %get-tuple-element.9, f32[1,8192]{1,0:T(1,128)S(1)} %get-tuple-element.17, f32[1,8192]{1,0:T(1,128)S(1)} %get-tuple-element.10, ...), dimensions={0} | concatenate | bytes 786432 | tf_op jit(solution)/shard_map/concatenate | solution.py:244
  29.5 0.0 collective-permute-done.1
  29.5 0.0 collective-permute-done
  29.5 0.6 pad_maximum_fusion.1.recv_ref
  30.1 16.7 %shard_map.158 = f32[6144,80]{1,0:T(8,128)} custom-call(s32[6144]{0:T(1024)} %copy-done.4, f32[6144,80]{1,0:T(8,128)} %copy-done, f32[6144,16]{1,0:T(8,128)} %bitcast.62, f32[128,96]{1,0:T(8,128)} %pad_maximum_fusion.1.recv_ref, bf16[96,80]{1,0:T(8,128)(2,1)} %constant.137.clone.spread_ref), custom_call_target="tpu_custom_call" | custom-call | flops 566231040 | bytes 9486336 | tf_op jit(solution)/shard_map/pallas_call | solution.py:166
  46.9 2.4 %copy.30 = f32[6144,80]{0,1:T(8,128)S(1)} copy(f32[6144,80]{1,0:T(8,128)} %shard_map.158) | data formatting | bytes 3932160 | tf_op jit(solution)/shard_map/pallas_call | solution.py:166
  49.2 2.1 %reshape.112 = f32[6,1024,16,5]{1,0,3,2:T(8,128)} reshape(f32[6144,80]{0,1:T(8,128)S(1)} %copy.30) | data formatting | bytes 3932160 | tf_op jit(solution)/shard_map/reshape | solution.py:203
  51.3 6.2 %multiply_add_fusion = (f32[5,64,1024]{2,1,0:T(8,128)S(1)}, f32[5,64,1024]{2,1,0:T(8,128)}) fusion(f32[5,64,1024]{2,1,0:T(8,128)S(1)} %copy-done.1, f32[64,16,6,1]{0,1,2,3:T(8,128)} %constant.145, f32[6,1024,16,5]{1,0,3,2:T(8,128)} %reshape.112, f32[64,5,1024]{2,0,1:T(8,128)} %multiply_reduce_fusion, f32[64,1024]{1,0:T(8,128)S(1)} %neg.4), kind=kOutput, calls=%fused_computation.26 | convolution fusion | flops 378798080 | bytes 7495680 | tf_op jit(solution)/shard_map/pqf,feqv->vpe/dot_general | solution.py:205
  57.5 0.2 reduce-precision_convert_fusion.1
  57.7 1.2 %pad_maximum_fusion.rows_ref = bf16[640,1024]{1,0:T(8,128)(2,1)} fusion(bf16[320,1024]{1,0:T(8,128)(2,1)S(1)} %get-tuple-element.5, bf16[320,1024]{1,0:T(8,128)(2,1)S(1)} %get-tuple-element.4), kind=kLoop, calls=%fused_computation.23 | loop fusion | flops 2621440 | bytes 2621440 | tf_op jit(solution)/shard_map/concatenate | solution.py:246
  58.9 0.0 copy-start.6
  58.9 16.2 %shard_map.159 = f32[5,8192]{1,0:T(8,128)} custom-call(bf16[640,1024]{1,0:T(8,128)(2,1)} %pad_maximum_fusion.rows_ref, s32[1,8192]{1,0:T(1,128)} %bitcast.71, f32[12,8192]{1,0:T(8,128)} %concatenate.18.basis_ref), custom_call_target="tpu_custom_call" | custom-call | flops 10737418240 | bytes 1900544 | tf_op jit(solution)/shard_map/pallas_call | solution.py:248
  75.1 0.0 copy-done.6
  75.1 0.0 copy-done.13
  75.1 3.5 %reduce-precision_convert_fusion = (bf16[8192,80]{0,1:T(8,128)(2,1)S(1)}, bf16[8192,80]{0,1:T(8,128)(2,1)S(1)}) fusion(f32[5,8192]{1,0:T(8,128)} %shard_map.159, f32[5,80]{1,0:T(8,128)S(1)} %copy-done.13, s32[80]{0:T(128)S(1)} %and_select_fusion, s32[8192]{0:T(1024)S(1)} %bitcast.70), kind=kOutput, calls=%fused_computation.8 | convolution fusion | flops 43253760 | bytes 2819968 | tf_op jit(solution)/shard_map/dot_general | solution.py:291
  78.6 0.0 copy-done.10
  78.6 7.3 %fusion = f32[1024,160]{0,1:T(8,128)S(1)} fusion(s32[8192]{0:T(1024)S(1)} %copy-done.10, bf16[8192,80]{0,1:T(8,128)(2,1)S(1)} %get-tuple-element.3, bf16[8192,80]{0,1:T(8,128)(2,1)S(1)} %get-tuple-element.2), kind=kOutput, calls=%fused_computation.3 | convolution fusion | flops 2697986048 | bytes 3309568 | tf_op jit(solution)/shard_map/dot_general | solution.py:298
  85.9 0.1 reshape.116
  86.0 19.9 %all_to_all.5 = f32[16,5,1024]{2,1,0:T(8,128)S(1)} all-to-all(f32[16,5,1024]{2,1,0:T(8,128)S(1)} %bitcast.67), channel_id=1, replica_groups=mesh['valve'=8,'bulk'=16] {'bulk'}, dimensions={0} | all-to-all | bytes 655360 | tf_op jit(solution)/shard_map/all_to_all | solution.py:301
  105.9 0.8 copy.47
  (9 shorter events, 0.1 us)
Async XLA Ops:
  1.4 4.8 %copy-start.4 = (s32[6144]{0:T(1024)}, s32[6144]{0:T(1024)S(1)}, u32[]{:S(2)}) copy-start(s32[6144]{0:T(1024)S(1)} %reshape.108.idx_ref) | copy-start | bytes 73732
  8.8 2.2 %copy-start.2 = (f32[96,1024]{1,0:T(8,128)S(1)}, f32[96,1024]{1,0:T(8,128)}, u32[]{:S(2)}) copy-start(f32[96,1024]{1,0:T(8,128)} %param.18) | copy-start | bytes 1179652
  11.0 4.3 %copy-start = (f32[6144,80]{1,0:T(8,128)}, f32[6144,80]{1,0:T(8,128)S(1)}, u32[]{:S(2)}) copy-start(f32[6144,80]{1,0:T(8,128)S(1)} %copy.29.values_ref) | copy-start | bytes 5898244
  12.0 8.8 %copy-start.5 = (s32[8192,1]{0,1:T(1,128)S(1)}, s32[8192,1]{0,1:T(1,128)}, u32[]{:S(2)}) copy-start(s32[8192,1]{0,1:T(1,128)} %param.22) | copy-start | bytes 98308
  12.0 8.8 %copy-start.9 = (bf16[128,128,1]{1,0,2:T(8,128)(2,1)S(1)}, bf16[128,128,1]{1,0,2:T(8,128)(2,1)}, u32[]{:S(2)}) copy-start(bf16[128,128,1]{1,0,2:T(8,128)(2,1)} %constant.146) | copy-start | bytes 98308
  15.3 6.1 %copy-start.12 = (bf16[64,64]{1,0:T(8,128)(2,1)S(1)}, bf16[64,64]{1,0:T(8,128)(2,1)}, u32[]{:S(2)}) copy-start(bf16[64,64]{1,0:T(8,128)(2,1)} %constant.139.clone) | copy-start | bytes 24580
  15.3 7.0 %copy-start.8 = (f32[3,8192]{1,0:T(4,128)S(1)}, f32[3,8192]{1,0:T(4,128)}, u32[]{:S(2)}) copy-start(f32[3,8192]{1,0:T(4,128)} %param.21) | copy-start | bytes 294916
  15.3 7.8 %copy-start.7 = (f32[3,64,64,1]{2,1,3,0:T(8,128)S(1)}, f32[3,64,64,1]{2,1,3,0:T(8,128)}, u32[]{:S(2)}) copy-start(f32[3,64,64,1]{2,1,3,0:T(8,128)} %constant.143) | copy-start | bytes 147460
  15.3 7.8 %copy-start.11 = (f32[3,1024]{1,0:T(4,128)S(1)}, f32[3,1024]{1,0:T(4,128)}, u32[]{:S(2)}) copy-start(f32[3,1024]{1,0:T(4,128)} %param.16) | copy-start | bytes 36868
  16.0 7.1 %copy-start.1 = (f32[5,64,1024]{2,1,0:T(8,128)S(1)}, f32[5,64,1024]{2,1,0:T(8,128)}, u32[]{:S(2)}) copy-start(f32[5,64,1024]{2,1,0:T(8,128)} %param.15) | copy-start | bytes 3932164
  18.9 10.6 %collective-permute-start.1 = (f32[64,96]{1,0:T(8,128)S(1)}, f32[64,96]{1,0:T(8,128)S(1)}, u32[]{:S(2)}, u32[]{:S(2)}) collective-permute-start(f32[64,96]{1,0:T(8,128)S(1)} %get-tuple-element.19), channel_id=1, source_target_pairs={{16,0},{32,16},{48,32},{64,48},{80,64},{96,80},{112,96},{0,112},{1... | collective-permute-start | bytes 73736 | tf_op jit(solution)/shard_map/ppermute | solution.py:22
  19.6 9.9 %collective-permute-start = (f32[64,96]{1,0:T(8,128)S(1)}, f32[64,96]{1,0:T(8,128)S(1)}, u32[]{:S(2)}, u32[]{:S(2)}) collective-permute-start(f32[64,96]{1,0:T(8,128)S(1)} %get-tuple-element.18), channel_id=1, source_target_pairs={{0,16},{16,32},{32,48},{48,64},{64,80},{80,96},{96,112},{112,0},{1... | collective-permute-start | bytes 73736 | tf_op jit(solution)/shard_map/ppermute | solution.py:21
  21.4 6.1 %copy-start.3 = (f32[64,1024]{1,0:T(8,128)S(1)}, f32[64,1024]{1,0:T(8,128)}, u32[]{:S(2)}) copy-start(f32[64,1024]{1,0:T(8,128)} %param.17) | copy-start | bytes 786436
  58.9 16.2 %copy-start.6 = (s32[8192,1]{0,1:T(1,128)S(1)}, s32[8192,1]{0,1:T(1,128)}, u32[]{:S(2)}) copy-start(s32[8192,1]{0,1:T(1,128)} %param.22) | copy-start | bytes 98308
  58.9 16.2 %copy-start.13 = (f32[5,80]{1,0:T(8,128)S(1)}, f32[5,80]{1,0:T(8,128)}, u32[]{:S(2)}) copy-start(f32[5,80]{1,0:T(8,128)} %constant.140.clone) | copy-start | bytes 4804
  75.1 3.5 %copy-start.10 = (s32[8192]{0:T(1024)S(1)}, s32[8192]{0:T(1024)}, u32[]{:S(2)}) copy-start(s32[8192]{0:T(1024)} %add_bitcast_fusion) | copy-start | bytes 98308

commit v6 on v5

--- a/solution.py
+++ b/solution.py
@@ -244,7 +244,7 @@
     basis = jnp.concatenate([jnp.stack(lagrange_at(coords[d])) for d in range(3)], axis=0)
     hi, lo = split_bf16(advanced.reshape(nvars * 64, elems))
     rows = jnp.concatenate([hi, lo], axis=0)
-    tile = 512
+    tile = 1024
     return pl.pallas_call(
         _interp_kernel,
         out_shape=jax.ShapeDtypeStruct((nvars, receptors), jnp.float32),

time: 107 us -> 106 us (level)
  Pallas kernels: 32.9 us -> 31.6 us
    pallas_call x1, Pallas kernels: 16.2 us -> 14.9 us  [receptor_rows(): pl.pallas_call(_interp_kernel, out_shape=jax.ShapeDtypeStruct((nvars, rec...]
where the time goes in v6:
time: 106 us; the launch traced here: 105 us
  Pallas kernels  31.6 us (30%)
  matrix products  24.7 us (23%)
  local copies, waits for them, and re-layouts  21.9 us (21%)
  blocking collectives  19.8 us (19%)
  other arithmetic  4.47 us (4%)
  starting transfers between devices  1.9 us (2%)
    all_to_all x1, blocking collectives, on_device(): got = lax.all_to_all(send, 'bulk', 0, 0, tiled=True)  19.8 us
    pallas_call x1, Pallas kernels, jump_rows(): pl.pallas_call(_jump_kernel, out_shape=jax.ShapeDtypeStruct((idx.shape[0]...  16.7 us
    pallas_call x1, Pallas kernels, receptor_rows(): pl.pallas_call(_interp_kernel, out_shape=jax.ShapeDtypeStruct((nvars, rec...  14.9 us
    dot_general x1, matrix products, on_device(): jnp.dot(by_rank, jnp.concatenate([hi, lo], axis=1), preferred_element_typ...  7.27 us
    dot_general x1, matrix products, surface_term(): jnp.einsum('pqf,feqv->vpe', lift_faces, jump_term, precision=lax.Precisio...  6.17 us
    dot_general x1, matrix products, volume_term(): jnp.einsum('dpq,vqe->dvpe', derivative, solution, precision=lax.Precision...  4.36 us
    dot_general x1, matrix products, on_device(): lax.dot_general(receptor_vals, copies, (((0,), (0,)), ((), ())), precisio...  3.52 us
    unnamed x30, local copies, waits for them, and re-layouts  3.38 us
  transfers between devices with their start and end apart: 2, of which 0 were waited for; matrix products, arithmetic and copies ran while one was open for 8% of the time, Pallas kernels for 0%

profile of v6, /device:TPU:9, one launch (start us, length us, event | category | flops | bytes accessed | tf_op | source)
XLA Modules:
  0.0 105.3 jit_solution(15758585504572703407)
XLA Ops:
  0.6 0.8 reshape.108.idx_ref
  1.4 0.0 copy-start.4
  1.4 0.6 select_reduce_fusion
  2.0 3.0 %convolution_bitcast_fusion = f32[6,1024,16,5]{1,2,3,0:T(8,128)S(1)} fusion(f32[16,6,64,1]{2,0,3,1:T(8,128)} %constant.144, f32[5,64,1024]{2,1,0:T(8,128)} %param.15), kind=kOutput, calls=%fused_computation.18 | convolution fusion | flops 377487360 | bytes 3301376 | tf_op jit(solution)/shard_map/qfp,vpe->feqv/dot_general | solution.py:88
  5.0 1.2 %copy.26 = f32[6,1024,16,5]{1,0,3,2:T(8,128)S(1)} copy(f32[6,1024,16,5]{1,2,3,0:T(8,128)S(1)} %convolution_bitcast_fusion) | data formatting | bytes 3932160 | tf_op jit(solution)/shard_map/qfp,vpe->feqv/transpose | solution.py:88
  6.2 0.0 copy-done.4
  6.2 2.5 %copy.35 = f32[10,8,6,1024]{3,1,2,0:T(8,128)} copy(f32[10,8,6,1024]{3,2,1,0:T(8,128)S(1)} %bitcast.63) | data formatting | bytes 3932160
  8.8 0.0 copy-start.2
  8.8 2.2 %copy.29.values_ref = f32[6144,80]{1,0:T(8,128)S(1)} copy(f32[6144,80]{0,1:T(8,128)} %bitcast.64) | data formatting | bytes 3932160 | tf_op jit(solution)/shard_map/reshape;reshape | solution.py:276
  11.0 0.0 copy-done.2
  11.0 0.0 copy-start
  11.0 0.9 reshape.110
  12.0 0.0 copy-start.5
  12.0 0.0 copy-start.9
  12.0 3.3 %copy.27 = f32[6,1024,16]{2,1,0:T(8,128)} copy(f32[6,1024,16]{1,0,2:T(8,128)} %bitcast.65) | data formatting | bytes 786432 | tf_op jit(solution)/shard_map/transpose | solution.py:90
  15.3 0.0 copy-start.12
  15.3 0.0 copy-start.8
  15.3 0.0 copy-start.7
  15.3 0.0 copy-start.11
  15.3 0.0 copy-done
  15.3 0.6 gather_fusion
  16.0 0.0 copy-start.1
  16.0 2.6 %gather_fusion.1 = f32[128,16]{1,0:T(8,128)S(1)} fusion(f32[6144,16]{1,0:T(8,128)} %bitcast.61, s32[1024]{0:T(1024)S(1)} %pad_clamp_fusion), kind=kCustom, calls=%fused_computation.1 | custom fusion | bytes 16896 | tf_op jit(solution)/shard_map/jit(_take)/gather | solution.py:100
  18.6 0.1 broadcast_select_fusion.1
  18.7 0.1 broadcast_select_fusion
  18.8 0.1 fusion.24
  18.9 0.7 collective-permute-start.1
  19.6 1.2 %collective-permute-start = (f32[64,96]{1,0:T(8,128)S(1)}, f32[64,96]{1,0:T(8,128)S(1)}, u32[]{:S(2)}, u32[]{:S(2)}) collective-permute-start(f32[64,96]{1,0:T(8,128)S(1)} %get-tuple-element.18), channel_id=1, source_target_pairs={{0,16},{16,32},{32,48},{48,64},{64,80},{80,96},{96,112},{112,0},{1... | collective-permute-start | bytes 73736 | tf_op jit(solution)/shard_map/ppermute | solution.py:21
  20.8 0.0 copy-done.5
  20.8 0.0 copy-done.9
  20.8 0.2 fusion.20
  21.0 0.4 fusion.22
  21.4 0.0 copy-done.12
  21.4 0.0 copy-start.3
  21.4 0.1 fusion.27
  21.5 0.2 select_reduce_fusion.1
  21.7 0.6 add_bitcast_fusion
  22.3 0.0 copy-done.8
  22.3 0.8 multiply_multiply_fusion
  23.1 0.0 copy-done.7
  23.1 0.0 copy-done.11
  23.1 0.0 copy-done.1
  23.1 4.4 %multiply_reduce_fusion = f32[64,5,1024]{2,0,1:T(8,128)} fusion(f32[3,64,64,1]{2,1,3,0:T(8,128)S(1)} %copy-done.7, f32[3,1024]{1,0:T(4,128)S(1)} %copy-done.11, f32[5,64,1024]{2,1,0:T(8,128)S(1)} %copy-done.1), kind=kOutput, calls=%fused_computation.6 | convolution fusion | flops 756613120 | bytes 2682880 | tf_op jit(solution)/shard_map/dpq,vqe->dvpe/dot_general | solution.py:209
  27.5 0.0 copy-done.3
  27.5 2.0 %concatenate.18.basis_ref = f32[12,8192]{1,0:T(8,128)} concatenate(f32[1,8192]{1,0:T(1,128)S(1)} %get-tuple-element.15, f32[1,8192]{1,0:T(1,128)S(1)} %get-tuple-element.7, f32[1,8192]{1,0:T(1,128)S(1)} %get-tuple-element.8, f32[1,8192]{1,0:T(1,128)S(1)} %get-tuple-element.9, f32[1,8192]{1,0:T(1,128)S(1)} %get-tuple-element.17, f32[1,8192]{1,0:T(1,128)S(1)} %get-tuple-element.10, ...), dimensions={0} | concatenate | bytes 786432 | tf_op jit(solution)/shard_map/concatenate | solution.py:244
  29.5 0.0 collective-permute-done.1
  29.5 0.0 collective-permute-done
  29.5 0.6 pad_maximum_fusion.1.recv_ref
  30.1 16.7 %shard_map.158 = f32[6144,80]{1,0:T(8,128)} custom-call(s32[6144]{0:T(1024)} %copy-done.4, f32[6144,80]{1,0:T(8,128)} %copy-done, f32[6144,16]{1,0:T(8,128)} %bitcast.62, f32[128,96]{1,0:T(8,128)} %pad_maximum_fusion.1.recv_ref, bf16[96,80]{1,0:T(8,128)(2,1)} %constant.137.clone.spread_ref), custom_call_target="tpu_custom_call" | custom-call | flops 566231040 | bytes 9486336 | tf_op jit(solution)/shard_map/pallas_call | solution.py:166
  46.9 2.4 %copy.30 = f32[6144,80]{0,1:T(8,128)S(1)} copy(f32[6144,80]{1,0:T(8,128)} %shard_map.158) | data formatting | bytes 3932160 | tf_op jit(solution)/shard_map/pallas_call | solution.py:166
  49.2 2.1 %reshape.112 = f32[6,1024,16,5]{1,0,3,2:T(8,128)} reshape(f32[6144,80]{0,1:T(8,128)S(1)} %copy.30) | data formatting | bytes 3932160 | tf_op jit(solution)/shard_map/reshape | solution.py:203
  51.3 6.2 %multiply_add_fusion = (f32[5,64,1024]{2,1,0:T(8,128)S(1)}, f32[5,64,1024]{2,1,0:T(8,128)}) fusion(f32[5,64,1024]{2,1,0:T(8,128)S(1)} %copy-done.1, f32[64,16,6,1]{0,1,2,3:T(8,128)} %constant.145, f32[6,1024,16,5]{1,0,3,2:T(8,128)} %reshape.112, f32[64,5,1024]{2,0,1:T(8,128)} %multiply_reduce_fusion, f32[64,1024]{1,0:T(8,128)S(1)} %neg.4), kind=kOutput, calls=%fused_computation.26 | convolution fusion | flops 378798080 | bytes 7495680 | tf_op jit(solution)/shard_map/pqf,feqv->vpe/dot_general | solution.py:205
  57.5 0.2 reduce-precision_convert_fusion.1
  57.7 1.2 %pad_maximum_fusion.rows_ref = bf16[640,1024]{1,0:T(8,128)(2,1)} fusion(bf16[320,1024]{1,0:T(8,128)(2,1)S(1)} %get-tuple-element.5, bf16[320,1024]{1,0:T(8,128)(2,1)S(1)} %get-tuple-element.4), kind=kLoop, calls=%fused_computation.23 | loop fusion | flops 2621440 | bytes 2621440 | tf_op jit(solution)/shard_map/concatenate | solution.py:246
  58.9 0.0 copy-start.6
  58.9 14.9 %shard_map.159 = f32[5,8192]{1,0:T(8,128)} custom-call(bf16[640,1024]{1,0:T(8,128)(2,1)} %pad_maximum_fusion.rows_ref, s32[1,8192]{1,0:T(1,128)} %bitcast.71, f32[12,8192]{1,0:T(8,128)} %concatenate.18.basis_ref), custom_call_target="tpu_custom_call" | custom-call | flops 10737418240 | bytes 1900544 | tf_op jit(solution)/shard_map/pallas_call | solution.py:248
  73.8 0.0 copy-done.6
  73.8 0.0 copy-done.13
  73.8 3.5 %reduce-precision_convert_fusion = (bf16[8192,80]{0,1:T(8,128)(2,1)S(1)}, bf16[8192,80]{0,1:T(8,128)(2,1)S(1)}) fusion(f32[5,8192]{1,0:T(8,128)} %shard_map.159, f32[5,80]{1,0:T(8,128)S(1)} %copy-done.13, s32[80]{0:T(128)S(1)} %and_select_fusion, s32[8192]{0:T(1024)S(1)} %bitcast.70), kind=kOutput, calls=%fused_computation.8 | convolution fusion | flops 43253760 | bytes 2819968 | tf_op jit(solution)/shard_map/dot_general | solution.py:291
  77.3 0.0 copy-done.10
  77.3 7.3 %fusion = f32[1024,160]{0,1:T(8,128)S(1)} fusion(s32[8192]{0:T(1024)S(1)} %copy-done.10, bf16[8192,80]{0,1:T(8,128)(2,1)S(1)} %get-tuple-element.3, bf16[8192,80]{0,1:T(8,128)(2,1)S(1)} %get-tuple-element.2), kind=kOutput, calls=%fused_computation.3 | convolution fusion | flops 2697986048 | bytes 3309568 | tf_op jit(solution)/shard_map/dot_general | solution.py:298
  84.6 0.1 reshape.116
  84.7 19.8 %all_to_all.5 = f32[16,5,1024]{2,1,0:T(8,128)S(1)} all-to-all(f32[16,5,1024]{2,1,0:T(8,128)S(1)} %bitcast.67), channel_id=1, replica_groups=mesh['valve'=8,'bulk'=16] {'bulk'}, dimensions={0} | all-to-all | bytes 655360 | tf_op jit(solution)/shard_map/all_to_all | solution.py:301
  104.5 0.8 copy.47
  (9 shorter events, 0.1 us)
Async XLA Ops:
  1.4 4.8 %copy-start.4 = (s32[6144]{0:T(1024)}, s32[6144]{0:T(1024)S(1)}, u32[]{:S(2)}) copy-start(s32[6144]{0:T(1024)S(1)} %reshape.108.idx_ref) | copy-start | bytes 73732
  8.8 2.2 %copy-start.2 = (f32[96,1024]{1,0:T(8,128)S(1)}, f32[96,1024]{1,0:T(8,128)}, u32[]{:S(2)}) copy-start(f32[96,1024]{1,0:T(8,128)} %param.18) | copy-start | bytes 1179652
  11.0 4.3 %copy-start = (f32[6144,80]{1,0:T(8,128)}, f32[6144,80]{1,0:T(8,128)S(1)}, u32[]{:S(2)}) copy-start(f32[6144,80]{1,0:T(8,128)S(1)} %copy.29.values_ref) | copy-start | bytes 5898244
  12.0 8.8 %copy-start.5 = (s32[8192,1]{0,1:T(1,128)S(1)}, s32[8192,1]{0,1:T(1,128)}, u32[]{:S(2)}) copy-start(s32[8192,1]{0,1:T(1,128)} %param.22) | copy-start | bytes 98308
  12.0 8.8 %copy-start.9 = (bf16[128,128,1]{1,0,2:T(8,128)(2,1)S(1)}, bf16[128,128,1]{1,0,2:T(8,128)(2,1)}, u32[]{:S(2)}) copy-start(bf16[128,128,1]{1,0,2:T(8,128)(2,1)} %constant.146) | copy-start | bytes 98308
  15.3 6.1 %copy-start.12 = (bf16[64,64]{1,0:T(8,128)(2,1)S(1)}, bf16[64,64]{1,0:T(8,128)(2,1)}, u32[]{:S(2)}) copy-start(bf16[64,64]{1,0:T(8,128)(2,1)} %constant.139.clone) | copy-start | bytes 24580
  15.3 7.0 %copy-start.8 = (f32[3,8192]{1,0:T(4,128)S(1)}, f32[3,8192]{1,0:T(4,128)}, u32[]{:S(2)}) copy-start(f32[3,8192]{1,0:T(4,128)} %param.21) | copy-start | bytes 294916
  15.3 7.8 %copy-start.7 = (f32[3,64,64,1]{2,1,3,0:T(8,128)S(1)}, f32[3,64,64,1]{2,1,3,0:T(8,128)}, u32[]{:S(2)}) copy-start(f32[3,64,64,1]{2,1,3,0:T(8,128)} %constant.143) | copy-start | bytes 147460
  15.3 7.8 %copy-start.11 = (f32[3,1024]{1,0:T(4,128)S(1)}, f32[3,1024]{1,0:T(4,128)}, u32[]{:S(2)}) copy-start(f32[3,1024]{1,0:T(4,128)} %param.16) | copy-start | bytes 36868
  16.0 7.1 %copy-start.1 = (f32[5,64,1024]{2,1,0:T(8,128)S(1)}, f32[5,64,1024]{2,1,0:T(8,128)}, u32[]{:S(2)}) copy-start(f32[5,64,1024]{2,1,0:T(8,128)} %param.15) | copy-start | bytes 3932164
  18.9 10.6 %collective-permute-start.1 = (f32[64,96]{1,0:T(8,128)S(1)}, f32[64,96]{1,0:T(8,128)S(1)}, u32[]{:S(2)}, u32[]{:S(2)}) collective-permute-start(f32[64,96]{1,0:T(8,128)S(1)} %get-tuple-element.19), channel_id=1, source_target_pairs={{16,0},{32,16},{48,32},{64,48},{80,64},{96,80},{112,96},{0,112},{1... | collective-permute-start | bytes 73736 | tf_op jit(solution)/shard_map/ppermute | solution.py:22
  19.6 9.9 %collective-permute-start = (f32[64,96]{1,0:T(8,128)S(1)}, f32[64,96]{1,0:T(8,128)S(1)}, u32[]{:S(2)}, u32[]{:S(2)}) collective-permute-start(f32[64,96]{1,0:T(8,128)S(1)} %get-tuple-element.18), channel_id=1, source_target_pairs={{0,16},{16,32},{32,48},{48,64},{64,80},{80,96},{96,112},{112,0},{1... | collective-permute-start | bytes 73736 | tf_op jit(solution)/shard_map/ppermute | solution.py:21
  21.4 6.1 %copy-start.3 = (f32[64,1024]{1,0:T(8,128)S(1)}, f32[64,1024]{1,0:T(8,128)}, u32[]{:S(2)}) copy-start(f32[64,1024]{1,0:T(8,128)} %param.17) | copy-start | bytes 786436
  58.9 14.9 %copy-start.6 = (s32[8192,1]{0,1:T(1,128)S(1)}, s32[8192,1]{0,1:T(1,128)}, u32[]{:S(2)}) copy-start(s32[8192,1]{0,1:T(1,128)} %param.22) | copy-start | bytes 98308
  58.9 14.9 %copy-start.13 = (f32[5,80]{1,0:T(8,128)S(1)}, f32[5,80]{1,0:T(8,128)}, u32[]{:S(2)}) copy-start(f32[5,80]{1,0:T(8,128)} %constant.140.clone) | copy-start | bytes 4804
  73.8 3.5 %copy-start.10 = (s32[8192]{0:T(1024)S(1)}, s32[8192]{0:T(1024)}, u32[]{:S(2)}) copy-start(s32[8192]{0:T(1024)} %add_bitcast_fusion) | copy-start | bytes 98308

commit v7 on v6

--- a/solution.py
+++ b/solution.py
@@ -244,7 +244,7 @@
     basis = jnp.concatenate([jnp.stack(lagrange_at(coords[d])) for d in range(3)], axis=0)
     hi, lo = split_bf16(advanced.reshape(nvars * 64, elems))
     rows = jnp.concatenate([hi, lo], axis=0)
-    tile = 1024
+    tile = 2048
     return pl.pallas_call(
         _interp_kernel,
         out_shape=jax.ShapeDtypeStruct((nvars, receptors), jnp.float32),

time: 106 us -> 105 us (level)
  no operation moved by 1% of the time
where the time goes in v7:
time: 105 us
  Pallas kernels  31 us (30%)
  matrix products  24.7 us (24%)
  local copies, waits for them, and re-layouts  21.9 us (21%)
  blocking collectives  19.8 us (19%)
  other arithmetic  4.47 us (4%)
  starting transfers between devices  1.89 us (2%)
    all_to_all x1, blocking collectives, on_device(): got = lax.all_to_all(send, 'bulk', 0, 0, tiled=True)  19.8 us
    pallas_call x1, Pallas kernels, jump_rows(): pl.pallas_call(_jump_kernel, out_shape=jax.ShapeDtypeStruct((idx.shape[0]...  16.7 us
    pallas_call x1, Pallas kernels, receptor_rows(): pl.pallas_call(_interp_kernel, out_shape=jax.ShapeDtypeStruct((nvars, rec...  14.2 us
    dot_general x1, matrix products, on_device(): jnp.dot(by_rank, jnp.concatenate([hi, lo], axis=1), preferred_element_typ...  7.28 us
    dot_general x1, matrix products, surface_term(): jnp.einsum('pqf,feqv->vpe', lift_faces, jump_term, precision=lax.Precisio...  6.17 us
    dot_general x1, matrix products, volume_term(): jnp.einsum('dpq,vqe->dvpe', derivative, solution, precision=lax.Precision...  4.36 us
    dot_general x1, matrix products, on_device(): lax.dot_general(receptor_vals, copies, (((0,), (0,)), ((), ())), precisio...  3.52 us
    unnamed x30, local copies, waits for them, and re-layouts  3.38 us
  transfers between devices with their start and end apart: 2, of which 0 were waited for; matrix products, arithmetic and copies ran while one was open for 8% of the time, Pallas kernels for 0%

profile of v7, /device:TPU:9, one launch (start us, length us, event | category | flops | bytes accessed | tf_op | source)
XLA Modules:
  0.0 104.7 jit_solution(7940967167571079937)
XLA Ops:
  0.6 0.8 reshape.108.idx_ref
  1.4 0.0 copy-start.4
  1.4 0.6 select_reduce_fusion
  2.0 3.0 %convolution_bitcast_fusion = f32[6,1024,16,5]{1,2,3,0:T(8,128)S(1)} fusion(f32[16,6,64,1]{2,0,3,1:T(8,128)} %constant.144, f32[5,64,1024]{2,1,0:T(8,128)} %param.15), kind=kOutput, calls=%fused_computation.18 | convolution fusion | flops 377487360 | bytes 3301376 | tf_op jit(solution)/shard_map/qfp,vpe->feqv/dot_general | solution.py:88
  5.0 1.2 %copy.26 = f32[6,1024,16,5]{1,0,3,2:T(8,128)S(1)} copy(f32[6,1024,16,5]{1,2,3,0:T(8,128)S(1)} %convolution_bitcast_fusion) | data formatting | bytes 3932160 | tf_op jit(solution)/shard_map/qfp,vpe->feqv/transpose | solution.py:88
  6.2 0.0 copy-done.4
  6.2 2.5 %copy.35 = f32[10,8,6,1024]{3,1,2,0:T(8,128)} copy(f32[10,8,6,1024]{3,2,1,0:T(8,128)S(1)} %bitcast.63) | data formatting | bytes 3932160
  8.8 0.0 copy-start.2
  8.8 2.2 %copy.29.values_ref = f32[6144,80]{1,0:T(8,128)S(1)} copy(f32[6144,80]{0,1:T(8,128)} %bitcast.64) | data formatting | bytes 3932160 | tf_op jit(solution)/shard_map/reshape;reshape | solution.py:276
  11.0 0.0 copy-done.2
  11.0 0.0 copy-start
  11.0 0.9 reshape.110
  12.0 0.0 copy-start.5
  12.0 0.0 copy-start.9
  12.0 3.3 %copy.27 = f32[6,1024,16]{2,1,0:T(8,128)} copy(f32[6,1024,16]{1,0,2:T(8,128)} %bitcast.65) | data formatting | bytes 786432 | tf_op jit(solution)/shard_map/transpose | solution.py:90
  15.3 0.0 copy-start.12
  15.3 0.0 copy-start.8
  15.3 0.0 copy-start.7
  15.3 0.0 copy-start.11
  15.3 0.0 copy-done
  15.3 0.6 gather_fusion
  16.0 0.0 copy-start.1
  16.0 2.6 %gather_fusion.1 = f32[128,16]{1,0:T(8,128)S(1)} fusion(f32[6144,16]{1,0:T(8,128)} %bitcast.61, s32[1024]{0:T(1024)S(1)} %pad_clamp_fusion), kind=kCustom, calls=%fused_computation.1 | custom fusion | bytes 16896 | tf_op jit(solution)/shard_map/jit(_take)/gather | solution.py:100
  18.6 0.1 broadcast_select_fusion.1
  18.7 0.1 broadcast_select_fusion
  18.8 0.1 fusion.24
  18.9 0.7 collective-permute-start.1
  19.6 1.2 %collective-permute-start = (f32[64,96]{1,0:T(8,128)S(1)}, f32[64,96]{1,0:T(8,128)S(1)}, u32[]{:S(2)}, u32[]{:S(2)}) collective-permute-start(f32[64,96]{1,0:T(8,128)S(1)} %get-tuple-element.18), channel_id=1, source_target_pairs={{0,16},{16,32},{32,48},{48,64},{64,80},{80,96},{96,112},{112,0},{1... | collective-permute-start | bytes 73736 | tf_op jit(solution)/shard_map/ppermute | solution.py:21
  20.8 0.0 copy-done.5
  20.8 0.0 copy-done.9
  20.8 0.2 fusion.20
  21.0 0.4 fusion.22
  21.4 0.0 copy-done.12
  21.4 0.0 copy-start.3
  21.4 0.1 fusion.27
  21.5 0.2 select_reduce_fusion.1
  21.7 0.6 add_bitcast_fusion
  22.3 0.0 copy-done.8
  22.3 0.8 multiply_multiply_fusion
  23.1 0.0 copy-done.7
  23.1 0.0 copy-done.11
  23.1 0.0 copy-done.1
  23.1 4.4 %multiply_reduce_fusion = f32[64,5,1024]{2,0,1:T(8,128)} fusion(f32[3,64,64,1]{2,1,3,0:T(8,128)S(1)} %copy-done.7, f32[3,1024]{1,0:T(4,128)S(1)} %copy-done.11, f32[5,64,1024]{2,1,0:T(8,128)S(1)} %copy-done.1), kind=kOutput, calls=%fused_computation.6 | convolution fusion | flops 756613120 | bytes 2682880 | tf_op jit(solution)/shard_map/dpq,vqe->dvpe/dot_general | solution.py:209
  27.5 0.0 copy-done.3
  27.5 2.0 %concatenate.18.basis_ref = f32[12,8192]{1,0:T(8,128)} concatenate(f32[1,8192]{1,0:T(1,128)S(1)} %get-tuple-element.15, f32[1,8192]{1,0:T(1,128)S(1)} %get-tuple-element.7, f32[1,8192]{1,0:T(1,128)S(1)} %get-tuple-element.8, f32[1,8192]{1,0:T(1,128)S(1)} %get-tuple-element.9, f32[1,8192]{1,0:T(1,128)S(1)} %get-tuple-element.17, f32[1,8192]{1,0:T(1,128)S(1)} %get-tuple-element.10, ...), dimensions={0} | concatenate | bytes 786432 | tf_op jit(solution)/shard_map/concatenate | solution.py:244
  29.5 0.0 collective-permute-done.1
  29.5 0.0 collective-permute-done
  29.5 0.6 pad_maximum_fusion.1.recv_ref
  30.1 16.7 %shard_map.158 = f32[6144,80]{1,0:T(8,128)} custom-call(s32[6144]{0:T(1024)} %copy-done.4, f32[6144,80]{1,0:T(8,128)} %copy-done, f32[6144,16]{1,0:T(8,128)} %bitcast.62, f32[128,96]{1,0:T(8,128)} %pad_maximum_fusion.1.recv_ref, bf16[96,80]{1,0:T(8,128)(2,1)} %constant.137.clone.spread_ref), custom_call_target="tpu_custom_call" | custom-call | flops 566231040 | bytes 9486336 | tf_op jit(solution)/shard_map/pallas_call | solution.py:166
  46.9 2.4 %copy.30 = f32[6144,80]{0,1:T(8,128)S(1)} copy(f32[6144,80]{1,0:T(8,128)} %shard_map.158) | data formatting | bytes 3932160 | tf_op jit(solution)/shard_map/pallas_call | solution.py:166
  49.2 2.1 %reshape.112 = f32[6,1024,16,5]{1,0,3,2:T(8,128)} reshape(f32[6144,80]{0,1:T(8,128)S(1)} %copy.30) | data formatting | bytes 3932160 | tf_op jit(solution)/shard_map/reshape | solution.py:203
  51.3 6.2 %multiply_add_fusion = (f32[5,64,1024]{2,1,0:T(8,128)S(1)}, f32[5,64,1024]{2,1,0:T(8,128)}) fusion(f32[5,64,1024]{2,1,0:T(8,128)S(1)} %copy-done.1, f32[64,16,6,1]{0,1,2,3:T(8,128)} %constant.145, f32[6,1024,16,5]{1,0,3,2:T(8,128)} %reshape.112, f32[64,5,1024]{2,0,1:T(8,128)} %multiply_reduce_fusion, f32[64,1024]{1,0:T(8,128)S(1)} %neg.4), kind=kOutput, calls=%fused_computation.26 | convolution fusion | flops 378798080 | bytes 7495680 | tf_op jit(solution)/shard_map/pqf,feqv->vpe/dot_general | solution.py:205
  57.5 0.2 reduce-precision_convert_fusion.1
  57.7 1.2 %pad_maximum_fusion.rows_ref = bf16[640,1024]{1,0:T(8,128)(2,1)} fusion(bf16[320,1024]{1,0:T(8,128)(2,1)S(1)} %get-tuple-element.5, bf16[320,1024]{1,0:T(8,128)(2,1)S(1)} %get-tuple-element.4), kind=kLoop, calls=%fused_computation.23 | loop fusion | flops 2621440 | bytes 2621440 | tf_op jit(solution)/shard_map/concatenate | solution.py:246
  58.9 0.0 copy-start.6
  58.9 14.2 %shard_map.159 = f32[5,8192]{1,0:T(8,128)} custom-call(bf16[640,1024]{1,0:T(8,128)(2,1)} %pad_maximum_fusion.rows_ref, s32[1,8192]{1,0:T(1,128)} %bitcast.71, f32[12,8192]{1,0:T(8,128)} %concatenate.18.basis_ref), custom_call_target="tpu_custom_call" | custom-call | flops 10737418240 | bytes 1900544 | tf_op jit(solution)/shard_map/pallas_call | solution.py:248
  73.1 0.0 copy-done.6
  73.1 0.0 copy-done.13
  73.1 3.5 %reduce-precision_convert_fusion = (bf16[8192,80]{0,1:T(8,128)(2,1)S(1)}, bf16[8192,80]{0,1:T(8,128)(2,1)S(1)}) fusion(f32[5,8192]{1,0:T(8,128)} %shard_map.159, f32[5,80]{1,0:T(8,128)S(1)} %copy-done.13, s32[80]{0:T(128)S(1)} %and_select_fusion, s32[8192]{0:T(1024)S(1)} %bitcast.70), kind=kOutput, calls=%fused_computation.8 | convolution fusion | flops 43253760 | bytes 2819968 | tf_op jit(solution)/shard_map/dot_general | solution.py:291
  76.7 0.0 copy-done.10
  76.7 7.3 %fusion = f32[1024,160]{0,1:T(8,128)S(1)} fusion(s32[8192]{0:T(1024)S(1)} %copy-done.10, bf16[8192,80]{0,1:T(8,128)(2,1)S(1)} %get-tuple-element.3, bf16[8192,80]{0,1:T(8,128)(2,1)S(1)} %get-tuple-element.2), kind=kOutput, calls=%fused_computation.3 | convolution fusion | flops 2697986048 | bytes 3309568 | tf_op jit(solution)/shard_map/dot_general | solution.py:298
  84.0 0.1 reshape.116
  84.1 19.8 %all_to_all.5 = f32[16,5,1024]{2,1,0:T(8,128)S(1)} all-to-all(f32[16,5,1024]{2,1,0:T(8,128)S(1)} %bitcast.67), channel_id=1, replica_groups=mesh['valve'=8,'bulk'=16] {'bulk'}, dimensions={0} | all-to-all | bytes 655360 | tf_op jit(solution)/shard_map/all_to_all | solution.py:301
  103.9 0.8 copy.47
  (9 shorter events, 0.1 us)
Async XLA Ops:
  1.4 4.8 %copy-start.4 = (s32[6144]{0:T(1024)}, s32[6144]{0:T(1024)S(1)}, u32[]{:S(2)}) copy-start(s32[6144]{0:T(1024)S(1)} %reshape.108.idx_ref) | copy-start | bytes 73732
  8.8 2.2 %copy-start.2 = (f32[96,1024]{1,0:T(8,128)S(1)}, f32[96,1024]{1,0:T(8,128)}, u32[]{:S(2)}) copy-start(f32[96,1024]{1,0:T(8,128)} %param.18) | copy-start | bytes 1179652
  11.0 4.3 %copy-start = (f32[6144,80]{1,0:T(8,128)}, f32[6144,80]{1,0:T(8,128)S(1)}, u32[]{:S(2)}) copy-start(f32[6144,80]{1,0:T(8,128)S(1)} %copy.29.values_ref) | copy-start | bytes 5898244
  12.0 8.8 %copy-start.5 = (s32[8192,1]{0,1:T(1,128)S(1)}, s32[8192,1]{0,1:T(1,128)}, u32[]{:S(2)}) copy-start(s32[8192,1]{0,1:T(1,128)} %param.22) | copy-start | bytes 98308
  12.0 8.8 %copy-start.9 = (bf16[128,128,1]{1,0,2:T(8,128)(2,1)S(1)}, bf16[128,128,1]{1,0,2:T(8,128)(2,1)}, u32[]{:S(2)}) copy-start(bf16[128,128,1]{1,0,2:T(8,128)(2,1)} %constant.146) | copy-start | bytes 98308
  15.3 6.1 %copy-start.12 = (bf16[64,64]{1,0:T(8,128)(2,1)S(1)}, bf16[64,64]{1,0:T(8,128)(2,1)}, u32[]{:S(2)}) copy-start(bf16[64,64]{1,0:T(8,128)(2,1)} %constant.139.clone) | copy-start | bytes 24580
  15.3 7.0 %copy-start.8 = (f32[3,8192]{1,0:T(4,128)S(1)}, f32[3,8192]{1,0:T(4,128)}, u32[]{:S(2)}) copy-start(f32[3,8192]{1,0:T(4,128)} %param.21) | copy-start | bytes 294916
  15.3 7.8 %copy-start.7 = (f32[3,64,64,1]{2,1,3,0:T(8,128)S(1)}, f32[3,64,64,1]{2,1,3,0:T(8,128)}, u32[]{:S(2)}) copy-start(f32[3,64,64,1]{2,1,3,0:T(8,128)} %constant.143) | copy-start | bytes 147460
  15.3 7.8 %copy-start.11 = (f32[3,1024]{1,0:T(4,128)S(1)}, f32[3,1024]{1,0:T(4,128)}, u32[]{:S(2)}) copy-start(f32[3,1024]{1,0:T(4,128)} %param.16) | copy-start | bytes 36868
  16.0 7.1 %copy-start.1 = (f32[5,64,1024]{2,1,0:T(8,128)S(1)}, f32[5,64,1024]{2,1,0:T(8,128)}, u32[]{:S(2)}) copy-start(f32[5,64,1024]{2,1,0:T(8,128)} %param.15) | copy-start | bytes 3932164
  18.9 10.6 %collective-permute-start.1 = (f32[64,96]{1,0:T(8,128)S(1)}, f32[64,96]{1,0:T(8,128)S(1)}, u32[]{:S(2)}, u32[]{:S(2)}) collective-permute-start(f32[64,96]{1,0:T(8,128)S(1)} %get-tuple-element.19), channel_id=1, source_target_pairs={{16,0},{32,16},{48,32},{64,48},{80,64},{96,80},{112,96},{0,112},{1... | collective-permute-start | bytes 73736 | tf_op jit(solution)/shard_map/ppermute | solution.py:22
  19.6 9.9 %collective-permute-start = (f32[64,96]{1,0:T(8,128)S(1)}, f32[64,96]{1,0:T(8,128)S(1)}, u32[]{:S(2)}, u32[]{:S(2)}) collective-permute-start(f32[64,96]{1,0:T(8,128)S(1)} %get-tuple-element.18), channel_id=1, source_target_pairs={{0,16},{16,32},{32,48},{48,64},{64,80},{80,96},{96,112},{112,0},{1... | collective-permute-start | bytes 73736 | tf_op jit(solution)/shard_map/ppermute | solution.py:21
  21.4 6.1 %copy-start.3 = (f32[64,1024]{1,0:T(8,128)S(1)}, f32[64,1024]{1,0:T(8,128)}, u32[]{:S(2)}) copy-start(f32[64,1024]{1,0:T(8,128)} %param.17) | copy-start | bytes 786436
  58.9 14.2 %copy-start.6 = (s32[8192,1]{0,1:T(1,128)S(1)}, s32[8192,1]{0,1:T(1,128)}, u32[]{:S(2)}) copy-start(s32[8192,1]{0,1:T(1,128)} %param.22) | copy-start | bytes 98308
  58.9 14.2 %copy-start.13 = (f32[5,80]{1,0:T(8,128)S(1)}, f32[5,80]{1,0:T(8,128)}, u32[]{:S(2)}) copy-start(f32[5,80]{1,0:T(8,128)} %constant.140.clone) | copy-start | bytes 4804
  73.1 3.5 %copy-start.10 = (s32[8192]{0:T(1024)S(1)}, s32[8192]{0:T(1024)}, u32[]{:S(2)}) copy-start(s32[8192]{0:T(1024)} %add_bitcast_fusion) | copy-start | bytes 98308

commit v8 on v7

--- a/solution.py
+++ b/solution.py
@@ -129,14 +129,14 @@
     table_ref[pl.ds(own_rows, recv_ref.shape[0]), :] = recv_ref[...]
 
     def body(i, carry):
-        base = pl.multiple_of(i * 16, 16)
-        for j in range(16):
+        base = pl.multiple_of(i * 32, 32)
+        for j in range(32):
             row = idx_ref[base + j]
             outer_ref[pl.ds(base + j, 1), :] = table_ref[pl.ds(row, 1), :]
         return carry
 
-    lax.fori_loop(0, own_rows // 16, body, 0)
-    chunk = 512
+    lax.fori_loop(0, own_rows // 32, body, 0)
+    chunk = 1024
     spread = spread_ref[...]
 
     def rows(c, carry):

time: 105 us -> 103 us (0.981)
  Pallas kernels: 31 us -> 29.3 us
    pallas_call x1, Pallas kernels: 16.7 us -> 15.1 us  [jump_rows(): pl.pallas_call(_jump_kernel, out_shape=jax.ShapeDtypeStruct((idx.shape[0]...]
where the time goes in v8:
time: 103 us
  Pallas kernels  29.3 us (28%)
  matrix products  24.7 us (24%)
  local copies, waits for them, and re-layouts  21.9 us (21%)
  blocking collectives  19.8 us (19%)
  other arithmetic  4.47 us (4%)
  starting transfers between devices  1.89 us (2%)
    all_to_all x1, blocking collectives, on_device(): got = lax.all_to_all(send, 'bulk', 0, 0, tiled=True)  19.8 us
    pallas_call x1, Pallas kernels, jump_rows(): pl.pallas_call(_jump_kernel, out_shape=jax.ShapeDtypeStruct((idx.shape[0]...  15.1 us
    pallas_call x1, Pallas kernels, receptor_rows(): pl.pallas_call(_interp_kernel, out_shape=jax.ShapeDtypeStruct((nvars, rec...  14.2 us
    dot_general x1, matrix products, on_device(): jnp.dot(by_rank, jnp.concatenate([hi, lo], axis=1), preferred_element_typ...  7.28 us
    dot_general x1, matrix products, surface_term(): jnp.einsum('pqf,feqv->vpe', lift_faces, jump_term, precision=lax.Precisio...  6.17 us
    dot_general x1, matrix products, volume_term(): jnp.einsum('dpq,vqe->dvpe', derivative, solution, precision=lax.Precision...  4.36 us
    dot_general x1, matrix products, on_device(): lax.dot_general(receptor_vals, copies, (((0,), (0,)), ((), ())), precisio...  3.52 us
    unnamed x30, local copies, waits for them, and re-layouts  3.38 us
  transfers between devices with their start and end apart: 2, of which 0 were waited for; matrix products, arithmetic and copies ran while one was open for 8% of the time, Pallas kernels for 0%

profile of v8, /device:TPU:9, one launch (start us, length us, event | category | flops | bytes accessed | tf_op | source)
XLA Modules:
  0.0 103.0 jit_solution(18027601103742955943)
XLA Ops:
  0.6 0.8 reshape.108.idx_ref
  1.4 0.0 copy-start.4
  1.4 0.6 select_reduce_fusion
  2.0 3.0 %convolution_bitcast_fusion = f32[6,1024,16,5]{1,2,3,0:T(8,128)S(1)} fusion(f32[16,6,64,1]{2,0,3,1:T(8,128)} %constant.144, f32[5,64,1024]{2,1,0:T(8,128)} %param.15), kind=kOutput, calls=%fused_computation.18 | convolution fusion | flops 377487360 | bytes 3301376 | tf_op jit(solution)/shard_map/qfp,vpe->feqv/dot_general | solution.py:88
  5.0 1.2 %copy.26 = f32[6,1024,16,5]{1,0,3,2:T(8,128)S(1)} copy(f32[6,1024,16,5]{1,2,3,0:T(8,128)S(1)} %convolution_bitcast_fusion) | data formatting | bytes 3932160 | tf_op jit(solution)/shard_map/qfp,vpe->feqv/transpose | solution.py:88
  6.2 0.0 copy-done.4
  6.2 2.5 %copy.35 = f32[10,8,6,1024]{3,1,2,0:T(8,128)} copy(f32[10,8,6,1024]{3,2,1,0:T(8,128)S(1)} %bitcast.63) | data formatting | bytes 3932160
  8.8 0.0 copy-start.2
  8.8 2.2 %copy.29.values_ref = f32[6144,80]{1,0:T(8,128)S(1)} copy(f32[6144,80]{0,1:T(8,128)} %bitcast.64) | data formatting | bytes 3932160 | tf_op jit(solution)/shard_map/reshape;reshape | solution.py:276
  11.0 0.0 copy-done.2
  11.0 0.0 copy-start
  11.0 0.9 reshape.110
  12.0 0.0 copy-start.5
  12.0 0.0 copy-start.9
  12.0 3.3 %copy.27 = f32[6,1024,16]{2,1,0:T(8,128)} copy(f32[6,1024,16]{1,0,2:T(8,128)} %bitcast.65) | data formatting | bytes 786432 | tf_op jit(solution)/shard_map/transpose | solution.py:90
  15.3 0.0 copy-start.12
  15.3 0.0 copy-start.8
  15.3 0.0 copy-start.7
  15.3 0.0 copy-start.11
  15.3 0.0 copy-done
  15.3 0.6 gather_fusion
  16.0 0.0 copy-start.1
  16.0 2.6 %gather_fusion.1 = f32[128,16]{1,0:T(8,128)S(1)} fusion(f32[6144,16]{1,0:T(8,128)} %bitcast.61, s32[1024]{0:T(1024)S(1)} %pad_clamp_fusion), kind=kCustom, calls=%fused_computation.1 | custom fusion | bytes 16896 | tf_op jit(solution)/shard_map/jit(_take)/gather | solution.py:100
  18.6 0.1 broadcast_select_fusion.1
  18.7 0.1 broadcast_select_fusion
  18.8 0.1 fusion.24
  18.9 0.7 collective-permute-start.1
  19.6 1.2 %collective-permute-start = (f32[64,96]{1,0:T(8,128)S(1)}, f32[64,96]{1,0:T(8,128)S(1)}, u32[]{:S(2)}, u32[]{:S(2)}) collective-permute-start(f32[64,96]{1,0:T(8,128)S(1)} %get-tuple-element.18), channel_id=1, source_target_pairs={{0,16},{16,32},{32,48},{48,64},{64,80},{80,96},{96,112},{112,0},{1... | collective-permute-start | bytes 73736 | tf_op jit(solution)/shard_map/ppermute | solution.py:21
  20.8 0.0 copy-done.5
  20.8 0.0 copy-done.9
  20.8 0.2 fusion.20
  21.0 0.4 fusion.22
  21.4 0.0 copy-done.12
  21.4 0.0 copy-start.3
  21.4 0.1 fusion.27
  21.5 0.2 select_reduce_fusion.1
  21.7 0.6 add_bitcast_fusion
  22.3 0.0 copy-done.8
  22.3 0.8 multiply_multiply_fusion
  23.1 0.0 copy-done.7
  23.1 0.0 copy-done.11
  23.1 0.0 copy-done.1
  23.1 4.4 %multiply_reduce_fusion = f32[64,5,1024]{2,0,1:T(8,128)} fusion(f32[3,64,64,1]{2,1,3,0:T(8,128)S(1)} %copy-done.7, f32[3,1024]{1,0:T(4,128)S(1)} %copy-done.11, f32[5,64,1024]{2,1,0:T(8,128)S(1)} %copy-done.1), kind=kOutput, calls=%fused_computation.6 | convolution fusion | flops 756613120 | bytes 2682880 | tf_op jit(solution)/shard_map/dpq,vqe->dvpe/dot_general | solution.py:209
  27.5 0.0 copy-done.3
  27.5 2.0 %concatenate.18.basis_ref = f32[12,8192]{1,0:T(8,128)} concatenate(f32[1,8192]{1,0:T(1,128)S(1)} %get-tuple-element.15, f32[1,8192]{1,0:T(1,128)S(1)} %get-tuple-element.7, f32[1,8192]{1,0:T(1,128)S(1)} %get-tuple-element.8, f32[1,8192]{1,0:T(1,128)S(1)} %get-tuple-element.9, f32[1,8192]{1,0:T(1,128)S(1)} %get-tuple-element.17, f32[1,8192]{1,0:T(1,128)S(1)} %get-tuple-element.10, ...), dimensions={0} | concatenate | bytes 786432 | tf_op jit(solution)/shard_map/concatenate | solution.py:244
  29.5 0.0 collective-permute-done.1
  29.5 0.0 collective-permute-done
  29.5 0.6 pad_maximum_fusion.1.recv_ref
  30.1 15.1 %shard_map.158 = f32[6144,80]{1,0:T(8,128)} custom-call(s32[6144]{0:T(1024)} %copy-done.4, f32[6144,80]{1,0:T(8,128)} %copy-done, f32[6144,16]{1,0:T(8,128)} %bitcast.62, f32[128,96]{1,0:T(8,128)} %pad_maximum_fusion.1.recv_ref, bf16[96,80]{1,0:T(8,128)(2,1)} %constant.137.clone.spread_ref), custom_call_target="tpu_custom_call" | custom-call | flops 566231040 | bytes 9486336 | tf_op jit(solution)/shard_map/pallas_call | solution.py:166
  45.2 2.4 %copy.30 = f32[6144,80]{0,1:T(8,128)S(1)} copy(f32[6144,80]{1,0:T(8,128)} %shard_map.158) | data formatting | bytes 3932160 | tf_op jit(solution)/shard_map/pallas_call | solution.py:166
  47.6 2.1 %reshape.112 = f32[6,1024,16,5]{1,0,3,2:T(8,128)} reshape(f32[6144,80]{0,1:T(8,128)S(1)} %copy.30) | data formatting | bytes 3932160 | tf_op jit(solution)/shard_map/reshape | solution.py:203
  49.7 6.2 %multiply_add_fusion = (f32[5,64,1024]{2,1,0:T(8,128)S(1)}, f32[5,64,1024]{2,1,0:T(8,128)}) fusion(f32[5,64,1024]{2,1,0:T(8,128)S(1)} %copy-done.1, f32[64,16,6,1]{0,1,2,3:T(8,128)} %constant.145, f32[6,1024,16,5]{1,0,3,2:T(8,128)} %reshape.112, f32[64,5,1024]{2,0,1:T(8,128)} %multiply_reduce_fusion, f32[64,1024]{1,0:T(8,128)S(1)} %neg.4), kind=kOutput, calls=%fused_computation.26 | convolution fusion | flops 378798080 | bytes 7495680 | tf_op jit(solution)/shard_map/pqf,feqv->vpe/dot_general | solution.py:205
  55.8 0.2 reduce-precision_convert_fusion.1
  56.0 1.2 %pad_maximum_fusion.rows_ref = bf16[640,1024]{1,0:T(8,128)(2,1)} fusion(bf16[320,1024]{1,0:T(8,128)(2,1)S(1)} %get-tuple-element.5, bf16[320,1024]{1,0:T(8,128)(2,1)S(1)} %get-tuple-element.4), kind=kLoop, calls=%fused_computation.23 | loop fusion | flops 2621440 | bytes 2621440 | tf_op jit(solution)/shard_map/concatenate | solution.py:246
  57.2 0.0 copy-start.6
  57.2 14.2 %shard_map.159 = f32[5,8192]{1,0:T(8,128)} custom-call(bf16[640,1024]{1,0:T(8,128)(2,1)} %pad_maximum_fusion.rows_ref, s32[1,8192]{1,0:T(1,128)} %bitcast.71, f32[12,8192]{1,0:T(8,128)} %concatenate.18.basis_ref), custom_call_target="tpu_custom_call" | custom-call | flops 10737418240 | bytes 1900544 | tf_op jit(solution)/shard_map/pallas_call | solution.py:248
  71.5 0.0 copy-done.6
  71.5 0.0 copy-done.13
  71.5 3.5 %reduce-precision_convert_fusion = (bf16[8192,80]{0,1:T(8,128)(2,1)S(1)}, bf16[8192,80]{0,1:T(8,128)(2,1)S(1)}) fusion(f32[5,8192]{1,0:T(8,128)} %shard_map.159, f32[5,80]{1,0:T(8,128)S(1)} %copy-done.13, s32[80]{0:T(128)S(1)} %and_select_fusion, s32[8192]{0:T(1024)S(1)} %bitcast.70), kind=kOutput, calls=%fused_computation.8 | convolution fusion | flops 43253760 | bytes 2819968 | tf_op jit(solution)/shard_map/dot_general | solution.py:291
  75.0 0.0 copy-done.10
  75.0 7.3 %fusion = f32[1024,160]{0,1:T(8,128)S(1)} fusion(s32[8192]{0:T(1024)S(1)} %copy-done.10, bf16[8192,80]{0,1:T(8,128)(2,1)S(1)} %get-tuple-element.3, bf16[8192,80]{0,1:T(8,128)(2,1)S(1)} %get-tuple-element.2), kind=kOutput, calls=%fused_computation.3 | convolution fusion | flops 2697986048 | bytes 3309568 | tf_op jit(solution)/shard_map/dot_general | solution.py:298
  82.3 0.1 reshape.116
  82.4 19.8 %all_to_all.5 = f32[16,5,1024]{2,1,0:T(8,128)S(1)} all-to-all(f32[16,5,1024]{2,1,0:T(8,128)S(1)} %bitcast.67), channel_id=1, replica_groups=mesh['valve'=8,'bulk'=16] {'bulk'}, dimensions={0} | all-to-all | bytes 655360 | tf_op jit(solution)/shard_map/all_to_all | solution.py:301
  102.2 0.8 copy.47
  (9 shorter events, 0.1 us)
Async XLA Ops:
  1.4 4.8 %copy-start.4 = (s32[6144]{0:T(1024)}, s32[6144]{0:T(1024)S(1)}, u32[]{:S(2)}) copy-start(s32[6144]{0:T(1024)S(1)} %reshape.108.idx_ref) | copy-start | bytes 73732
  8.8 2.2 %copy-start.2 = (f32[96,1024]{1,0:T(8,128)S(1)}, f32[96,1024]{1,0:T(8,128)}, u32[]{:S(2)}) copy-start(f32[96,1024]{1,0:T(8,128)} %param.18) | copy-start | bytes 1179652
  11.0 4.3 %copy-start = (f32[6144,80]{1,0:T(8,128)}, f32[6144,80]{1,0:T(8,128)S(1)}, u32[]{:S(2)}) copy-start(f32[6144,80]{1,0:T(8,128)S(1)} %copy.29.values_ref) | copy-start | bytes 5898244
  12.0 8.8 %copy-start.5 = (s32[8192,1]{0,1:T(1,128)S(1)}, s32[8192,1]{0,1:T(1,128)}, u32[]{:S(2)}) copy-start(s32[8192,1]{0,1:T(1,128)} %param.22) | copy-start | bytes 98308
  12.0 8.8 %copy-start.9 = (bf16[128,128,1]{1,0,2:T(8,128)(2,1)S(1)}, bf16[128,128,1]{1,0,2:T(8,128)(2,1)}, u32[]{:S(2)}) copy-start(bf16[128,128,1]{1,0,2:T(8,128)(2,1)} %constant.146) | copy-start | bytes 98308
  15.3 6.1 %copy-start.12 = (bf16[64,64]{1,0:T(8,128)(2,1)S(1)}, bf16[64,64]{1,0:T(8,128)(2,1)}, u32[]{:S(2)}) copy-start(bf16[64,64]{1,0:T(8,128)(2,1)} %constant.139.clone) | copy-start | bytes 24580
  15.3 7.0 %copy-start.8 = (f32[3,8192]{1,0:T(4,128)S(1)}, f32[3,8192]{1,0:T(4,128)}, u32[]{:S(2)}) copy-start(f32[3,8192]{1,0:T(4,128)} %param.21) | copy-start | bytes 294916
  15.3 7.8 %copy-start.7 = (f32[3,64,64,1]{2,1,3,0:T(8,128)S(1)}, f32[3,64,64,1]{2,1,3,0:T(8,128)}, u32[]{:S(2)}) copy-start(f32[3,64,64,1]{2,1,3,0:T(8,128)} %constant.143) | copy-start | bytes 147460
  15.3 7.8 %copy-start.11 = (f32[3,1024]{1,0:T(4,128)S(1)}, f32[3,1024]{1,0:T(4,128)}, u32[]{:S(2)}) copy-start(f32[3,1024]{1,0:T(4,128)} %param.16) | copy-start | bytes 36868
  16.0 7.1 %copy-start.1 = (f32[5,64,1024]{2,1,0:T(8,128)S(1)}, f32[5,64,1024]{2,1,0:T(8,128)}, u32[]{:S(2)}) copy-start(f32[5,64,1024]{2,1,0:T(8,128)} %param.15) | copy-start | bytes 3932164
  18.9 10.6 %collective-permute-start.1 = (f32[64,96]{1,0:T(8,128)S(1)}, f32[64,96]{1,0:T(8,128)S(1)}, u32[]{:S(2)}, u32[]{:S(2)}) collective-permute-start(f32[64,96]{1,0:T(8,128)S(1)} %get-tuple-element.19), channel_id=1, source_target_pairs={{16,0},{32,16},{48,32},{64,48},{80,64},{96,80},{112,96},{0,112},{1... | collective-permute-start | bytes 73736 | tf_op jit(solution)/shard_map/ppermute | solution.py:22
  19.6 9.9 %collective-permute-start = (f32[64,96]{1,0:T(8,128)S(1)}, f32[64,96]{1,0:T(8,128)S(1)}, u32[]{:S(2)}, u32[]{:S(2)}) collective-permute-start(f32[64,96]{1,0:T(8,128)S(1)} %get-tuple-element.18), channel_id=1, source_target_pairs={{0,16},{16,32},{32,48},{48,64},{64,80},{80,96},{96,112},{112,0},{1... | collective-permute-start | bytes 73736 | tf_op jit(solution)/shard_map/ppermute | solution.py:21
  21.4 6.1 %copy-start.3 = (f32[64,1024]{1,0:T(8,128)S(1)}, f32[64,1024]{1,0:T(8,128)}, u32[]{:S(2)}) copy-start(f32[64,1024]{1,0:T(8,128)} %param.17) | copy-start | bytes 786436
  57.2 14.2 %copy-start.6 = (s32[8192,1]{0,1:T(1,128)S(1)}, s32[8192,1]{0,1:T(1,128)}, u32[]{:S(2)}) copy-start(s32[8192,1]{0,1:T(1,128)} %param.22) | copy-start | bytes 98308
  57.2 14.2 %copy-start.13 = (f32[5,80]{1,0:T(8,128)S(1)}, f32[5,80]{1,0:T(8,128)}, u32[]{:S(2)}) copy-start(f32[5,80]{1,0:T(8,128)} %constant.140.clone) | copy-start | bytes 4804
  71.5 3.5 %copy-start.10 = (s32[8192]{0:T(1024)S(1)}, s32[8192]{0:T(1024)}, u32[]{:S(2)}) copy-start(s32[8192]{0:T(1024)} %add_bitcast_fusion) | copy-start | bytes 98308

commit v9 on v8

--- a/solution.py
+++ b/solution.py
@@ -129,14 +129,14 @@
     table_ref[pl.ds(own_rows, recv_ref.shape[0]), :] = recv_ref[...]
 
     def body(i, carry):
-        base = pl.multiple_of(i * 32, 32)
-        for j in range(32):
+        base = pl.multiple_of(i * 64, 64)
+        for j in range(64):
             row = idx_ref[base + j]
             outer_ref[pl.ds(base + j, 1), :] = table_ref[pl.ds(row, 1), :]
         return carry
 
-    lax.fori_loop(0, own_rows // 32, body, 0)
-    chunk = 1024
+    lax.fori_loop(0, own_rows // 64, body, 0)
+    chunk = 2048
     spread = spread_ref[...]
 
     def rows(c, carry):

time: 103 us -> 102 us (level)
  no operation moved by 1% of the time
where the time goes in v9:
time: 102 us
  Pallas kernels  28.4 us (28%)
  matrix products  24.7 us (24%)
  local copies, waits for them, and re-layouts  21.9 us (21%)
  blocking collectives  19.8 us (19%)
  other arithmetic  4.47 us (4%)
  starting transfers between devices  1.89 us (2%)
    all_to_all x1, blocking collectives, on_device(): got = lax.all_to_all(send, 'bulk', 0, 0, tiled=True)  19.8 us
    pallas_call x1, Pallas kernels, jump_rows(): pl.pallas_call(_jump_kernel, out_shape=jax.ShapeDtypeStruct((idx.shape[0]...  14.4 us
    pallas_call x1, Pallas kernels, receptor_rows(): pl.pallas_call(_interp_kernel, out_shape=jax.ShapeDtypeStruct((nvars, rec...  14 us
    dot_general x1, matrix products, on_device(): jnp.dot(by_rank, jnp.concatenate([hi, lo], axis=1), preferred_element_typ...  7.27 us
    dot_general x1, matrix products, surface_term(): jnp.einsum('pqf,feqv->vpe', lift_faces, jump_term, precision=lax.Precisio...  6.17 us
    dot_general x1, matrix products, volume_term(): jnp.einsum('dpq,vqe->dvpe', derivative, solution, precision=lax.Precision...  4.36 us
    dot_general x1, matrix products, on_device(): lax.dot_general(receptor_vals, copies, (((0,), (0,)), ((), ())), precisio...  3.51 us
    unnamed x30, local copies, waits for them, and re-layouts  3.38 us
  transfers between devices with their start and end apart: 2, of which 0 were waited for; matrix products, arithmetic and copies ran while one was open for 8% of the time, Pallas kernels for 0%

profile of v9, /device:TPU:9, one launch (start us, length us, event | category | flops | bytes accessed | tf_op | source)
XLA Modules:
  0.0 102.1 jit_solution(5863045837477043436)
XLA Ops:
  0.6 0.8 reshape.108.idx_ref
  1.4 0.0 copy-start.4
  1.4 0.6 select_reduce_fusion
  2.0 3.0 %convolution_bitcast_fusion = f32[6,1024,16,5]{1,2,3,0:T(8,128)S(1)} fusion(f32[16,6,64,1]{2,0,3,1:T(8,128)} %constant.144, f32[5,64,1024]{2,1,0:T(8,128)} %param.15), kind=kOutput, calls=%fused_computation.18 | convolution fusion | flops 377487360 | bytes 3301376 | tf_op jit(solution)/shard_map/qfp,vpe->feqv/dot_general | solution.py:88
  5.0 1.2 %copy.26 = f32[6,1024,16,5]{1,0,3,2:T(8,128)S(1)} copy(f32[6,1024,16,5]{1,2,3,0:T(8,128)S(1)} %convolution_bitcast_fusion) | data formatting | bytes 3932160 | tf_op jit(solution)/shard_map/qfp,vpe->feqv/transpose | solution.py:88
  6.2 0.0 copy-done.4
  6.2 2.5 %copy.35 = f32[10,8,6,1024]{3,1,2,0:T(8,128)} copy(f32[10,8,6,1024]{3,2,1,0:T(8,128)S(1)} %bitcast.63) | data formatting | bytes 3932160
  8.8 0.0 copy-start.2
  8.8 2.2 %copy.29.values_ref = f32[6144,80]{1,0:T(8,128)S(1)} copy(f32[6144,80]{0,1:T(8,128)} %bitcast.64) | data formatting | bytes 3932160 | tf_op jit(solution)/shard_map/reshape;reshape | solution.py:276
  11.0 0.0 copy-done.2
  11.0 0.0 copy-start
  11.0 0.9 reshape.110
  12.0 0.0 copy-start.5
  12.0 0.0 copy-start.9
  12.0 3.3 %copy.27 = f32[6,1024,16]{2,1,0:T(8,128)} copy(f32[6,1024,16]{1,0,2:T(8,128)} %bitcast.65) | data formatting | bytes 786432 | tf_op jit(solution)/shard_map/transpose | solution.py:90
  15.3 0.0 copy-start.12
  15.3 0.0 copy-start.8
  15.3 0.0 copy-start.11
  15.3 0.0 copy-done
  15.3 0.6 gather_fusion
  16.0 0.0 copy-start.1
  16.0 2.6 %gather_fusion.1 = f32[128,16]{1,0:T(8,128)S(1)} fusion(f32[6144,16]{1,0:T(8,128)} %bitcast.61, s32[1024]{0:T(1024)S(1)} %pad_clamp_fusion), kind=kCustom, calls=%fused_computation.1 | custom fusion | bytes 16896 | tf_op jit(solution)/shard_map/jit(_take)/gather | solution.py:100
  18.6 0.1 broadcast_select_fusion.1
  18.7 0.1 broadcast_select_fusion
  18.8 0.1 fusion.24
  18.9 0.7 collective-permute-start.1
  19.6 1.2 %collective-permute-start = (f32[64,96]{1,0:T(8,128)S(1)}, f32[64,96]{1,0:T(8,128)S(1)}, u32[]{:S(2)}, u32[]{:S(2)}) collective-permute-start(f32[64,96]{1,0:T(8,128)S(1)} %get-tuple-element.18), channel_id=1, source_target_pairs={{0,16},{16,32},{32,48},{48,64},{64,80},{80,96},{96,112},{112,0},{1... | collective-permute-start | bytes 73736 | tf_op jit(solution)/shard_map/ppermute | solution.py:21
  20.8 0.0 copy-done.5
  20.8 0.0 copy-done.9
  20.8 0.2 fusion.20
  21.0 0.4 fusion.22
  21.4 0.0 copy-done.12
  21.4 0.0 copy-start.3
  21.4 0.1 fusion.27
  21.5 0.2 select_reduce_fusion.1
  21.7 0.6 add_bitcast_fusion
  22.3 0.0 copy-done.8
  22.3 0.8 multiply_multiply_fusion
  23.1 0.0 copy-done.7
  23.1 0.0 copy-done.11
  23.1 0.0 copy-done.1
  23.1 4.4 %multiply_reduce_fusion = f32[64,5,1024]{2,0,1:T(8,128)} fusion(f32[3,64,64,1]{2,1,3,0:T(8,128)S(1)} %copy-done.7, f32[3,1024]{1,0:T(4,128)S(1)} %copy-done.11, f32[5,64,1024]{2,1,0:T(8,128)S(1)} %copy-done.1), kind=kOutput, calls=%fused_computation.6 | convolution fusion | flops 756613120 | bytes 2682880 | tf_op jit(solution)/shard_map/dpq,vqe->dvpe/dot_general | solution.py:209
  27.5 0.0 copy-done.3
  27.5 2.0 %concatenate.18.basis_ref = f32[12,8192]{1,0:T(8,128)} concatenate(f32[1,8192]{1,0:T(1,128)S(1)} %get-tuple-element.15, f32[1,8192]{1,0:T(1,128)S(1)} %get-tuple-element.7, f32[1,8192]{1,0:T(1,128)S(1)} %get-tuple-element.8, f32[1,8192]{1,0:T(1,128)S(1)} %get-tuple-element.9, f32[1,8192]{1,0:T(1,128)S(1)} %get-tuple-element.17, f32[1,8192]{1,0:T(1,128)S(1)} %get-tuple-element.10, ...), dimensions={0} | concatenate | bytes 786432 | tf_op jit(solution)/shard_map/concatenate | solution.py:244
  29.5 0.0 collective-permute-done.1
  29.5 0.0 collective-permute-done
  29.5 0.6 pad_maximum_fusion.1.recv_ref
  30.1 14.4 %shard_map.158 = f32[6144,80]{1,0:T(8,128)} custom-call(s32[6144]{0:T(1024)} %copy-done.4, f32[6144,80]{1,0:T(8,128)} %copy-done, f32[6144,16]{1,0:T(8,128)} %bitcast.62, f32[128,96]{1,0:T(8,128)} %pad_maximum_fusion.1.recv_ref, bf16[96,80]{1,0:T(8,128)(2,1)} %constant.137.clone.spread_ref), custom_call_target="tpu_custom_call" | custom-call | flops 566231040 | bytes 9486336 | tf_op jit(solution)/shard_map/pallas_call | solution.py:166
  44.5 2.4 %copy.30 = f32[6144,80]{0,1:T(8,128)S(1)} copy(f32[6144,80]{1,0:T(8,128)} %shard_map.158) | data formatting | bytes 3932160 | tf_op jit(solution)/shard_map/pallas_call | solution.py:166
  46.8 2.1 %reshape.112 = f32[6,1024,16,5]{1,0,3,2:T(8,128)} reshape(f32[6144,80]{0,1:T(8,128)S(1)} %copy.30) | data formatting | bytes 3932160 | tf_op jit(solution)/shard_map/reshape | solution.py:203
  48.9 6.2 %multiply_add_fusion = (f32[5,64,1024]{2,1,0:T(8,128)S(1)}, f32[5,64,1024]{2,1,0:T(8,128)}) fusion(f32[5,64,1024]{2,1,0:T(8,128)S(1)} %copy-done.1, f32[64,16,6,1]{0,1,2,3:T(8,128)} %constant.145, f32[6,1024,16,5]{1,0,3,2:T(8,128)} %reshape.112, f32[64,5,1024]{2,0,1:T(8,128)} %multiply_reduce_fusion, f32[64,1024]{1,0:T(8,128)S(1)} %neg.4), kind=kOutput, calls=%fused_computation.26 | convolution fusion | flops 378798080 | bytes 7495680 | tf_op jit(solution)/shard_map/pqf,feqv->vpe/dot_general | solution.py:205
  55.1 0.2 reduce-precision_convert_fusion.1
  55.3 1.2 %pad_maximum_fusion.rows_ref = bf16[640,1024]{1,0:T(8,128)(2,1)} fusion(bf16[320,1024]{1,0:T(8,128)(2,1)S(1)} %get-tuple-element.5, bf16[320,1024]{1,0:T(8,128)(2,1)S(1)} %get-tuple-element.4), kind=kLoop, calls=%fused_computation.23 | loop fusion | flops 2621440 | bytes 2621440 | tf_op jit(solution)/shard_map/concatenate | solution.py:246
  56.5 0.0 copy-start.6
  56.5 0.0 copy-start.13
  56.5 14.0 %shard_map.159 = f32[5,8192]{1,0:T(8,128)} custom-call(bf16[640,1024]{1,0:T(8,128)(2,1)} %pad_maximum_fusion.rows_ref, s32[1,8192]{1,0:T(1,128)} %bitcast.71, f32[12,8192]{1,0:T(8,128)} %concatenate.18.basis_ref), custom_call_target="tpu_custom_call" | custom-call | flops 10737418240 | bytes 1900544 | tf_op jit(solution)/shard_map/pallas_call | solution.py:248
  70.5 0.0 copy-done.6
  70.5 0.0 copy-done.13
  70.5 3.5 %reduce-precision_convert_fusion = (bf16[8192,80]{0,1:T(8,128)(2,1)S(1)}, bf16[8192,80]{0,1:T(8,128)(2,1)S(1)}) fusion(f32[5,8192]{1,0:T(8,128)} %shard_map.159, f32[5,80]{1,0:T(8,128)S(1)} %copy-done.13, s32[80]{0:T(128)S(1)} %and_select_fusion, s32[8192]{0:T(1024)S(1)} %bitcast.70), kind=kOutput, calls=%fused_computation.8 | convolution fusion | flops 43253760 | bytes 2819968 | tf_op jit(solution)/shard_map/dot_general | solution.py:291
  74.1 0.0 copy-done.10
  74.1 7.3 %fusion = f32[1024,160]{0,1:T(8,128)S(1)} fusion(s32[8192]{0:T(1024)S(1)} %copy-done.10, bf16[8192,80]{0,1:T(8,128)(2,1)S(1)} %get-tuple-element.3, bf16[8192,80]{0,1:T(8,128)(2,1)S(1)} %get-tuple-element.2), kind=kOutput, calls=%fused_computation.3 | convolution fusion | flops 2697986048 | bytes 3309568 | tf_op jit(solution)/shard_map/dot_general | solution.py:298
  81.4 0.1 reshape.116
  81.5 19.8 %all_to_all.5 = f32[16,5,1024]{2,1,0:T(8,128)S(1)} all-to-all(f32[16,5,1024]{2,1,0:T(8,128)S(1)} %bitcast.67), channel_id=1, replica_groups=mesh['valve'=8,'bulk'=16] {'bulk'}, dimensions={0} | all-to-all | bytes 655360 | tf_op jit(solution)/shard_map/all_to_all | solution.py:301
  101.3 0.8 copy.47
  (9 shorter events, 0.1 us)
Async XLA Ops:
  1.4 4.8 %copy-start.4 = (s32[6144]{0:T(1024)}, s32[6144]{0:T(1024)S(1)}, u32[]{:S(2)}) copy-start(s32[6144]{0:T(1024)S(1)} %reshape.108.idx_ref) | copy-start | bytes 73732
  8.8 2.2 %copy-start.2 = (f32[96,1024]{1,0:T(8,128)S(1)}, f32[96,1024]{1,0:T(8,128)}, u32[]{:S(2)}) copy-start(f32[96,1024]{1,0:T(8,128)} %param.18) | copy-start | bytes 1179652
  11.0 4.3 %copy-start = (f32[6144,80]{1,0:T(8,128)}, f32[6144,80]{1,0:T(8,128)S(1)}, u32[]{:S(2)}) copy-start(f32[6144,80]{1,0:T(8,128)S(1)} %copy.29.values_ref) | copy-start | bytes 5898244
  12.0 8.8 %copy-start.5 = (s32[8192,1]{0,1:T(1,128)S(1)}, s32[8192,1]{0,1:T(1,128)}, u32[]{:S(2)}) copy-start(s32[8192,1]{0,1:T(1,128)} %param.22) | copy-start | bytes 98308
  12.0 8.8 %copy-start.9 = (bf16[128,128,1]{1,0,2:T(8,128)(2,1)S(1)}, bf16[128,128,1]{1,0,2:T(8,128)(2,1)}, u32[]{:S(2)}) copy-start(bf16[128,128,1]{1,0,2:T(8,128)(2,1)} %constant.146) | copy-start | bytes 98308
  15.3 6.1 %copy-start.12 = (bf16[64,64]{1,0:T(8,128)(2,1)S(1)}, bf16[64,64]{1,0:T(8,128)(2,1)}, u32[]{:S(2)}) copy-start(bf16[64,64]{1,0:T(8,128)(2,1)} %constant.139.clone) | copy-start | bytes 24580
  15.3 7.0 %copy-start.8 = (f32[3,8192]{1,0:T(4,128)S(1)}, f32[3,8192]{1,0:T(4,128)}, u32[]{:S(2)}) copy-start(f32[3,8192]{1,0:T(4,128)} %param.21) | copy-start | bytes 294916
  15.3 7.8 %copy-start.7 = (f32[3,64,64,1]{2,1,3,0:T(8,128)S(1)}, f32[3,64,64,1]{2,1,3,0:T(8,128)}, u32[]{:S(2)}) copy-start(f32[3,64,64,1]{2,1,3,0:T(8,128)} %constant.143) | copy-start | bytes 147460
  15.3 7.8 %copy-start.11 = (f32[3,1024]{1,0:T(4,128)S(1)}, f32[3,1024]{1,0:T(4,128)}, u32[]{:S(2)}) copy-start(f32[3,1024]{1,0:T(4,128)} %param.16) | copy-start | bytes 36868
  16.0 7.1 %copy-start.1 = (f32[5,64,1024]{2,1,0:T(8,128)S(1)}, f32[5,64,1024]{2,1,0:T(8,128)}, u32[]{:S(2)}) copy-start(f32[5,64,1024]{2,1,0:T(8,128)} %param.15) | copy-start | bytes 3932164
  18.9 10.6 %collective-permute-start.1 = (f32[64,96]{1,0:T(8,128)S(1)}, f32[64,96]{1,0:T(8,128)S(1)}, u32[]{:S(2)}, u32[]{:S(2)}) collective-permute-start(f32[64,96]{1,0:T(8,128)S(1)} %get-tuple-element.19), channel_id=1, source_target_pairs={{16,0},{32,16},{48,32},{64,48},{80,64},{96,80},{112,96},{0,112},{1... | collective-permute-start | bytes 73736 | tf_op jit(solution)/shard_map/ppermute | solution.py:22
  19.6 9.9 %collective-permute-start = (f32[64,96]{1,0:T(8,128)S(1)}, f32[64,96]{1,0:T(8,128)S(1)}, u32[]{:S(2)}, u32[]{:S(2)}) collective-permute-start(f32[64,96]{1,0:T(8,128)S(1)} %get-tuple-element.18), channel_id=1, source_target_pairs={{0,16},{16,32},{32,48},{48,64},{64,80},{80,96},{96,112},{112,0},{1... | collective-permute-start | bytes 73736 | tf_op jit(solution)/shard_map/ppermute | solution.py:21
  21.4 6.1 %copy-start.3 = (f32[64,1024]{1,0:T(8,128)S(1)}, f32[64,1024]{1,0:T(8,128)}, u32[]{:S(2)}) copy-start(f32[64,1024]{1,0:T(8,128)} %param.17) | copy-start | bytes 786436
  56.5 14.0 %copy-start.6 = (s32[8192,1]{0,1:T(1,128)S(1)}, s32[8192,1]{0,1:T(1,128)}, u32[]{:S(2)}) copy-start(s32[8192,1]{0,1:T(1,128)} %param.22) | copy-start | bytes 98308
  56.5 14.0 %copy-start.13 = (f32[5,80]{1,0:T(8,128)S(1)}, f32[5,80]{1,0:T(8,128)}, u32[]{:S(2)}) copy-start(f32[5,80]{1,0:T(8,128)} %constant.140.clone) | copy-start | bytes 4804
  70.5 3.5 %copy-start.10 = (s32[8192]{0:T(1024)S(1)}, s32[8192]{0:T(1024)}, u32[]{:S(2)}) copy-start(s32[8192]{0:T(1024)} %add_bitcast_fusion) | copy-start | bytes 98308

commit v10 on v9

--- a/solution.py
+++ b/solution.py
@@ -129,14 +129,14 @@
     table_ref[pl.ds(own_rows, recv_ref.shape[0]), :] = recv_ref[...]
 
     def body(i, carry):
-        base = pl.multiple_of(i * 64, 64)
-        for j in range(64):
+        base = pl.multiple_of(i * 128, 128)
+        for j in range(128):
             row = idx_ref[base + j]
             outer_ref[pl.ds(base + j, 1), :] = table_ref[pl.ds(row, 1), :]
         return carry
 
-    lax.fori_loop(0, own_rows // 64, body, 0)
-    chunk = 2048
+    lax.fori_loop(0, own_rows // 128, body, 0)
+    chunk = 3072
     spread = spread_ref[...]
 
     def rows(c, carry):

time: 102 us -> 102 us (level)
  no operation moved by 1% of the time
where the time goes in v10:
time: 102 us
  Pallas kernels  28.3 us (28%)
  matrix products  24.7 us (24%)
  local copies, waits for them, and re-layouts  21.9 us (21%)
  blocking collectives  19.8 us (19%)
  other arithmetic  4.47 us (4%)
  starting transfers between devices  1.89 us (2%)
    all_to_all x1, blocking collectives, on_device(): got = lax.all_to_all(send, 'bulk', 0, 0, tiled=True)  19.8 us
    pallas_call x1, Pallas kernels, jump_rows(): pl.pallas_call(_jump_kernel, out_shape=jax.ShapeDtypeStruct((idx.shape[0]...  14.3 us
    pallas_call x1, Pallas kernels, receptor_rows(): pl.pallas_call(_interp_kernel, out_shape=jax.ShapeDtypeStruct((nvars, rec...  14 us
    dot_general x1, matrix products, on_device(): jnp.dot(by_rank, jnp.concatenate([hi, lo], axis=1), preferred_element_typ...  7.28 us
    dot_general x1, matrix products, surface_term(): jnp.einsum('pqf,feqv->vpe', lift_faces, jump_term, precision=lax.Precisio...  6.17 us
    dot_general x1, matrix products, volume_term(): jnp.einsum('dpq,vqe->dvpe', derivative, solution, precision=lax.Precision...  4.36 us
    dot_general x1, matrix products, on_device(): lax.dot_general(receptor_vals, copies, (((0,), (0,)), ((), ())), precisio...  3.52 us
    unnamed x30, local copies, waits for them, and re-layouts  3.38 us
  transfers between devices with their start and end apart: 2, of which 0 were waited for; matrix products, arithmetic and copies ran while one was open for 8% of the time, Pallas kernels for 0%

profile of v10, /device:TPU:9, one launch (start us, length us, event | category | flops | bytes accessed | tf_op | source)
XLA Modules:
  0.0 102.0 jit_solution(12922378075082789300)
XLA Ops:
  0.6 0.8 reshape.108.idx_ref
  1.4 0.0 copy-start.4
  1.4 0.6 select_reduce_fusion
  2.0 3.0 %convolution_bitcast_fusion = f32[6,1024,16,5]{1,2,3,0:T(8,128)S(1)} fusion(f32[16,6,64,1]{2,0,3,1:T(8,128)} %constant.144, f32[5,64,1024]{2,1,0:T(8,128)} %param.15), kind=kOutput, calls=%fused_computation.18 | convolution fusion | flops 377487360 | bytes 3301376 | tf_op jit(solution)/shard_map/qfp,vpe->feqv/dot_general | solution.py:88
  5.0 1.2 %copy.26 = f32[6,1024,16,5]{1,0,3,2:T(8,128)S(1)} copy(f32[6,1024,16,5]{1,2,3,0:T(8,128)S(1)} %convolution_bitcast_fusion) | data formatting | bytes 3932160 | tf_op jit(solution)/shard_map/qfp,vpe->feqv/transpose | solution.py:88
  6.2 0.0 copy-done.4
  6.2 2.5 %copy.35 = f32[10,8,6,1024]{3,1,2,0:T(8,128)} copy(f32[10,8,6,1024]{3,2,1,0:T(8,128)S(1)} %bitcast.63) | data formatting | bytes 3932160
  8.8 0.0 copy-start.2
  8.8 2.2 %copy.29.values_ref = f32[6144,80]{1,0:T(8,128)S(1)} copy(f32[6144,80]{0,1:T(8,128)} %bitcast.64) | data formatting | bytes 3932160 | tf_op jit(solution)/shard_map/reshape;reshape | solution.py:276
  11.0 0.0 copy-done.2
  11.0 0.0 copy-start
  11.0 0.9 reshape.110
  12.0 0.0 copy-start.5
  12.0 0.0 copy-start.9
  12.0 3.3 %copy.27 = f32[6,1024,16]{2,1,0:T(8,128)} copy(f32[6,1024,16]{1,0,2:T(8,128)} %bitcast.65) | data formatting | bytes 786432 | tf_op jit(solution)/shard_map/transpose | solution.py:90
  15.3 0.0 copy-start.12
  15.3 0.0 copy-start.8
  15.3 0.0 copy-start.7
  15.3 0.0 copy-start.11
  15.3 0.0 copy-done
  15.3 0.6 gather_fusion
  16.0 0.0 copy-start.1
  16.0 2.6 %gather_fusion.1 = f32[128,16]{1,0:T(8,128)S(1)} fusion(f32[6144,16]{1,0:T(8,128)} %bitcast.61, s32[1024]{0:T(1024)S(1)} %pad_clamp_fusion), kind=kCustom, calls=%fused_computation.1 | custom fusion | bytes 16896 | tf_op jit(solution)/shard_map/jit(_take)/gather | solution.py:100
  18.6 0.1 broadcast_select_fusion.1
  18.7 0.1 broadcast_select_fusion
  18.8 0.1 fusion.24
  18.9 0.7 collective-permute-start.1
  19.6 1.2 %collective-permute-start = (f32[64,96]{1,0:T(8,128)S(1)}, f32[64,96]{1,0:T(8,128)S(1)}, u32[]{:S(2)}, u32[]{:S(2)}) collective-permute-start(f32[64,96]{1,0:T(8,128)S(1)} %get-tuple-element.18), channel_id=1, source_target_pairs={{0,16},{16,32},{32,48},{48,64},{64,80},{80,96},{96,112},{112,0},{1... | collective-permute-start | bytes 73736 | tf_op jit(solution)/shard_map/ppermute | solution.py:21
  20.8 0.0 copy-done.5
  20.8 0.0 copy-done.9
  20.8 0.2 fusion.20
  21.0 0.4 fusion.22
  21.4 0.0 copy-done.12
  21.4 0.0 copy-start.3
  21.4 0.1 fusion.27
  21.5 0.2 select_reduce_fusion.1
  21.7 0.6 add_bitcast_fusion
  22.3 0.0 copy-done.8
  22.3 0.8 multiply_multiply_fusion
  23.1 0.0 copy-done.7
  23.1 0.0 copy-done.11
  23.1 0.0 copy-done.1
  23.1 4.4 %multiply_reduce_fusion = f32[64,5,1024]{2,0,1:T(8,128)} fusion(f32[3,64,64,1]{2,1,3,0:T(8,128)S(1)} %copy-done.7, f32[3,1024]{1,0:T(4,128)S(1)} %copy-done.11, f32[5,64,1024]{2,1,0:T(8,128)S(1)} %copy-done.1), kind=kOutput, calls=%fused_computation.6 | convolution fusion | flops 756613120 | bytes 2682880 | tf_op jit(solution)/shard_map/dpq,vqe->dvpe/dot_general | solution.py:209
  27.5 0.0 copy-done.3
  27.5 2.0 %concatenate.18.basis_ref = f32[12,8192]{1,0:T(8,128)} concatenate(f32[1,8192]{1,0:T(1,128)S(1)} %get-tuple-element.15, f32[1,8192]{1,0:T(1,128)S(1)} %get-tuple-element.7, f32[1,8192]{1,0:T(1,128)S(1)} %get-tuple-element.8, f32[1,8192]{1,0:T(1,128)S(1)} %get-tuple-element.9, f32[1,8192]{1,0:T(1,128)S(1)} %get-tuple-element.17, f32[1,8192]{1,0:T(1,128)S(1)} %get-tuple-element.10, ...), dimensions={0} | concatenate | bytes 786432 | tf_op jit(solution)/shard_map/concatenate | solution.py:244
  29.5 0.0 collective-permute-done.1
  29.5 0.0 collective-permute-done
  29.5 0.6 pad_maximum_fusion.1.recv_ref
  30.1 14.3 %shard_map.158 = f32[6144,80]{1,0:T(8,128)} custom-call(s32[6144]{0:T(1024)} %copy-done.4, f32[6144,80]{1,0:T(8,128)} %copy-done, f32[6144,16]{1,0:T(8,128)} %bitcast.62, f32[128,96]{1,0:T(8,128)} %pad_maximum_fusion.1.recv_ref, bf16[96,80]{1,0:T(8,128)(2,1)} %constant.137.clone.spread_ref), custom_call_target="tpu_custom_call" | custom-call | flops 566231040 | bytes 9486336 | tf_op jit(solution)/shard_map/pallas_call | solution.py:166
  44.4 2.4 %copy.30 = f32[6144,80]{0,1:T(8,128)S(1)} copy(f32[6144,80]{1,0:T(8,128)} %shard_map.158) | data formatting | bytes 3932160 | tf_op jit(solution)/shard_map/pallas_call | solution.py:166
  46.8 2.1 %reshape.112 = f32[6,1024,16,5]{1,0,3,2:T(8,128)} reshape(f32[6144,80]{0,1:T(8,128)S(1)} %copy.30) | data formatting | bytes 3932160 | tf_op jit(solution)/shard_map/reshape | solution.py:203
  48.9 6.2 %multiply_add_fusion = (f32[5,64,1024]{2,1,0:T(8,128)S(1)}, f32[5,64,1024]{2,1,0:T(8,128)}) fusion(f32[5,64,1024]{2,1,0:T(8,128)S(1)} %copy-done.1, f32[64,16,6,1]{0,1,2,3:T(8,128)} %constant.145, f32[6,1024,16,5]{1,0,3,2:T(8,128)} %reshape.112, f32[64,5,1024]{2,0,1:T(8,128)} %multiply_reduce_fusion, f32[64,1024]{1,0:T(8,128)S(1)} %neg.4), kind=kOutput, calls=%fused_computation.26 | convolution fusion | flops 378798080 | bytes 7495680 | tf_op jit(solution)/shard_map/pqf,feqv->vpe/dot_general | solution.py:205
  55.1 0.2 reduce-precision_convert_fusion.1
  55.3 1.2 %pad_maximum_fusion.rows_ref = bf16[640,1024]{1,0:T(8,128)(2,1)} fusion(bf16[320,1024]{1,0:T(8,128)(2,1)S(1)} %get-tuple-element.5, bf16[320,1024]{1,0:T(8,128)(2,1)S(1)} %get-tuple-element.4), kind=kLoop, calls=%fused_computation.23 | loop fusion | flops 2621440 | bytes 2621440 | tf_op jit(solution)/shard_map/concatenate | solution.py:246
  56.4 0.0 copy-start.6
  56.4 14.0 %shard_map.159 = f32[5,8192]{1,0:T(8,128)} custom-call(bf16[640,1024]{1,0:T(8,128)(2,1)} %pad_maximum_fusion.rows_ref, s32[1,8192]{1,0:T(1,128)} %bitcast.71, f32[12,8192]{1,0:T(8,128)} %concatenate.18.basis_ref), custom_call_target="tpu_custom_call" | custom-call | flops 10737418240 | bytes 1900544 | tf_op jit(solution)/shard_map/pallas_call | solution.py:248
  70.5 0.0 copy-done.6
  70.5 0.0 copy-done.13
  70.5 3.5 %reduce-precision_convert_fusion = (bf16[8192,80]{0,1:T(8,128)(2,1)S(1)}, bf16[8192,80]{0,1:T(8,128)(2,1)S(1)}) fusion(f32[5,8192]{1,0:T(8,128)} %shard_map.159, f32[5,80]{1,0:T(8,128)S(1)} %copy-done.13, s32[80]{0:T(128)S(1)} %and_select_fusion, s32[8192]{0:T(1024)S(1)} %bitcast.70), kind=kOutput, calls=%fused_computation.8 | convolution fusion | flops 43253760 | bytes 2819968 | tf_op jit(solution)/shard_map/dot_general | solution.py:291
  74.0 0.0 copy-done.10
  74.0 7.3 %fusion = f32[1024,160]{0,1:T(8,128)S(1)} fusion(s32[8192]{0:T(1024)S(1)} %copy-done.10, bf16[8192,80]{0,1:T(8,128)(2,1)S(1)} %get-tuple-element.3, bf16[8192,80]{0,1:T(8,128)(2,1)S(1)} %get-tuple-element.2), kind=kOutput, calls=%fused_computation.3 | convolution fusion | flops 2697986048 | bytes 3309568 | tf_op jit(solution)/shard_map/dot_general | solution.py:298
  81.4 0.1 reshape.116
  81.4 19.8 %all_to_all.5 = f32[16,5,1024]{2,1,0:T(8,128)S(1)} all-to-all(f32[16,5,1024]{2,1,0:T(8,128)S(1)} %bitcast.67), channel_id=1, replica_groups=mesh['valve'=8,'bulk'=16] {'bulk'}, dimensions={0} | all-to-all | bytes 655360 | tf_op jit(solution)/shard_map/all_to_all | solution.py:301
  101.2 0.8 copy.47
  (9 shorter events, 0.1 us)
Async XLA Ops:
  1.4 4.8 %copy-start.4 = (s32[6144]{0:T(1024)}, s32[6144]{0:T(1024)S(1)}, u32[]{:S(2)}) copy-start(s32[6144]{0:T(1024)S(1)} %reshape.108.idx_ref) | copy-start | bytes 73732
  8.8 2.2 %copy-start.2 = (f32[96,1024]{1,0:T(8,128)S(1)}, f32[96,1024]{1,0:T(8,128)}, u32[]{:S(2)}) copy-start(f32[96,1024]{1,0:T(8,128)} %param.18) | copy-start | bytes 1179652
  11.0 4.3 %copy-start = (f32[6144,80]{1,0:T(8,128)}, f32[6144,80]{1,0:T(8,128)S(1)}, u32[]{:S(2)}) copy-start(f32[6144,80]{1,0:T(8,128)S(1)} %copy.29.values_ref) | copy-start | bytes 5898244
  12.0 8.8 %copy-start.5 = (s32[8192,1]{0,1:T(1,128)S(1)}, s32[8192,1]{0,1:T(1,128)}, u32[]{:S(2)}) copy-start(s32[8192,1]{0,1:T(1,128)} %param.22) | copy-start | bytes 98308
  12.0 8.8 %copy-start.9 = (bf16[128,128,1]{1,0,2:T(8,128)(2,1)S(1)}, bf16[128,128,1]{1,0,2:T(8,128)(2,1)}, u32[]{:S(2)}) copy-start(bf16[128,128,1]{1,0,2:T(8,128)(2,1)} %constant.146) | copy-start | bytes 98308
  15.3 6.1 %copy-start.12 = (bf16[64,64]{1,0:T(8,128)(2,1)S(1)}, bf16[64,64]{1,0:T(8,128)(2,1)}, u32[]{:S(2)}) copy-start(bf16[64,64]{1,0:T(8,128)(2,1)} %constant.139.clone) | copy-start | bytes 24580
  15.3 7.0 %copy-start.8 = (f32[3,8192]{1,0:T(4,128)S(1)}, f32[3,8192]{1,0:T(4,128)}, u32[]{:S(2)}) copy-start(f32[3,8192]{1,0:T(4,128)} %param.21) | copy-start | bytes 294916
  15.3 7.8 %copy-start.7 = (f32[3,64,64,1]{2,1,3,0:T(8,128)S(1)}, f32[3,64,64,1]{2,1,3,0:T(8,128)}, u32[]{:S(2)}) copy-start(f32[3,64,64,1]{2,1,3,0:T(8,128)} %constant.143) | copy-start | bytes 147460
  15.3 7.8 %copy-start.11 = (f32[3,1024]{1,0:T(4,128)S(1)}, f32[3,1024]{1,0:T(4,128)}, u32[]{:S(2)}) copy-start(f32[3,1024]{1,0:T(4,128)} %param.16) | copy-start | bytes 36868
  16.0 7.1 %copy-start.1 = (f32[5,64,1024]{2,1,0:T(8,128)S(1)}, f32[5,64,1024]{2,1,0:T(8,128)}, u32[]{:S(2)}) copy-start(f32[5,64,1024]{2,1,0:T(8,128)} %param.15) | copy-start | bytes 3932164
  18.9 10.6 %collective-permute-start.1 = (f32[64,96]{1,0:T(8,128)S(1)}, f32[64,96]{1,0:T(8,128)S(1)}, u32[]{:S(2)}, u32[]{:S(2)}) collective-permute-start(f32[64,96]{1,0:T(8,128)S(1)} %get-tuple-element.19), channel_id=1, source_target_pairs={{16,0},{32,16},{48,32},{64,48},{80,64},{96,80},{112,96},{0,112},{1... | collective-permute-start | bytes 73736 | tf_op jit(solution)/shard_map/ppermute | solution.py:22
  19.6 9.9 %collective-permute-start = (f32[64,96]{1,0:T(8,128)S(1)}, f32[64,96]{1,0:T(8,128)S(1)}, u32[]{:S(2)}, u32[]{:S(2)}) collective-permute-start(f32[64,96]{1,0:T(8,128)S(1)} %get-tuple-element.18), channel_id=1, source_target_pairs={{0,16},{16,32},{32,48},{48,64},{64,80},{80,96},{96,112},{112,0},{1... | collective-permute-start | bytes 73736 | tf_op jit(solution)/shard_map/ppermute | solution.py:21
  21.4 6.1 %copy-start.3 = (f32[64,1024]{1,0:T(8,128)S(1)}, f32[64,1024]{1,0:T(8,128)}, u32[]{:S(2)}) copy-start(f32[64,1024]{1,0:T(8,128)} %param.17) | copy-start | bytes 786436
  56.4 14.0 %copy-start.6 = (s32[8192,1]{0,1:T(1,128)S(1)}, s32[8192,1]{0,1:T(1,128)}, u32[]{:S(2)}) copy-start(s32[8192,1]{0,1:T(1,128)} %param.22) | copy-start | bytes 98308
  56.4 14.0 %copy-start.13 = (f32[5,80]{1,0:T(8,128)S(1)}, f32[5,80]{1,0:T(8,128)}, u32[]{:S(2)}) copy-start(f32[5,80]{1,0:T(8,128)} %constant.140.clone) | copy-start | bytes 4804
  70.5 3.5 %copy-start.10 = (s32[8192]{0:T(1024)S(1)}, s32[8192]{0:T(1024)}, u32[]{:S(2)}) copy-start(s32[8192]{0:T(1024)} %add_bitcast_fusion) | copy-start | bytes 98308
